TPU v7x, 256 devices: a whole 4x4x8 slice. The times are simulated.
256 devices in a mesh: shell: 4 (over x_lo, core), tile: 64 (over z, x_hi, y).
Axes of the slice: x: 4 (x_hi: 2, x_lo: 2; x = x_hi * 2 + x_lo), y: 4, z: 8, core: 2. Of those that a mesh axis runs over, the one named last changes fastest.
Arguments:
- latent: float32 [64, 2048, 512], P('shell', 'tile'), may hold values from -5 to 5
- shell_sigma: float32 [64], P('shell'), may hold values from 0.15 to 0.6
- lens_weight: float32 [5, 64], P(None, 'shell'), may hold values from 0 to 0.5
- shear_kernel: bfloat16 [2, 33, 33], replicated, may hold values from -0.1875 to 0.1875
- star_mask: int32 [2048, 512], P('tile', 'shell'), may hold values 0 or 1
- gal_pix: int32 [16, 4096, 128], P('shell', 'tile'), may hold values from 0 to 4095
- gal_bin: int32 [16, 4096, 128], P('shell', 'tile'), may hold values from 0 to 4
- gal_shape: float32 [2, 16, 4096, 128], P(None, 'shell', 'tile'), may hold values from -3 to 3
- gal_weight: float32 [16, 4096, 128], P('shell', 'tile'), may hold values from 0.5 to 4
- gal_counts: int32 [16, 4096], P('shell', 'tile'), may hold values from 0 to 128, as said below
Outputs:
- grad_field: float32 [64, 2048, 512], P('shell', 'tile')
Inputs may be any that keep to these rules, and one draw needn't show every extreme that they name: Bucket (i, j) of the galaxy arrays holds galaxies for the tile j mod 64 and the column block i mod 4, in its first gal_counts[i, j] slots; in every draw some destination block receives 128 galaxies from every device, and buckets' loads range from near zero to 128.
All inputs are finite; a program needn't handle non-finite values. No bound on the sum of `star_mask` on one device may be relied on, other than what follows from the above.
Results may differ from a plain program's by a relative error of at most 0.0023.
Values may be sent and summed in bfloat16 or wider, within the bound.
No kernel may reach another device: no remote copies, remote signals or barrier semaphores. Data moves between devices by JAX's collectives and lax.ppermute only.
A program may use at most 64 MiB of HBM per device.

v0:
```python
import jax
import jax.numpy as jnp
from jax import lax
from jax.sharding import PartitionSpec as P

NBIN = 5
KER = 33
HALF = 16


def extended(block, sides, width):
    for axis, dim in sides:
        count = lax.axis_size(axis)
        forward = [(i, i + 1) for i in range(count - 1)]
        backward = [(target, source) for source, target in forward]
        low = lax.ppermute(
            lax.slice_in_dim(block, block.shape[dim] - width, None, axis=dim), axis, forward
        )
        high = lax.ppermute(lax.slice_in_dim(block, 0, width, axis=dim), axis, backward)
        block = jnp.concatenate([low, block, high], axis=dim)
    return block


def build_bands(kernel, columns):
    span = columns + KER - 1
    grid_shape = (KER, span, columns)
    lagged = lax.broadcasted_iota(jnp.int32, grid_shape, 1) - lax.broadcasted_iota(
        jnp.int32, grid_shape, 2
    )
    onehot = (lagged == lax.broadcasted_iota(jnp.int32, grid_shape, 0)).astype(jnp.bfloat16)
    bands = jnp.einsum("kdv,vjc->kdjc", kernel, onehot, preferred_element_type=jnp.float32)
    return bands.astype(jnp.bfloat16)


def stacked_rows(padded, height):
    return jnp.stack([padded[..., offset : offset + height, :] for offset in range(KER)], axis=-3)


def deposit_block(shear_rows, codes, observed, weights, columns):
    row_count = shear_rows.shape[1]
    usable = codes >= 0
    safe_codes = jnp.where(usable, codes, 0)
    row_of = safe_codes // columns
    col_of = safe_codes % columns
    rows_hot = (
        row_of[:, None] == lax.broadcasted_iota(jnp.int32, (codes.shape[0], row_count), 1)
    ).astype(jnp.float32)
    cols_hot = (
        col_of[:, None] == lax.broadcasted_iota(jnp.int32, (codes.shape[0], columns), 1)
    ).astype(jnp.float32)
    picked = jnp.einsum(
        "gr,krc->kgc",
        rows_hot,
        shear_rows,
        precision=lax.Precision.HIGHEST,
        preferred_element_type=jnp.float32,
    )
    predicted = jnp.sum(picked * cols_hot[None], axis=2)
    scaled = jnp.where(usable, weights, 0.0)
    residual = scaled[None] * (predicted - observed)
    spread = residual[:, :, None] * cols_hot[None]
    return jnp.einsum(
        "gr,kgc->krc",
        rows_hot,
        spread,
        precision=lax.Precision.HIGHEST,
        preferred_element_type=jnp.float32,
    )


def per_device(
    latent,
    shell_sigma,
    lens_weight,
    shear_kernel,
    star_mask,
    gal_pix,
    gal_bin,
    gal_shape,
    gal_weight,
    gal_counts,
):
    height = latent.shape[1]
    width = latent.shape[2]
    shell_count = lax.axis_size("shell")
    columns = width // shell_count
    pixels = height * columns
    sigma = shell_sigma[:, None, None]
    growth = jnp.exp(sigma * latent - 0.5 * sigma * sigma)
    partial_bins = jnp.einsum(
        "bs,srw->brw",
        lens_weight,
        growth - 1.0,
        precision=lax.Precision.HIGHEST,
        preferred_element_type=jnp.float32,
    )
    bin_map = lax.psum_scatter(partial_bins, "shell", scatter_dimension=2, tiled=True).astype(
        jnp.bfloat16
    )
    padded = extended(bin_map, (("shell", 2), ("tile", 1)), HALF)
    forward_bands = build_bands(shear_kernel, columns)
    shear = jnp.einsum(
        "bdrj,kdjc->kbrc",
        stacked_rows(padded, height),
        forward_bands,
        preferred_element_type=jnp.float32,
    )
    slot_index = lax.broadcasted_iota(jnp.int32, gal_pix.shape, 2)
    codes = jnp.where(slot_index < gal_counts[:, :, None], gal_bin * pixels + gal_pix, -1).astype(
        jnp.float32
    )
    packet = jnp.concatenate([codes[None], gal_shape, gal_weight[None]], axis=0)
    arrived = lax.all_to_all(
        lax.all_to_all(packet, "shell", split_axis=1, concat_axis=1, tiled=True),
        "tile",
        split_axis=2,
        concat_axis=2,
        tiled=True,
    )
    shear_rows = shear.reshape(2, NBIN * height, columns)
    groups = arrived.shape[1]

    def add_group(group, total):
        block = lax.dynamic_index_in_dim(arrived, group, 1, keepdims=False).reshape(4, -1)
        group_codes = block[0].astype(jnp.int32)
        return total + deposit_block(shear_rows, group_codes, block[1:3], block[3], columns)

    summed = lax.fori_loop(0, groups, add_group, jnp.zeros_like(shear_rows))
    shear_grad = summed.reshape(2, NBIN, height, columns)
    masked = (shear_grad * star_mask.astype(jnp.float32)).astype(jnp.bfloat16)
    rims = extended(masked, (("shell", 3), ("tile", 2)), HALF)
    back_bands = build_bands(jnp.flip(shear_kernel, (1, 2)), columns)
    bin_grad = jnp.einsum(
        "kbdrj,kdjc->brc",
        stacked_rows(rims, height),
        back_bands,
        preferred_element_type=jnp.float32,
    )
    full_grad = lax.all_gather(bin_grad, "shell", axis=2, tiled=True)
    mixed = jnp.einsum(
        "bs,brw->srw",
        lens_weight,
        full_grad,
        precision=lax.Precision.HIGHEST,
        preferred_element_type=jnp.float32,
    )
    return sigma * growth * mixed


def solution(mesh):
    return jax.shard_map(
        per_device,
        mesh=mesh,
        in_specs=(
            P("shell", "tile", None),
            P("shell"),
            P(None, "shell"),
            P(),
            P("tile", "shell"),
            P("shell", "tile", None),
            P("shell", "tile", None),
            P(None, "shell", "tile", None),
            P("shell", "tile", None),
            P("shell", "tile"),
        ),
        out_specs=P("shell", "tile", None),
        check_vma=False,
    )
```

profile of v0, /device:TPU:124, one launch (start us, length us, event | category | flops | bytes accessed | tf_op | source)
XLA Modules:
  0.0 208.0 jit_solution(7721434345518271787)
XLA Ops:
  7.2 3.4 %convolution_bitcast_fusion.1 = f32[5,32,512]{2,0,1:T(8,128)} fusion(f32[16,32,512]{2,1,0:T(8,128)} %param.12, f32[16]{0:T(128)S(1)} %multiply_multiply_fusion, f32[16]{0:T(128)} %param.13, f32[5,16]{1,0:T(8,128)S(1)} %copy-done), kind=kOutput, calls=%fused_computation.44 | convolution fusion | flops 16515072 | bytes 1376704 | tf_op jit(solution)/shard_map/bs,srw->brw/dot_general | solution.py:90
  12.8 19.8 %reduce-scatter.2.cloned.1.call-done = f32[5,32,128]{2,0,1:T(8,128)} async-done(((f32[5,32,512]{2,0,1:T(8,128)}), f32[5,32,128]{2,0,1:T(8,128)}) %reduce-scatter.2.cloned.1.call-update) | async-done | bytes 81936 | tf_op jit(solution)/shard_map/reduce_scatter | solution.py:97
  33.6 2.6 %collective-permute-start = (bf16[5,32,16]{2,0,1:T(8,128)(2,1)S(1)}, bf16[5,32,16]{2,0,1:T(8,128)(2,1)S(1)}, u32[]{:S(2)}, u32[]{:S(2)}) collective-permute-start(bf16[5,32,16]{2,0,1:T(8,128)(2,1)S(1)} %get-tuple-element.164), channel_id=1, source_target_pairs={{0,64},{64,128},{128,192},{1,65},{65,129},{129,193},{2,66},{66,130... | collective-permute-start | bytes 15368 | tf_op jit(solution)/shard_map/ppermute | solution.py:16
  39.6 4.1 %all-to-all-start = ((f32[4,4,64,128]{3,0,2,1:T(4,128)}), f32[4,4,64,128]{3,0,2,1:T(4,128)}, u32[]{:S(2)}, u32[]{:S(2)}) async-start(f32[4,4,64,128]{3,0,2,1:T(4,128)} %pad_maximum_fusion), calls=%async_computation | async-start | bytes 1048576 | tf_op jit(solution)/shard_map/all_to_all | solution.py:114
  44.6 4.9 %collective-permute-start.2 = (bf16[5,16,160]{2,0,1:T(8,128)(2,1)}, bf16[5,16,160]{2,0,1:T(8,128)(2,1)}, u32[]{:S(2)}, u32[]{:S(2)}) collective-permute-start(bf16[5,16,160]{2,0,1:T(8,128)(2,1)} %get-tuple-element.161), channel_id=1, source_target_pairs={{0,1},{1,2},{2,3},{3,4},{4,5},{5,6},{6,7},{7,8},{8,9},{9,10},{10,1... | collective-permute-start | bytes 76808 | tf_op jit(solution)/shard_map/ppermute | solution.py:16
  56.0 11.8 %all-to-all-start.1 = ((f32[4,4,64,128]{3,0,1,2:T(4,128)}), f32[4,4,64,128]{3,0,1,2:T(4,128)}, u32[]{:S(2)}, u32[]{:S(2)}) async-start(f32[4,4,64,128]{3,0,1,2:T(4,128)} %copy.27), calls=%async_computation.1 | async-start | bytes 1048576 | tf_op jit(solution)/shard_map/all_to_all | solution.py:113
  71.2 11.1 %all-to-all-done.1 = f32[4,4,64,128]{3,0,1,2:T(4,128)} async-done(((f32[4,4,64,128]{3,0,1,2:T(4,128)}), f32[4,4,64,128]{3,0,1,2:T(4,128)}, u32[]{:S(2)}, u32[]{:S(2)}) %all-to-all-start.1) | async-done | bytes 524320 | tf_op jit(solution)/shard_map/all_to_all | solution.py:113
  82.3 79.2 %while.16 = (s32[]{:T(128)}, f32[2,160,128]{2,1,0:T(8,128)}, f32[4,4,64,128]{3,0,1,2:T(4,128)}, f32[2,160,128]{2,1,0:T(8,128)S(1)}, s32[]{:T(128)}, /*index=5*/s32[]{:T(128)}, s32[]{}, s32[]{}) while((s32[]{:T(128)}, f32[2,160,128]{2,1,0:T(8,128)}, f32[4,4,64,128]{3,0,1,2:T(4,128)}, f32[2,160,128]{2,1,0:T(8,128)S(1)}, s32[]{:T(128)}, ...), condition=%wide.region_3.4_spmd.clone, body=%wide.region_1.3_spmd.clone.sunk | while | flops 8064376832 | bytes 40337624 | solution.py:128
  83.8 4.4 %fusion.112 = f32[8192,2]{0,1:T(2,128)S(1)} fusion(f32[8192,128]{0,1:T(8,128)S(1)} %fusion.111, f32[2,160,128]{2,1,0:T(8,128)S(1)} %get-tuple-element.218, s32[8192]{0:T(1024)S(1)} %get-tuple-element.196), kind=kOutput, calls=%fused_computation.11.clone.1 | convolution fusion | flops 4032020480 | bytes 4456448 | tf_op jit(solution)/shard_map/while/body/eval_jaxpr/gr,krc->kgc/dot_general | solution.py:51
  89.3 5.6 %copy.80 = f32[8192,128]{1,0:T(8,128)} copy(f32[8192,128]{0,1:T(8,128)} %copy-done.1) | data formatting | bytes 8388608 | tf_op jit(solution)/shard_map/while/body/eval_jaxpr/convert_element_type | solution.py:50
  94.9 6.6 %fusion.114 = f32[2,160,128]{2,1,0:T(8,128)S(1)} fusion(s32[8192]{0:T(1024)S(1)} %get-tuple-element.196, f32[8192,128]{1,0:T(8,128)} %copy.80, f32[2,8192]{1,0:T(2,128)S(1)} %fusion.113, f32[2,160,128]{2,1,0:T(8,128)S(1)} %copy-done.3, pred[]{:T(512)S(6)} %compare.19), kind=kOutput, calls=%fused_computation.13.clone.1 | convolution fusion | flops 4030021632 | bytes 4620289 | tf_op jit(solution)/shard_map/while/body/eval_jaxpr/gr,kgc->krc/dot_general | solution.py:62
  103.6 4.4 %fusion.112 = f32[8192,2]{0,1:T(2,128)S(1)} fusion(f32[8192,128]{0,1:T(8,128)S(1)} %fusion.111, f32[2,160,128]{2,1,0:T(8,128)S(1)} %get-tuple-element.218, s32[8192]{0:T(1024)S(1)} %get-tuple-element.196), kind=kOutput, calls=%fused_computation.11.clone.1 | convolution fusion | flops 4032020480 | bytes 4456448 | tf_op jit(solution)/shard_map/while/body/eval_jaxpr/gr,krc->kgc/dot_general | solution.py:51
  109.1 5.6 %copy.80 = f32[8192,128]{1,0:T(8,128)} copy(f32[8192,128]{0,1:T(8,128)} %copy-done.1) | data formatting | bytes 8388608 | tf_op jit(solution)/shard_map/while/body/eval_jaxpr/convert_element_type | solution.py:50
  114.7 6.6 %fusion.114 = f32[2,160,128]{2,1,0:T(8,128)S(1)} fusion(s32[8192]{0:T(1024)S(1)} %get-tuple-element.196, f32[8192,128]{1,0:T(8,128)} %copy.80, f32[2,8192]{1,0:T(2,128)S(1)} %fusion.113, f32[2,160,128]{2,1,0:T(8,128)S(1)} %copy-done.3, pred[]{:T(512)S(6)} %compare.19), kind=kOutput, calls=%fused_computation.13.clone.1 | convolution fusion | flops 4030021632 | bytes 4620289 | tf_op jit(solution)/shard_map/while/body/eval_jaxpr/gr,kgc->krc/dot_general | solution.py:62
  123.4 4.4 %fusion.112 = f32[8192,2]{0,1:T(2,128)S(1)} fusion(f32[8192,128]{0,1:T(8,128)S(1)} %fusion.111, f32[2,160,128]{2,1,0:T(8,128)S(1)} %get-tuple-element.218, s32[8192]{0:T(1024)S(1)} %get-tuple-element.196), kind=kOutput, calls=%fused_computation.11.clone.1 | convolution fusion | flops 4032020480 | bytes 4456448 | tf_op jit(solution)/shard_map/while/body/eval_jaxpr/gr,krc->kgc/dot_general | solution.py:51
  128.9 5.6 %copy.80 = f32[8192,128]{1,0:T(8,128)} copy(f32[8192,128]{0,1:T(8,128)} %copy-done.1) | data formatting | bytes 8388608 | tf_op jit(solution)/shard_map/while/body/eval_jaxpr/convert_element_type | solution.py:50
  134.5 6.6 %fusion.114 = f32[2,160,128]{2,1,0:T(8,128)S(1)} fusion(s32[8192]{0:T(1024)S(1)} %get-tuple-element.196, f32[8192,128]{1,0:T(8,128)} %copy.80, f32[2,8192]{1,0:T(2,128)S(1)} %fusion.113, f32[2,160,128]{2,1,0:T(8,128)S(1)} %copy-done.3, pred[]{:T(512)S(6)} %compare.19), kind=kOutput, calls=%fused_computation.13.clone.1 | convolution fusion | flops 4030021632 | bytes 4620289 | tf_op jit(solution)/shard_map/while/body/eval_jaxpr/gr,kgc->krc/dot_general | solution.py:62
  143.2 4.4 %fusion.112 = f32[8192,2]{0,1:T(2,128)S(1)} fusion(f32[8192,128]{0,1:T(8,128)S(1)} %fusion.111, f32[2,160,128]{2,1,0:T(8,128)S(1)} %get-tuple-element.218, s32[8192]{0:T(1024)S(1)} %get-tuple-element.196), kind=kOutput, calls=%fused_computation.11.clone.1 | convolution fusion | flops 4032020480 | bytes 4456448 | tf_op jit(solution)/shard_map/while/body/eval_jaxpr/gr,krc->kgc/dot_general | solution.py:51
  148.7 5.6 %copy.80 = f32[8192,128]{1,0:T(8,128)} copy(f32[8192,128]{0,1:T(8,128)} %copy-done.1) | data formatting | bytes 8388608 | tf_op jit(solution)/shard_map/while/body/eval_jaxpr/convert_element_type | solution.py:50
  154.3 6.6 %fusion.114 = f32[2,160,128]{2,1,0:T(8,128)S(1)} fusion(s32[8192]{0:T(1024)S(1)} %get-tuple-element.196, f32[8192,128]{1,0:T(8,128)} %copy.80, f32[2,8192]{1,0:T(2,128)S(1)} %fusion.113, f32[2,160,128]{2,1,0:T(8,128)S(1)} %copy-done.3, pred[]{:T(512)S(6)} %compare.19), kind=kOutput, calls=%fused_computation.13.clone.1 | convolution fusion | flops 4030021632 | bytes 4620289 | tf_op jit(solution)/shard_map/while/body/eval_jaxpr/gr,kgc->krc/dot_general | solution.py:62
  165.3 3.5 %collective-permute-done.5 = bf16[2,5,32,16]{3,2,1,0:T(8,128)(2,1)S(1)} collective-permute-done((bf16[2,5,32,16]{3,2,1,0:T(8,128)(2,1)S(1)}, bf16[2,5,32,16]{3,2,1,0:T(8,128)(2,1)S(1)}, u32[]{:S(2)}, u32[]{:S(2)}) %collective-permute-start.5) | collective-permute-done | bytes 10272 | tf_op jit(solution)/shard_map/ppermute | solution.py:19
  169.0 5.2 %collective-permute-start.6 = (bf16[2,5,16,160]{3,2,1,0:T(8,128)(2,1)S(1)}, bf16[2,5,16,160]{3,2,1,0:T(8,128)(2,1)S(1)}, u32[]{:S(2)}, u32[]{:S(2)}) collective-permute-start(bf16[2,5,16,160]{3,2,1,0:T(8,128)(2,1)S(1)} %get-tuple-element.159), channel_id=1, source_target_pairs={{0,1},{1,2},{2,3},{3,4},{4,5},{5,6},{6,7},{7,8},{8,9},{9,10},{10,1... | collective-permute-start | bytes 153608 | tf_op jit(solution)/shard_map/ppermute | solution.py:16
  177.4 8.9 %collective-permute-done.7 = bf16[2,5,16,160]{3,2,1,0:T(8,128)(2,1)S(1)} collective-permute-done((bf16[2,5,16,160]{3,2,1,0:T(8,128)(2,1)S(1)}, bf16[2,5,16,160]{3,2,1,0:T(8,128)(2,1)S(1)}, u32[]{:S(2)}, u32[]{:S(2)}) %collective-permute-start.7) | collective-permute-done | bytes 51232 | tf_op jit(solution)/shard_map/ppermute | solution.py:19
  189.8 8.1 %all_gather.3 = f32[5,32,512]{2,1,0:T(8,128)S(1)} all-gather(f32[5,32,128]{2,1,0:T(8,128)S(1)} %fusion.43), channel_id=1, replica_groups=mesh['shell'=4,'tile'=64] {'shell'}, dimensions={2}, use_global_device_ids=true | all-gather | bytes 409600 | tf_op jit(solution)/shard_map/all_gather | solution.py:139
  (158 shorter events, 44.0 us)
Async XLA Ops:
  6.5 0.7 copy-start
  6.5 44.9 %copy-start.5 = (bf16[2,33,33]{2,0,1:T(2,128)(2,1)S(1)}, bf16[2,33,33]{2,0,1:T(2,128)(2,1)}, u32[]{:S(2)}) copy-start(bf16[2,33,33]{2,0,1:T(2,128)(2,1)} %param.15) | copy-start | bytes 13072
  6.5 26.1 %reduce-scatter.2.cloned.1.call-start = ((), (), s32[]{:S(2)}) async-start(), calls=%async_computation.3 | async-start | bytes 655360 | tf_op jit(solution)/shard_map/reduce_scatter | solution.py:97
  10.6 41.9 %copy-start.6 = (s32[32,128]{1,0:T(8,128)S(1)}, s32[32,128]{1,0:T(8,128)}, u32[]{:S(2)}) copy-start(s32[32,128]{1,0:T(8,128)} %param.16) | copy-start | bytes 49156
  33.6 10.1 %collective-permute-start = (bf16[5,32,16]{2,0,1:T(8,128)(2,1)S(1)}, bf16[5,32,16]{2,0,1:T(8,128)(2,1)S(1)}, u32[]{:S(2)}, u32[]{:S(2)}) collective-permute-start(bf16[5,32,16]{2,0,1:T(8,128)(2,1)S(1)} %get-tuple-element.164), channel_id=1, source_target_pairs={{0,64},{64,128},{128,192},{1,65},{65,129},{129,193},{2,66},{66,130... | collective-permute-start | bytes 15368 | tf_op jit(solution)/shard_map/ppermute | solution.py:16
  36.3 7.5 %collective-permute-start.1 = (bf16[5,32,16]{2,0,1:T(8,128)(2,1)S(1)}, bf16[5,32,16]{2,0,1:T(8,128)(2,1)S(1)}, u32[]{:S(2)}, u32[]{:S(2)}) collective-permute-start(bf16[5,32,16]{2,0,1:T(8,128)(2,1)S(1)} %get-tuple-element.165), channel_id=1, source_target_pairs={{64,0},{128,64},{192,128},{65,1},{129,65},{193,129},{66,2},{130,66... | collective-permute-start | bytes 15368 | tf_op jit(solution)/shard_map/ppermute | solution.py:19
  39.6 14.4 %all-to-all-start = ((f32[4,4,64,128]{3,0,2,1:T(4,128)}), f32[4,4,64,128]{3,0,2,1:T(4,128)}, u32[]{:S(2)}, u32[]{:S(2)}) async-start(f32[4,4,64,128]{3,0,2,1:T(4,128)} %pad_maximum_fusion), calls=%async_computation | async-start | bytes 1048576 | tf_op jit(solution)/shard_map/all_to_all | solution.py:114
  44.6 23.2 %collective-permute-start.2 = (bf16[5,16,160]{2,0,1:T(8,128)(2,1)}, bf16[5,16,160]{2,0,1:T(8,128)(2,1)}, u32[]{:S(2)}, u32[]{:S(2)}) collective-permute-start(bf16[5,16,160]{2,0,1:T(8,128)(2,1)} %get-tuple-element.161), channel_id=1, source_target_pairs={{0,1},{1,2},{2,3},{3,4},{4,5},{5,6},{6,7},{7,8},{8,9},{9,10},{10,1... | collective-permute-start | bytes 76808 | tf_op jit(solution)/shard_map/ppermute | solution.py:16
  49.5 18.3 %collective-permute-start.3 = (bf16[5,16,160]{2,0,1:T(8,128)(2,1)}, bf16[5,16,160]{2,0,1:T(8,128)(2,1)}, u32[]{:S(2)}, u32[]{:S(2)}) collective-permute-start(bf16[5,16,160]{2,0,1:T(8,128)(2,1)} %get-tuple-element.160), channel_id=1, source_target_pairs={{1,0},{2,1},{3,2},{4,3},{5,4},{6,5},{7,6},{8,7},{9,8},{10,9},{11,1... | collective-permute-start | bytes 76808 | tf_op jit(solution)/shard_map/ppermute | solution.py:19
  56.0 26.3 %all-to-all-start.1 = ((f32[4,4,64,128]{3,0,1,2:T(4,128)}), f32[4,4,64,128]{3,0,1,2:T(4,128)}, u32[]{:S(2)}, u32[]{:S(2)}) async-start(f32[4,4,64,128]{3,0,1,2:T(4,128)} %copy.27), calls=%async_computation.1 | async-start | bytes 1048576 | tf_op jit(solution)/shard_map/all_to_all | solution.py:113
  83.8 4.4 %copy-start.1 = (f32[8192,128]{0,1:T(8,128)}, f32[8192,128]{0,1:T(8,128)S(1)}, u32[]{:S(2)}) copy-start(f32[8192,128]{0,1:T(8,128)S(1)} %fusion.111) | copy-start | bytes 12582916 | tf_op jit(solution)/shard_map/while
  88.3 6.6 %copy-start.3 = (f32[2,160,128]{2,1,0:T(8,128)S(1)}, f32[2,160,128]{2,1,0:T(8,128)}, u32[]{:S(2)}) copy-start(f32[2,160,128]{2,1,0:T(8,128)} %get-tuple-element.208) | copy-start | bytes 491524 | tf_op jit(solution)/shard_map/while
  103.6 4.4 %copy-start.1 = (f32[8192,128]{0,1:T(8,128)}, f32[8192,128]{0,1:T(8,128)S(1)}, u32[]{:S(2)}) copy-start(f32[8192,128]{0,1:T(8,128)S(1)} %fusion.111) | copy-start | bytes 12582916 | tf_op jit(solution)/shard_map/while
  108.1 6.6 %copy-start.3 = (f32[2,160,128]{2,1,0:T(8,128)S(1)}, f32[2,160,128]{2,1,0:T(8,128)}, u32[]{:S(2)}) copy-start(f32[2,160,128]{2,1,0:T(8,128)} %get-tuple-element.208) | copy-start | bytes 491524 | tf_op jit(solution)/shard_map/while
  123.4 4.4 %copy-start.1 = (f32[8192,128]{0,1:T(8,128)}, f32[8192,128]{0,1:T(8,128)S(1)}, u32[]{:S(2)}) copy-start(f32[8192,128]{0,1:T(8,128)S(1)} %fusion.111) | copy-start | bytes 12582916 | tf_op jit(solution)/shard_map/while
  127.9 6.6 %copy-start.3 = (f32[2,160,128]{2,1,0:T(8,128)S(1)}, f32[2,160,128]{2,1,0:T(8,128)}, u32[]{:S(2)}) copy-start(f32[2,160,128]{2,1,0:T(8,128)} %get-tuple-element.208) | copy-start | bytes 491524 | tf_op jit(solution)/shard_map/while
  143.2 4.4 %copy-start.1 = (f32[8192,128]{0,1:T(8,128)}, f32[8192,128]{0,1:T(8,128)S(1)}, u32[]{:S(2)}) copy-start(f32[8192,128]{0,1:T(8,128)S(1)} %fusion.111) | copy-start | bytes 12582916 | tf_op jit(solution)/shard_map/while
  147.6 6.6 %copy-start.3 = (f32[2,160,128]{2,1,0:T(8,128)S(1)}, f32[2,160,128]{2,1,0:T(8,128)}, u32[]{:S(2)}) copy-start(f32[2,160,128]{2,1,0:T(8,128)} %get-tuple-element.208) | copy-start | bytes 491524 | tf_op jit(solution)/shard_map/while
  162.5 2.7 %collective-permute-start.4 = (bf16[2,5,32,16]{3,2,1,0:T(8,128)(2,1)S(1)}, bf16[2,5,32,16]{3,2,1,0:T(8,128)(2,1)S(1)}, u32[]{:S(2)}, u32[]{:S(2)}) collective-permute-start(bf16[2,5,32,16]{3,2,1,0:T(8,128)(2,1)S(1)} %get-tuple-element.162), channel_id=1, source_target_pairs={{0,64},{64,128},{128,192},{1,65},{65,129},{129,193},{2,66},{66,130... | collective-permute-start | bytes 30728 | tf_op jit(solution)/shard_map/ppermute | solution.py:16
  163.8 5.0 %collective-permute-start.5 = (bf16[2,5,32,16]{3,2,1,0:T(8,128)(2,1)S(1)}, bf16[2,5,32,16]{3,2,1,0:T(8,128)(2,1)S(1)}, u32[]{:S(2)}, u32[]{:S(2)}) collective-permute-start(bf16[2,5,32,16]{3,2,1,0:T(8,128)(2,1)S(1)} %get-tuple-element.163), channel_id=1, source_target_pairs={{64,0},{128,64},{192,128},{65,1},{129,65},{193,129},{66,2},{130,66... | collective-permute-start | bytes 30728 | tf_op jit(solution)/shard_map/ppermute | solution.py:19
  169.0 8.4 %collective-permute-start.6 = (bf16[2,5,16,160]{3,2,1,0:T(8,128)(2,1)S(1)}, bf16[2,5,16,160]{3,2,1,0:T(8,128)(2,1)S(1)}, u32[]{:S(2)}, u32[]{:S(2)}) collective-permute-start(bf16[2,5,16,160]{3,2,1,0:T(8,128)(2,1)S(1)} %get-tuple-element.159), channel_id=1, source_target_pairs={{0,1},{1,2},{2,3},{3,4},{4,5},{5,6},{6,7},{7,8},{8,9},{9,10},{10,1... | collective-permute-start | bytes 153608 | tf_op jit(solution)/shard_map/ppermute | solution.py:16
  174.2 12.1 %collective-permute-start.7 = (bf16[2,5,16,160]{3,2,1,0:T(8,128)(2,1)S(1)}, bf16[2,5,16,160]{3,2,1,0:T(8,128)(2,1)S(1)}, u32[]{:S(2)}, u32[]{:S(2)}) collective-permute-start(bf16[2,5,16,160]{3,2,1,0:T(8,128)(2,1)S(1)} %get-tuple-element.158), channel_id=1, source_target_pairs={{1,0},{2,1},{3,2},{4,3},{5,4},{6,5},{7,6},{8,7},{9,8},{10,9},{11,1... | collective-permute-start | bytes 153608 | tf_op jit(solution)/shard_map/ppermute | solution.py:19
  188.2 9.7 %copy-start.2 = (f32[16,32,512]{2,1,0:T(8,128)S(1)}, f32[16,32,512]{2,1,0:T(8,128)}, u32[]{:S(2)}) copy-start(f32[16,32,512]{2,1,0:T(8,128)} %param.12) | copy-start | bytes 3145732
  188.2 9.7 %copy-start.7 = (f32[16]{0:T(128)S(1)}, f32[16]{0:T(128)}, u32[]{:S(2)}) copy-start(f32[16]{0:T(128)} %param.13) | copy-start | bytes 196
  (4 other events, 2.6 us)
Sparse Core Ops, SparseCore 0:
  10.7 21.8 reduce-scatter.1
where the time goes:
time: 212 us; the launch traced here: 208 us
  matrix products  54 us (25%)
  waiting for transfers between devices  44.9 us (21%)
  starting transfers between devices  36.6 us (17%)
  local copies, waits for them, and re-layouts  36.4 us (17%)
  between operations  14.2 us (7%)
  other arithmetic  13.4 us (6%)
  blocking collectives  8.12 us (4%)
    dot_general x4, matrix products, deposit_block(): jnp.einsum('gr,kgc->krc', rows_hot, spread, precision=lax.Precision.HIGHE...  26.2 us
    convert_element_type x4, local copies, waits for them, and re-layouts, deposit_block(): cols_hot = (col_of[:, None] == lax.broadcasted_iota(jnp.int32, (codes.sha...  22.3 us
    reduce_scatter x1, waiting for transfers between devices, per_device(): lax.psum_scatter(partial_bins, 'shell', scatter_dimension=2, tiled=True)  19.8 us
    dot_general x4, matrix products, deposit_block(): jnp.einsum('gr,krc->kgc', rows_hot, shear_rows, precision=lax.Precision.H...  17.6 us
    ppermute x4, starting transfers between devices, extended(): lax.ppermute(lax.slice_in_dim(block, block.shape[dim] - width, None, axis...  14 us
    ppermute x4, waiting for transfers between devices, extended(): lax.ppermute(lax.slice_in_dim(block, 0, width, axis=dim), axis, backward)  12.4 us
    all_to_all x1, starting transfers between devices, per_device(): lax.all_to_all(lax.all_to_all(packet, 'shell', split_axis=1, concat_axis=...  11.8 us
    all_to_all x1, waiting for transfers between devices, per_device(): lax.all_to_all(lax.all_to_all(packet, 'shell', split_axis=1, concat_axis=...  11.1 us
  transfers between devices with their start and end apart: 11, of which 5 were waited for; matrix products, arithmetic and copies ran while one was open for 6% of the time, Pallas kernels for 0%

commit v1 on v0

--- a/solution.py
+++ b/solution.py
@@ -1,11 +1,16 @@
+import functools
+
 import jax
 import jax.numpy as jnp
 from jax import lax
+from jax.experimental import pallas as pl
+from jax.experimental.pallas import tpu as pltpu
 from jax.sharding import PartitionSpec as P
 
 NBIN = 5
 KER = 33
 HALF = 16
+CHUNK = 1024
 
 
 def extended(block, sides, width):
@@ -36,36 +41,55 @@
     return jnp.stack([padded[..., offset : offset + height, :] for offset in range(KER)], axis=-3)
 
 
-def deposit_block(shear_rows, codes, observed, weights, columns):
-    row_count = shear_rows.shape[1]
-    usable = codes >= 0
-    safe_codes = jnp.where(usable, codes, 0)
-    row_of = safe_codes // columns
-    col_of = safe_codes % columns
-    rows_hot = (
-        row_of[:, None] == lax.broadcasted_iota(jnp.int32, (codes.shape[0], row_count), 1)
-    ).astype(jnp.float32)
-    cols_hot = (
-        col_of[:, None] == lax.broadcasted_iota(jnp.int32, (codes.shape[0], columns), 1)
-    ).astype(jnp.float32)
-    picked = jnp.einsum(
-        "gr,krc->kgc",
-        rows_hot,
-        shear_rows,
-        precision=lax.Precision.HIGHEST,
-        preferred_element_type=jnp.float32,
-    )
-    predicted = jnp.sum(picked * cols_hot[None], axis=2)
-    scaled = jnp.where(usable, weights, 0.0)
-    residual = scaled[None] * (predicted - observed)
-    spread = residual[:, :, None] * cols_hot[None]
-    return jnp.einsum(
-        "gr,kgc->krc",
-        rows_hot,
-        spread,
-        precision=lax.Precision.HIGHEST,
-        preferred_element_type=jnp.float32,
-    )
+def split_bf16(value):
+    high = value.astype(jnp.bfloat16)
+    low = (value - high.astype(jnp.float32)).astype(jnp.bfloat16)
+    return high, low
+
+
+def scatter_kernel(rows, columns, packet_ref, out_ref):
+    out_ref[...] = jnp.zeros_like(out_ref)
+    steps = packet_ref.shape[1] // CHUNK
+
+    def body(step, carry):
+        start = pl.multiple_of(step * CHUNK, CHUNK)
+        block = packet_ref[:, pl.ds(start, CHUNK)]
+        code = block[0:1].astype(jnp.int32)
+        row_of = code >> 7
+        col_of = code & (columns - 1)
+        row_hot = (lax.broadcasted_iota(jnp.int32, (rows, CHUNK), 0) == row_of).astype(
+            jnp.bfloat16
+        )
+        col_hot = lax.broadcasted_iota(jnp.int32, (columns, CHUNK), 0) == col_of
+        zero = jnp.zeros((columns, CHUNK), jnp.bfloat16)
+        parts = []
+        for field in (1, 2, 3):
+            for piece in split_bf16(block[field : field + 1]):
+                parts.append(jnp.where(col_hot, jnp.broadcast_to(piece, (columns, CHUNK)), zero))
+        spread = jnp.concatenate(parts, axis=0)
+        out_ref[...] += lax.dot_general(
+            row_hot,
+            spread,
+            (((1,), (1,)), ((), ())),
+            preferred_element_type=jnp.float32,
+        )
+        return carry
+
+    lax.fori_loop(0, steps, body, 0)
+
+
+def deposit_sums(packet, rows, columns):
+    count = packet.shape[1]
+    flops = 2 * rows * 6 * columns * count
+    return pl.pallas_call(
+        functools.partial(scatter_kernel, rows, columns),
+        out_shape=jax.ShapeDtypeStruct((rows, 6 * columns), jnp.float32),
+        in_specs=[pl.BlockSpec(memory_space=pltpu.VMEM)],
+        out_specs=pl.BlockSpec(memory_space=pltpu.VMEM),
+        cost_estimate=pl.CostEstimate(
+            flops=flops, bytes_accessed=packet.size * 4 + rows * 6 * columns * 4, transcendentals=0
+        ),
+    )(packet)
 
 
 def per_device(
@@ -85,6 +109,27 @@
     shell_count = lax.axis_size("shell")
     columns = width // shell_count
     pixels = height * columns
+
+    slot_index = lax.broadcasted_iota(jnp.int32, gal_pix.shape, 2)
+    usable = slot_index < gal_counts[:, :, None]
+    codes = jnp.where(usable, gal_bin * pixels + gal_pix, 0).astype(jnp.float32)
+    weights = jnp.where(usable, gal_weight, 0.0)
+    packet = jnp.concatenate(
+        [codes[None], weights[None], weights[None] * gal_shape], axis=0
+    )
+    arrived = lax.all_to_all(
+        lax.all_to_all(packet, "shell", split_axis=1, concat_axis=1, tiled=True),
+        "tile",
+        split_axis=2,
+        concat_axis=2,
+        tiled=True,
+    )
+    sums = deposit_sums(arrived.reshape(4, -1), NBIN * height, columns)
+    sums = sums.reshape(NBIN, height, 6, columns)
+    sums = sums[:, :, 0::2] + sums[:, :, 1::2]
+    weight_sum = sums[:, :, 0]
+    shape_sum = jnp.stack([sums[:, :, 1], sums[:, :, 2]])
+
     sigma = shell_sigma[:, None, None]
     growth = jnp.exp(sigma * latent - 0.5 * sigma * sigma)
     partial_bins = jnp.einsum(
@@ -105,28 +150,7 @@
         forward_bands,
         preferred_element_type=jnp.float32,
     )
-    slot_index = lax.broadcasted_iota(jnp.int32, gal_pix.shape, 2)
-    codes = jnp.where(slot_index < gal_counts[:, :, None], gal_bin * pixels + gal_pix, -1).astype(
-        jnp.float32
-    )
-    packet = jnp.concatenate([codes[None], gal_shape, gal_weight[None]], axis=0)
-    arrived = lax.all_to_all(
-        lax.all_to_all(packet, "shell", split_axis=1, concat_axis=1, tiled=True),
-        "tile",
-        split_axis=2,
-        concat_axis=2,
-        tiled=True,
-    )
-    shear_rows = shear.reshape(2, NBIN * height, columns)
-    groups = arrived.shape[1]
-
-    def add_group(group, total):
-        block = lax.dynamic_index_in_dim(arrived, group, 1, keepdims=False).reshape(4, -1)
-        group_codes = block[0].astype(jnp.int32)
-        return total + deposit_block(shear_rows, group_codes, block[1:3], block[3], columns)
-
-    summed = lax.fori_loop(0, groups, add_group, jnp.zeros_like(shear_rows))
-    shear_grad = summed.reshape(2, NBIN, height, columns)
+    shear_grad = shear * weight_sum[None] - shape_sum
     masked = (shear_grad * star_mask.astype(jnp.float32)).astype(jnp.bfloat16)
     rims = extended(masked, (("shell", 3), ("tile", 2)), HALF)
     back_bands = build_bands(jnp.flip(shear_kernel, (1, 2)), columns)

time: 212 us -> 183 us (0.86)
  matrix products: 54 us -> 12.4 us
  Pallas kernels: 0 us -> 24.1 us
  waiting for transfers between devices: 44.9 us -> 32.7 us
  local copies, waits for them, and re-layouts: 36.4 us -> 43.3 us
  other arithmetic: 13.4 us -> 10 us
    dot_general x8 -> x0, matrix products: 43.8 us -> none  [the longest x4 26.2 us: deposit_block(): jnp.einsum('gr,kgc->krc', rows_hot, spread, precision=lax.Precision.HIGHE...]
    pallas_call x0 -> x1, Pallas kernels: none -> 24.1 us  [deposit_sums(): pl.pallas_call(functools.partial(scatter_kernel, rows, columns), out_shap...]
    convert_element_type x4 -> x0, local copies, waits for them, and re-layouts: 22.3 us -> none  [deposit_block(): cols_hot = (col_of[:, None] == lax.broadcasted_iota(jnp.int32, (codes.sha...]
    unnamed x73, local copies, waits for them, and re-layouts: 2.81 us -> 23 us
    all_to_all x1, waiting for transfers between devices: 11.1 us -> 0.01 us  [per_device(): lax.all_to_all(lax.all_to_all(packet, 'shell', split_axis=1, concat_axis=...]
    slice x4 -> x2, local copies, waits for them, and re-layouts: 4.17 us -> 11.8 us  [per_device(): sums = sums[:, :, 0::2] + sums[:, :, 1::2]]
    mul x4 -> x1, other arithmetic: 4.05 us -> 0.98 us  [per_device(): weights[None] * gal_shape]
    convert_element_type x5 -> x0, other arithmetic: 2.8 us -> none  [the longest x4 1.73 us: deposit_block(): cols_hot = (col_of[:, None] == lax.broadcasted_iota(jnp.int32, (codes.sha...]
  transfers between devices with their start and end apart: 11 -> 11, of which waited for: 5 -> 4; matrix products, arithmetic and copies ran while one was open for 6% -> 18% of each run, Pallas kernels for 0% -> 0%
where the time goes in v1:
time: 183 us; the launch traced here: 180 us
  local copies, waits for them, and re-layouts  43.3 us (24%)
  starting transfers between devices  35.6 us (19%)
  waiting for transfers between devices  32.7 us (18%)
  Pallas kernels  24.1 us (13%)
  between operations  14 us (8%)
  matrix products  12.4 us (7%)
  other arithmetic  10 us (5%)
  blocking collectives  8.13 us (4%)
    pallas_call x1, Pallas kernels, deposit_sums(): pl.pallas_call(functools.partial(scatter_kernel, rows, columns), out_shap...  24.1 us
    unnamed x73, local copies, waits for them, and re-layouts  23 us
    reduce_scatter x1, waiting for transfers between devices, per_device(): lax.psum_scatter(partial_bins, 'shell', scatter_dimension=2, tiled=True)  17.9 us
    ppermute x4, waiting for transfers between devices, extended(): lax.ppermute(lax.slice_in_dim(block, 0, width, axis=dim), axis, backward)  13.1 us
    ppermute x4, starting transfers between devices, extended(): lax.ppermute(lax.slice_in_dim(block, block.shape[dim] - width, None, axis...  13.1 us
    all_to_all x1, starting transfers between devices, per_device(): lax.all_to_all(lax.all_to_all(packet, 'shell', split_axis=1, concat_axis=...  11.8 us
    slice x2, local copies, waits for them, and re-layouts, per_device(): sums = sums[:, :, 0::2] + sums[:, :, 1::2]  11.8 us
    all_gather x1, blocking collectives, per_device(): full_grad = lax.all_gather(bin_grad, 'shell', axis=2, tiled=True)  8.13 us
  transfers between devices with their start and end apart: 11, of which 4 were waited for; matrix products, arithmetic and copies ran while one was open for 18% of the time, Pallas kernels for 0%

profile of v1, /device:TPU:124, one launch (start us, length us, event | category | flops | bytes accessed | tf_op | source)
XLA Modules:
  0.0 180.3 jit_solution(12222331154668740605)
XLA Ops:
  7.2 3.4 %convolution_bitcast_fusion.1 = f32[5,32,512]{2,0,1:T(8,128)} fusion(f32[16,32,512]{2,1,0:T(8,128)} %param.10, f32[16]{0:T(128)S(1)} %multiply_multiply_fusion, f32[16]{0:T(128)} %param.11, f32[5,16]{1,0:T(8,128)S(1)} %copy-done), kind=kOutput, calls=%fused_computation.14 | convolution fusion | flops 16515072 | bytes 1376704 | tf_op jit(solution)/shard_map/bs,srw->brw/dot_general | solution.py:135
  14.7 17.9 %reduce-scatter.2.cloned.1.call-done = f32[5,32,128]{2,0,1:T(8,128)} async-done(((f32[5,32,512]{2,0,1:T(8,128)}), f32[5,32,128]{2,0,1:T(8,128)}) %reduce-scatter.2.cloned.1.call-update) | async-done | bytes 81936 | tf_op jit(solution)/shard_map/reduce_scatter | solution.py:142
  33.6 2.6 %collective-permute-start = (bf16[5,32,16]{2,0,1:T(8,128)(2,1)S(1)}, bf16[5,32,16]{2,0,1:T(8,128)(2,1)S(1)}, u32[]{:S(2)}, u32[]{:S(2)}) collective-permute-start(bf16[5,32,16]{2,0,1:T(8,128)(2,1)S(1)} %get-tuple-element.18), channel_id=1, source_target_pairs={{0,64},{64,128},{128,192},{1,65},{65,129},{129,193},{2,66},{66,130... | collective-permute-start | bytes 15368 | tf_op jit(solution)/shard_map/ppermute | solution.py:21
  36.3 1.3 collective-permute-start.1
  38.4 4.1 %all-to-all-start = ((f32[4,4,64,128]{3,2,0,1:T(8,128)}), f32[4,4,64,128]{3,2,0,1:T(8,128)}, u32[]{:S(2)}, u32[]{:S(2)}) async-start(f32[4,4,64,128]{3,2,0,1:T(8,128)} %pad_maximum_fusion), calls=%async_computation.1 | async-start | bytes 1048576 | tf_op jit(solution)/shard_map/all_to_all | solution.py:121
  43.4 4.9 %collective-permute-start.2 = (bf16[5,16,160]{2,0,1:T(8,128)(2,1)}, bf16[5,16,160]{2,0,1:T(8,128)(2,1)}, u32[]{:S(2)}, u32[]{:S(2)}) collective-permute-start(bf16[5,16,160]{2,0,1:T(8,128)(2,1)} %get-tuple-element.15), channel_id=1, source_target_pairs={{0,1},{1,2},{2,3},{3,4},{4,5},{5,6},{6,7},{7,8},{8,9},{9,10},{10,1... | collective-permute-start | bytes 76808 | tf_op jit(solution)/shard_map/ppermute | solution.py:21
  48.2 1.9 %collective-permute-start.3 = (bf16[5,16,160]{2,0,1:T(8,128)(2,1)}, bf16[5,16,160]{2,0,1:T(8,128)(2,1)}, u32[]{:S(2)}, u32[]{:S(2)}) collective-permute-start(bf16[5,16,160]{2,0,1:T(8,128)(2,1)} %get-tuple-element.14), channel_id=1, source_target_pairs={{1,0},{2,1},{3,2},{4,3},{5,4},{6,5},{7,6},{8,7},{9,8},{10,9},{11,1... | collective-permute-start | bytes 76808 | tf_op jit(solution)/shard_map/ppermute | solution.py:24
  51.2 1.6 all-to-all-done
  52.8 2.2 %copy.27 = f32[4,4,64,128]{3,1,0,2:T(4,128)} copy(f32[4,4,64,128]{3,2,0,1:T(8,128)} %all-to-all-done) | data formatting | bytes 1048576 | tf_op jit(solution)/shard_map/all_to_all | solution.py:121
  55.0 11.8 %all-to-all-start.1 = ((f32[4,4,64,128]{3,1,0,2:T(4,128)}), f32[4,4,64,128]{3,1,0,2:T(4,128)}, u32[]{:S(2)}, u32[]{:S(2)}) async-start(f32[4,4,64,128]{3,1,0,2:T(4,128)} %copy.27), calls=%async_computation.2 | async-start | bytes 1048576 | tf_op jit(solution)/shard_map/all_to_all | solution.py:120
  92.2 24.1 %shard_map.100 = f32[160,768]{1,0:T(8,128)} custom-call(f32[4,32768]{1,0:T(4,128)} %bitcast.344), custom_call_target="tpu_custom_call" | custom-call | flops 8053063680 | bytes 1015808 | tf_op jit(solution)/shard_map/pallas_call | solution.py:84
  116.3 1.9 %reshape.15 = f32[5,32,6,128]{3,2,1,0:T(8,128)} reshape(f32[160,768]{1,0:T(8,128)} %shard_map.100) | data formatting | bytes 983040 | tf_op jit(solution)/shard_map/reshape | solution.py:128
  118.2 5.9 %slice.331 = f32[5,32,3,128]{3,2,1,0:T(4,128)} slice(f32[5,32,6,128]{3,2,1,0:T(8,128)} %reshape.15), slice={[0:5:1], [0:32:1], [0:6:2], [0:128:1]} | slice | bytes 491520 | tf_op jit(solution)/shard_map/slice | solution.py:129
  124.1 5.9 %slice.332 = f32[5,32,3,128]{3,2,1,0:T(4,128)} slice(f32[5,32,6,128]{3,2,1,0:T(8,128)} %reshape.15), slice={[0:5:1], [0:32:1], [1:6:2], [0:128:1]} | slice | bytes 491520 | tf_op jit(solution)/shard_map/slice | solution.py:129
  131.2 3.8 %fusion.36 = bf16[2,5,32,128]{3,2,1,0:T(8,128)(2,1)S(1)} fusion(bf16[5,33,32,160]{3,0,2,1:T(8,128)(2,1)} %constant_dynamic-update-slice_fusion, bf16[2,33,160,128,1]{3,1,0,2,4:T(8,128)(2,1)S(1)} %convert_bitcast_fusion.1, f32[1,5,32,128]{3,2,1,0:T(8,128)S(1)} %get-tuple-element.8, f32[1,5,32,128]{3,2,1,0:T(8,128)S(1)} %get-tuple-element.9, ...), kind=kOutput, calls=%fused_computation.19 | convolution fusion | flops 432742400 | bytes 4737024 | tf_op jit(solution)/shard_map/bdrj,kdjc->kbrc/dot_general | solution.py:147
  135.1 1.6 collective-permute-start.4
  138.2 4.2 %collective-permute-done.5 = bf16[2,5,32,16]{3,2,1,0:T(8,128)(2,1)S(1)} collective-permute-done((bf16[2,5,32,16]{3,2,1,0:T(8,128)(2,1)S(1)}, bf16[2,5,32,16]{3,2,1,0:T(8,128)(2,1)S(1)}, u32[]{:S(2)}, u32[]{:S(2)}) %collective-permute-start.5) | collective-permute-done | bytes 10272 | tf_op jit(solution)/shard_map/ppermute | solution.py:24
  142.5 4.0 %collective-permute-start.6 = (bf16[2,5,16,160]{3,2,1,0:T(8,128)(2,1)S(1)}, bf16[2,5,16,160]{3,2,1,0:T(8,128)(2,1)S(1)}, u32[]{:S(2)}, u32[]{:S(2)}) collective-permute-start(bf16[2,5,16,160]{3,2,1,0:T(8,128)(2,1)S(1)} %get-tuple-element.13), channel_id=1, source_target_pairs={{0,1},{1,2},{2,3},{3,4},{4,5},{5,6},{6,7},{7,8},{8,9},{9,10},{10,1... | collective-permute-start | bytes 153608 | tf_op jit(solution)/shard_map/ppermute | solution.py:21
  146.5 2.1 %collective-permute-start.7 = (bf16[2,5,16,160]{3,2,1,0:T(8,128)(2,1)S(1)}, bf16[2,5,16,160]{3,2,1,0:T(8,128)(2,1)S(1)}, u32[]{:S(2)}, u32[]{:S(2)}) collective-permute-start(bf16[2,5,16,160]{3,2,1,0:T(8,128)(2,1)S(1)} %get-tuple-element.12), channel_id=1, source_target_pairs={{1,0},{2,1},{3,2},{4,3},{5,4},{6,5},{7,6},{8,7},{9,8},{10,9},{11,1... | collective-permute-start | bytes 153608 | tf_op jit(solution)/shard_map/ppermute | solution.py:24
  149.6 8.9 %collective-permute-done.7 = bf16[2,5,16,160]{3,2,1,0:T(8,128)(2,1)S(1)} collective-permute-done((bf16[2,5,16,160]{3,2,1,0:T(8,128)(2,1)S(1)}, bf16[2,5,16,160]{3,2,1,0:T(8,128)(2,1)S(1)}, u32[]{:S(2)}, u32[]{:S(2)}) %collective-permute-start.7) | collective-permute-done | bytes 51232 | tf_op jit(solution)/shard_map/ppermute | solution.py:24
  160.5 1.6 fusion.41
  162.1 8.1 %all_gather.3 = f32[5,32,512]{2,1,0:T(8,128)S(1)} all-gather(f32[5,32,128]{2,1,0:T(8,128)S(1)} %fusion.41), channel_id=1, replica_groups=mesh['shell'=4,'tile'=64] {'shell'}, dimensions={2}, use_global_device_ids=true | all-gather | bytes 409600 | tf_op jit(solution)/shard_map/all_gather | solution.py:163
  170.2 1.7 fusion.15
  171.9 1.6 copy.34
  (109 shorter events, 39.3 us)
Async XLA Ops:
  6.5 0.7 copy-start
  6.5 43.6 %copy-start.2 = (bf16[2,33,33]{2,0,1:T(2,128)(2,1)S(1)}, bf16[2,33,33]{2,0,1:T(2,128)(2,1)}, u32[]{:S(2)}) copy-start(bf16[2,33,33]{2,0,1:T(2,128)(2,1)} %param.13) | copy-start | bytes 13072
  6.5 26.1 %reduce-scatter.2.cloned.1.call-start = ((), (), s32[]{:S(2)}) async-start(), calls=%async_computation.3 | async-start | bytes 655360 | tf_op jit(solution)/shard_map/reduce_scatter | solution.py:142
  10.6 40.6 %copy-start.3 = (s32[32,128]{1,0:T(8,128)S(1)}, s32[32,128]{1,0:T(8,128)}, u32[]{:S(2)}) copy-start(s32[32,128]{1,0:T(8,128)} %param.14) | copy-start | bytes 49156
  33.6 8.9 %collective-permute-start = (bf16[5,32,16]{2,0,1:T(8,128)(2,1)S(1)}, bf16[5,32,16]{2,0,1:T(8,128)(2,1)S(1)}, u32[]{:S(2)}, u32[]{:S(2)}) collective-permute-start(bf16[5,32,16]{2,0,1:T(8,128)(2,1)S(1)} %get-tuple-element.18), channel_id=1, source_target_pairs={{0,64},{64,128},{128,192},{1,65},{65,129},{129,193},{2,66},{66,130... | collective-permute-start | bytes 15368 | tf_op jit(solution)/shard_map/ppermute | solution.py:21
  36.3 6.3 %collective-permute-start.1 = (bf16[5,32,16]{2,0,1:T(8,128)(2,1)S(1)}, bf16[5,32,16]{2,0,1:T(8,128)(2,1)S(1)}, u32[]{:S(2)}, u32[]{:S(2)}) collective-permute-start(bf16[5,32,16]{2,0,1:T(8,128)(2,1)S(1)} %get-tuple-element.19), channel_id=1, source_target_pairs={{64,0},{128,64},{192,128},{65,1},{129,65},{193,129},{66,2},{130,66... | collective-permute-start | bytes 15368 | tf_op jit(solution)/shard_map/ppermute | solution.py:24
  38.4 14.4 %all-to-all-start = ((f32[4,4,64,128]{3,2,0,1:T(8,128)}), f32[4,4,64,128]{3,2,0,1:T(8,128)}, u32[]{:S(2)}, u32[]{:S(2)}) async-start(f32[4,4,64,128]{3,2,0,1:T(8,128)} %pad_maximum_fusion), calls=%async_computation.1 | async-start | bytes 1048576 | tf_op jit(solution)/shard_map/all_to_all | solution.py:121
  43.4 23.4 %collective-permute-start.2 = (bf16[5,16,160]{2,0,1:T(8,128)(2,1)}, bf16[5,16,160]{2,0,1:T(8,128)(2,1)}, u32[]{:S(2)}, u32[]{:S(2)}) collective-permute-start(bf16[5,16,160]{2,0,1:T(8,128)(2,1)} %get-tuple-element.15), channel_id=1, source_target_pairs={{0,1},{1,2},{2,3},{3,4},{4,5},{5,6},{6,7},{7,8},{8,9},{9,10},{10,1... | collective-permute-start | bytes 76808 | tf_op jit(solution)/shard_map/ppermute | solution.py:21
  48.2 18.6 %collective-permute-start.3 = (bf16[5,16,160]{2,0,1:T(8,128)(2,1)}, bf16[5,16,160]{2,0,1:T(8,128)(2,1)}, u32[]{:S(2)}, u32[]{:S(2)}) collective-permute-start(bf16[5,16,160]{2,0,1:T(8,128)(2,1)} %get-tuple-element.14), channel_id=1, source_target_pairs={{1,0},{2,1},{3,2},{4,3},{5,4},{6,5},{7,6},{8,7},{9,8},{10,9},{11,1... | collective-permute-start | bytes 76808 | tf_op jit(solution)/shard_map/ppermute | solution.py:24
  55.0 34.9 %all-to-all-start.1 = ((f32[4,4,64,128]{3,1,0,2:T(4,128)}), f32[4,4,64,128]{3,1,0,2:T(4,128)}, u32[]{:S(2)}, u32[]{:S(2)}) async-start(f32[4,4,64,128]{3,1,0,2:T(4,128)} %copy.27), calls=%async_computation.2 | async-start | bytes 1048576 | tf_op jit(solution)/shard_map/all_to_all | solution.py:120
  135.1 3.1 %collective-permute-start.4 = (bf16[2,5,32,16]{3,2,1,0:T(8,128)(2,1)S(1)}, bf16[2,5,32,16]{3,2,1,0:T(8,128)(2,1)S(1)}, u32[]{:S(2)}, u32[]{:S(2)}) collective-permute-start(bf16[2,5,32,16]{3,2,1,0:T(8,128)(2,1)S(1)} %get-tuple-element.16), channel_id=1, source_target_pairs={{0,64},{64,128},{128,192},{1,65},{65,129},{129,193},{2,66},{66,130... | collective-permute-start | bytes 30728 | tf_op jit(solution)/shard_map/ppermute | solution.py:21
  136.7 5.6 %collective-permute-start.5 = (bf16[2,5,32,16]{3,2,1,0:T(8,128)(2,1)S(1)}, bf16[2,5,32,16]{3,2,1,0:T(8,128)(2,1)S(1)}, u32[]{:S(2)}, u32[]{:S(2)}) collective-permute-start(bf16[2,5,32,16]{3,2,1,0:T(8,128)(2,1)S(1)} %get-tuple-element.17), channel_id=1, source_target_pairs={{64,0},{128,64},{192,128},{65,1},{129,65},{193,129},{66,2},{130,66... | collective-permute-start | bytes 30728 | tf_op jit(solution)/shard_map/ppermute | solution.py:24
  142.5 7.1 %collective-permute-start.6 = (bf16[2,5,16,160]{3,2,1,0:T(8,128)(2,1)S(1)}, bf16[2,5,16,160]{3,2,1,0:T(8,128)(2,1)S(1)}, u32[]{:S(2)}, u32[]{:S(2)}) collective-permute-start(bf16[2,5,16,160]{3,2,1,0:T(8,128)(2,1)S(1)} %get-tuple-element.13), channel_id=1, source_target_pairs={{0,1},{1,2},{2,3},{3,4},{4,5},{5,6},{6,7},{7,8},{8,9},{9,10},{10,1... | collective-permute-start | bytes 153608 | tf_op jit(solution)/shard_map/ppermute | solution.py:21
  146.5 12.1 %collective-permute-start.7 = (bf16[2,5,16,160]{3,2,1,0:T(8,128)(2,1)S(1)}, bf16[2,5,16,160]{3,2,1,0:T(8,128)(2,1)S(1)}, u32[]{:S(2)}, u32[]{:S(2)}) collective-permute-start(bf16[2,5,16,160]{3,2,1,0:T(8,128)(2,1)S(1)} %get-tuple-element.12), channel_id=1, source_target_pairs={{1,0},{2,1},{3,2},{4,3},{5,4},{6,5},{7,6},{8,7},{9,8},{10,9},{11,1... | collective-permute-start | bytes 153608 | tf_op jit(solution)/shard_map/ppermute | solution.py:24
  160.5 9.7 %copy-start.1 = (f32[16,32,512]{2,1,0:T(8,128)S(1)}, f32[16,32,512]{2,1,0:T(8,128)}, u32[]{:S(2)}) copy-start(f32[16,32,512]{2,1,0:T(8,128)} %param.10) | copy-start | bytes 3145732
  160.5 9.7 %copy-start.4 = (f32[16]{0:T(128)S(1)}, f32[16]{0:T(128)}, u32[]{:S(2)}) copy-start(f32[16]{0:T(128)} %param.11) | copy-start | bytes 196
Sparse Core Ops, SparseCore 0:
  10.7 21.8 reduce-scatter.1

commit v2 on v1

--- a/solution.py
+++ b/solution.py
@@ -47,8 +47,8 @@
     return high, low
 
 
-def scatter_kernel(rows, columns, packet_ref, out_ref):
-    out_ref[...] = jnp.zeros_like(out_ref)
+def scatter_kernel(rows, columns, packet_ref, out_ref, acc_ref):
+    acc_ref[...] = jnp.zeros_like(acc_ref)
     steps = packet_ref.shape[1] // CHUNK
 
     def body(step, carry):
@@ -62,12 +62,14 @@
         )
         col_hot = lax.broadcasted_iota(jnp.int32, (columns, CHUNK), 0) == col_of
         zero = jnp.zeros((columns, CHUNK), jnp.bfloat16)
-        parts = []
-        for field in (1, 2, 3):
-            for piece in split_bf16(block[field : field + 1]):
-                parts.append(jnp.where(col_hot, jnp.broadcast_to(piece, (columns, CHUNK)), zero))
+        pieces = [split_bf16(block[field : field + 1]) for field in (1, 2, 3)]
+        parts = [
+            jnp.where(col_hot, jnp.broadcast_to(piece[half], (columns, CHUNK)), zero)
+            for half in (0, 1)
+            for piece in pieces
+        ]
         spread = jnp.concatenate(parts, axis=0)
-        out_ref[...] += lax.dot_general(
+        acc_ref[...] += lax.dot_general(
             row_hot,
             spread,
             (((1,), (1,)), ((), ())),
@@ -76,6 +78,11 @@
         return carry
 
     lax.fori_loop(0, steps, body, 0)
+    for field in range(3):
+        out_ref[field] = (
+            acc_ref[:, field * columns : (field + 1) * columns]
+            + acc_ref[:, (field + 3) * columns : (field + 4) * columns]
+        )
 
 
 def deposit_sums(packet, rows, columns):
@@ -83,11 +90,12 @@
     flops = 2 * rows * 6 * columns * count
     return pl.pallas_call(
         functools.partial(scatter_kernel, rows, columns),
-        out_shape=jax.ShapeDtypeStruct((rows, 6 * columns), jnp.float32),
+        out_shape=jax.ShapeDtypeStruct((3, rows, columns), jnp.float32),
         in_specs=[pl.BlockSpec(memory_space=pltpu.VMEM)],
         out_specs=pl.BlockSpec(memory_space=pltpu.VMEM),
+        scratch_shapes=[pltpu.VMEM((rows, 6 * columns), jnp.float32)],
         cost_estimate=pl.CostEstimate(
-            flops=flops, bytes_accessed=packet.size * 4 + rows * 6 * columns * 4, transcendentals=0
+            flops=flops, bytes_accessed=packet.size * 4 + rows * 3 * columns * 4, transcendentals=0
         ),
     )(packet)
 
@@ -125,10 +133,9 @@
         tiled=True,
     )
     sums = deposit_sums(arrived.reshape(4, -1), NBIN * height, columns)
-    sums = sums.reshape(NBIN, height, 6, columns)
-    sums = sums[:, :, 0::2] + sums[:, :, 1::2]
-    weight_sum = sums[:, :, 0]
-    shape_sum = jnp.stack([sums[:, :, 1], sums[:, :, 2]])
+    sums = sums.reshape(3, NBIN, height, columns)
+    weight_sum = sums[0]
+    shape_sum = sums[1:]
 
     sigma = shell_sigma[:, None, None]
     growth = jnp.exp(sigma * latent - 0.5 * sigma * sigma)
@@ -139,10 +146,13 @@
         precision=lax.Precision.HIGHEST,
         preferred_element_type=jnp.float32,
     )
-    bin_map = lax.psum_scatter(partial_bins, "shell", scatter_dimension=2, tiled=True).astype(
-        jnp.bfloat16
-    )
-    padded = extended(bin_map, (("shell", 2), ("tile", 1)), HALF)
+    wide = jnp.pad(partial_bins, ((0, 0), (0, 0), (HALF, HALF)))
+    windows = jnp.stack(
+        [wide[:, :, owner * columns : owner * columns + columns + 2 * HALF] for owner in range(shell_count)]
+    )
+    gathered = lax.all_to_all(windows, "shell", split_axis=0, concat_axis=0, tiled=True)
+    bin_map = jnp.sum(gathered, axis=0).astype(jnp.bfloat16)
+    padded = extended(bin_map, (("tile", 1),), HALF)
     forward_bands = build_bands(shear_kernel, columns)
     shear = jnp.einsum(
         "bdrj,kdjc->kbrc",

time: 183 us -> 149 us (0.81)
  the two profiles are of different devices: /device:TPU:124 before, /device:TPU:31 now
where the time goes in v2:
time: 149 us
  starting transfers between devices  45 us (30%)
  Pallas kernels  23.9 us (16%)
  other arithmetic  23.8 us (16%)
  waiting for transfers between devices  22.7 us (15%)
  local copies, waits for them, and re-layouts  11.6 us (8%)
  matrix products  10.9 us (7%)
  blocking collectives  10.1 us (7%)
    pallas_call x1, Pallas kernels, deposit_sums(): pl.pallas_call(functools.partial(scatter_kernel, rows, columns), out_shap...  23.9 us
    unnamed x32, other arithmetic  20.8 us
    all_to_all x1, starting transfers between devices, per_device(): lax.all_to_all(lax.all_to_all(packet, 'shell', split_axis=1, concat_axis=...  14.8 us
    all_gather x1, blocking collectives, per_device(): full_grad = lax.all_gather(bin_grad, 'shell', axis=2, tiled=True)  10.1 us
    ppermute x3, starting transfers between devices, extended(): lax.ppermute(lax.slice_in_dim(block, block.shape[dim] - width, None, axis...  10.1 us
    ppermute x3, starting transfers between devices, extended(): lax.ppermute(lax.slice_in_dim(block, 0, width, axis=dim), axis, backward)  9.5 us
    all_to_all x1, waiting for transfers between devices, per_device(): lax.all_to_all(lax.all_to_all(packet, 'shell', split_axis=1, concat_axis=...  8.27 us
    ppermute x3, waiting for transfers between devices, extended(): lax.ppermute(lax.slice_in_dim(block, 0, width, axis=dim), axis, backward)  7.31 us
  transfers between devices with their start and end apart: 9, of which 4 were waited for; matrix products, arithmetic and copies ran while one was open for 17% of the time, Pallas kernels for 0%

profile of v2, /device:TPU:31, one launch (start us, length us, event | category | flops | bytes accessed | tf_op | source)
XLA Modules:
  0.0 148.6 jit_solution(17666427843660363552)
XLA Ops:
  0.7 2.6 %convolution_bitcast_fusion.1 = f32[5,32,512]{2,0,1:T(8,128)S(1)} fusion(f32[16,32,512]{2,1,0:T(8,128)} %param.10, f32[16]{0:T(128)S(1)} %multiply_multiply_fusion, f32[16]{0:T(128)} %param.11, f32[5,16]{1,0:T(8,128)S(1)} %copy-done), kind=kOutput, calls=%fused_computation.13 | convolution fusion | flops 16515072 | bytes 1376704 | tf_op jit(solution)/shard_map/bs,srw->brw/dot_general | solution.py:142
  3.8 1.0 copy.88
  4.8 4.7 %all-to-all-start = ((f32[4,5,32,160]{3,2,1,0:T(8,128)}), f32[4,5,32,160]{3,2,1,0:T(8,128)S(1)}, u32[]{:S(2)}, u32[]{:S(2)}) async-start(f32[4,5,32,160]{3,2,1,0:T(8,128)} %copy.88), calls=%async_computation | async-start | bytes 1310720 | tf_op jit(solution)/shard_map/all_to_all | solution.py:153
  10.8 7.1 %all-to-all-done = f32[4,5,32,160]{3,2,1,0:T(8,128)S(1)} async-done(((f32[4,5,32,160]{3,2,1,0:T(8,128)}), f32[4,5,32,160]{3,2,1,0:T(8,128)S(1)}, u32[]{:S(2)}, u32[]{:S(2)}) %all-to-all-start) | async-done | bytes 409632 | tf_op jit(solution)/shard_map/all_to_all | solution.py:153
  17.9 5.9 %all-to-all-start.1 = ((f32[4,4,64,128]{3,2,0,1:T(8,128)}), f32[4,4,64,128]{3,2,0,1:T(8,128)}, u32[]{:S(2)}, u32[]{:S(2)}) async-start(f32[4,4,64,128]{3,2,0,1:T(8,128)} %pad_maximum_fusion.1), calls=%async_computation.1 | async-start | bytes 1048576 | tf_op jit(solution)/shard_map/all_to_all | solution.py:129
  23.9 3.8 %collective-permute-start = (bf16[5,16,160]{2,1,0:T(8,128)(2,1)S(1)}, bf16[5,16,160]{2,1,0:T(8,128)(2,1)S(1)}, u32[]{:S(2)}, u32[]{:S(2)}) collective-permute-start(bf16[5,16,160]{2,1,0:T(8,128)(2,1)S(1)} %get-tuple-element.16), channel_id=1, source_target_pairs={{0,1},{1,2},{2,3},{3,4},{4,5},{5,6},{6,7},{7,8},{8,9},{9,10},{10,1... | collective-permute-start | bytes 76808 | tf_op jit(solution)/shard_map/ppermute | solution.py:21
  28.7 1.9 %collective-permute-start.1 = (bf16[5,16,160]{2,1,0:T(8,128)(2,1)S(1)}, bf16[5,16,160]{2,1,0:T(8,128)(2,1)S(1)}, u32[]{:S(2)}, u32[]{:S(2)}) collective-permute-start(bf16[5,16,160]{2,1,0:T(8,128)(2,1)S(1)} %get-tuple-element.15), channel_id=1, source_target_pairs={{1,0},{2,1},{3,2},{4,3},{5,4},{6,5},{7,6},{8,7},{9,8},{10,9},{11,1... | collective-permute-start | bytes 76808 | tf_op jit(solution)/shard_map/ppermute | solution.py:24
  46.0 2.2 %copy.126 = f32[4,4,64,128]{3,1,0,2:T(4,128)} copy(f32[4,4,64,128]{3,2,0,1:T(8,128)} %all-to-all-done.1) | data formatting | bytes 1048576 | tf_op jit(solution)/shard_map/all_to_all | solution.py:129
  48.1 14.8 %all-to-all-start.2 = ((f32[4,4,64,128]{3,1,0,2:T(4,128)}), f32[4,4,64,128]{3,1,0,2:T(4,128)}, u32[]{:S(2)}, u32[]{:S(2)}) async-start(f32[4,4,64,128]{3,1,0,2:T(4,128)} %copy.126), calls=%async_computation.2 | async-start | bytes 1048576 | tf_op jit(solution)/shard_map/all_to_all | solution.py:128
  69.6 8.3 %all-to-all-done.2 = f32[4,4,64,128]{3,1,0,2:T(4,128)} async-done(((f32[4,4,64,128]{3,1,0,2:T(4,128)}), f32[4,4,64,128]{3,1,0,2:T(4,128)}, u32[]{:S(2)}, u32[]{:S(2)}) %all-to-all-start.2) | async-done | bytes 524320 | tf_op jit(solution)/shard_map/all_to_all | solution.py:128
  77.9 1.2 copy.127
  79.1 1.1 copy.181
  80.2 23.9 %shard_map.100 = f32[3,160,128]{2,1,0:T(8,128)} custom-call(f32[4,32768]{1,0:T(4,128)} %bitcast.412), custom_call_target="tpu_custom_call" | custom-call | flops 8053063680 | bytes 770048 | tf_op jit(solution)/shard_map/pallas_call | solution.py:91
  106.0 3.0 %fusion.35 = bf16[2,5,32,128]{3,2,1,0:T(8,128)(2,1)S(1)} fusion(f32[2,5,32,128]{3,2,1,0:T(8,128)S(1)} %bitcast.413, bf16[5,33,32,160]{3,2,1,0:T(8,128)(2,1)} %constant_dynamic-update-slice_fusion, bf16[2,33,160,128,1]{3,1,0,2,4:T(8,128)(2,1)S(1)} %convert_bitcast_fusion.1, f32[32,128]{1,0:T(8,128)S(1)} %convert_element_type.43, f32[5,32,128]{2,1,0:T(8,128)S(1)} %bitcast.414), kind=kOutput, calls=%fused_computation.18 | convolution fusion | flops 432701440 | bytes 4737024 | tf_op jit(solution)/shard_map/bdrj,kdjc->kbrc/dot_general | solution.py:157
  109.1 1.3 collective-permute-start.2
  110.4 5.5 %collective-permute-start.3 = (bf16[2,5,32,16]{3,2,1,0:T(8,128)(2,1)S(1)}, bf16[2,5,32,16]{3,2,1,0:T(8,128)(2,1)S(1)}, u32[]{:S(2)}, u32[]{:S(2)}) collective-permute-start(bf16[2,5,32,16]{3,2,1,0:T(8,128)(2,1)S(1)} %get-tuple-element.14), channel_id=1, source_target_pairs={{64,0},{128,64},{192,128},{65,1},{129,65},{193,129},{66,2},{130,66... | collective-permute-start | bytes 30728 | tf_op jit(solution)/shard_map/ppermute | solution.py:24
  117.0 5.0 %collective-permute-start.4 = (bf16[2,5,16,160]{3,2,1,0:T(8,128)(2,1)S(1)}, bf16[2,5,16,160]{3,2,1,0:T(8,128)(2,1)S(1)}, u32[]{:S(2)}, u32[]{:S(2)}) collective-permute-start(bf16[2,5,16,160]{3,2,1,0:T(8,128)(2,1)S(1)} %get-tuple-element.12), channel_id=1, source_target_pairs={{0,1},{1,2},{2,3},{3,4},{4,5},{5,6},{6,7},{7,8},{8,9},{9,10},{10,1... | collective-permute-start | bytes 153608 | tf_op jit(solution)/shard_map/ppermute | solution.py:21
  122.0 2.1 %collective-permute-start.5 = (bf16[2,5,16,160]{3,2,1,0:T(8,128)(2,1)S(1)}, bf16[2,5,16,160]{3,2,1,0:T(8,128)(2,1)S(1)}, u32[]{:S(2)}, u32[]{:S(2)}) collective-permute-start(bf16[2,5,16,160]{3,2,1,0:T(8,128)(2,1)S(1)} %get-tuple-element.11), channel_id=1, source_target_pairs={{1,0},{2,1},{3,2},{4,3},{5,4},{6,5},{7,6},{8,7},{9,8},{10,9},{11,1... | collective-permute-start | bytes 153608 | tf_op jit(solution)/shard_map/ppermute | solution.py:24
  124.1 1.0 convert_bitcast_fusion
  125.2 6.6 %collective-permute-done.5 = bf16[2,5,16,160]{3,2,1,0:T(8,128)(2,1)S(1)} collective-permute-done((bf16[2,5,16,160]{3,2,1,0:T(8,128)(2,1)S(1)}, bf16[2,5,16,160]{3,2,1,0:T(8,128)(2,1)S(1)}, u32[]{:S(2)}, u32[]{:S(2)}) %collective-permute-start.5) | collective-permute-done | bytes 51232 | tf_op jit(solution)/shard_map/ppermute | solution.py:24
  133.6 1.6 %fusion.40 = f32[5,32,128]{2,1,0:T(8,128)S(1)} fusion(bf16[2,5,33,32,160]{4,3,1,0,2:T(8,128)(2,1)S(1)} %fusion.53, bf16[2,33,160,128,1]{3,1,0,2,4:T(8,128)(2,1)S(1)} %convert_bitcast_fusion), kind=kOutput, calls=%fused_computation.19 | convolution fusion | flops 432537600 | bytes 6164480 | tf_op jit(solution)/shard_map/kbdrj,kdjc->brc/dot_general | solution.py:167
  135.2 10.1 %all_gather.3 = f32[5,32,512]{2,1,0:T(8,128)S(1)} all-gather(f32[5,32,128]{2,1,0:T(8,128)S(1)} %fusion.40), channel_id=1, replica_groups=mesh['shell'=4,'tile'=64] {'shell'}, dimensions={2}, use_global_device_ids=true | all-gather | bytes 409600 | tf_op jit(solution)/shard_map/all_gather | solution.py:173
  145.3 1.7 %fusion.14 = f32[16,32,512]{2,0,1:T(8,128)S(1)} fusion(f32[16,32,512]{2,1,0:T(8,128)S(1)} %copy-done.1, f32[5,32,512]{2,1,0:T(8,128)S(1)} %all_gather.3, f32[16]{0:T(128)S(1)} %multiply_multiply_fusion, f32[16]{0:T(128)S(1)} %copy-done.9, f32[5,16]{1,0:T(8,128)S(1)} %copy-done), kind=kOutput, calls=%fused_computation.12 | convolution fusion | flops 16777216 | bytes 2425280 | tf_op jit(solution)/shard_map/bs,brw->srw/dot_general | solution.py:174
  147.0 1.6 %copy.131 = f32[16,32,512]{2,1,0:T(8,128)} copy(f32[16,32,512]{2,0,1:T(8,128)S(1)} %fusion.14) | data formatting | bytes 2097152 | tf_op jit(solution)/shard_map/mul | solution.py:181
  (111 shorter events, 30.0 us)
Async XLA Ops:
  0.0 0.7 copy-start
  3.3 6.3 %copy-start.2 = (f32[4,64,128]{2,1,0:T(8,128)S(1)}, f32[4,64,128]{2,1,0:T(8,128)}, u32[]{:S(2)}) copy-start(f32[4,64,128]{2,1,0:T(8,128)} %param.18) | copy-start | bytes 393220
  3.3 6.3 %copy-start.7 = (s32[4,64]{1,0:T(4,128)S(1)}, s32[4,64]{1,0:T(4,128)}, u32[]{:S(2)}) copy-start(s32[4,64]{1,0:T(4,128)} %param.19) | copy-start | bytes 3076
  3.3 6.4 %copy-start.3 = (f32[2,4,64,128]{3,2,1,0:T(8,128)S(1)}, f32[2,4,64,128]{3,2,1,0:T(8,128)}, u32[]{:S(2)}) copy-start(f32[2,4,64,128]{3,2,1,0:T(8,128)} %param.17) | copy-start | bytes 786436
  3.6 6.0 %copy-start.4 = (s32[4,64,128]{2,1,0:T(8,128)S(1)}, s32[4,64,128]{2,1,0:T(8,128)}, u32[]{:S(2)}) copy-start(s32[4,64,128]{2,1,0:T(8,128)} %param.15) | copy-start | bytes 393220
  3.6 6.0 %copy-start.5 = (s32[4,64,128]{2,1,0:T(8,128)S(1)}, s32[4,64,128]{2,1,0:T(8,128)}, u32[]{:S(2)}) copy-start(s32[4,64,128]{2,1,0:T(8,128)} %param.16) | copy-start | bytes 393220
  4.8 22.8 %copy-start.6 = (bf16[2,33,33]{2,0,1:T(2,128)(2,1)S(1)}, bf16[2,33,33]{2,0,1:T(2,128)(2,1)}, u32[]{:S(2)}) copy-start(bf16[2,33,33]{2,0,1:T(2,128)(2,1)} %param.13) | copy-start | bytes 13072
  4.8 13.1 %all-to-all-start = ((f32[4,5,32,160]{3,2,1,0:T(8,128)}), f32[4,5,32,160]{3,2,1,0:T(8,128)S(1)}, u32[]{:S(2)}, u32[]{:S(2)}) async-start(f32[4,5,32,160]{3,2,1,0:T(8,128)} %copy.88), calls=%async_computation | async-start | bytes 1310720 | tf_op jit(solution)/shard_map/all_to_all | solution.py:153
  9.8 18.9 %copy-start.8 = (s32[32,128]{1,0:T(8,128)S(1)}, s32[32,128]{1,0:T(8,128)}, u32[]{:S(2)}) copy-start(s32[32,128]{1,0:T(8,128)} %param.14) | copy-start | bytes 49156
  17.9 28.1 %all-to-all-start.1 = ((f32[4,4,64,128]{3,2,0,1:T(8,128)}), f32[4,4,64,128]{3,2,0,1:T(8,128)}, u32[]{:S(2)}, u32[]{:S(2)}) async-start(f32[4,4,64,128]{3,2,0,1:T(8,128)} %pad_maximum_fusion.1), calls=%async_computation.1 | async-start | bytes 1048576 | tf_op jit(solution)/shard_map/all_to_all | solution.py:129
  23.9 6.7 %collective-permute-start = (bf16[5,16,160]{2,1,0:T(8,128)(2,1)S(1)}, bf16[5,16,160]{2,1,0:T(8,128)(2,1)S(1)}, u32[]{:S(2)}, u32[]{:S(2)}) collective-permute-start(bf16[5,16,160]{2,1,0:T(8,128)(2,1)S(1)} %get-tuple-element.16), channel_id=1, source_target_pairs={{0,1},{1,2},{2,3},{3,4},{4,5},{5,6},{6,7},{7,8},{8,9},{9,10},{10,1... | collective-permute-start | bytes 76808 | tf_op jit(solution)/shard_map/ppermute | solution.py:21
  28.7 13.2 %collective-permute-start.1 = (bf16[5,16,160]{2,1,0:T(8,128)(2,1)S(1)}, bf16[5,16,160]{2,1,0:T(8,128)(2,1)S(1)}, u32[]{:S(2)}, u32[]{:S(2)}) collective-permute-start(bf16[5,16,160]{2,1,0:T(8,128)(2,1)S(1)} %get-tuple-element.15), channel_id=1, source_target_pairs={{1,0},{2,1},{3,2},{4,3},{5,4},{6,5},{7,6},{8,7},{9,8},{10,9},{11,1... | collective-permute-start | bytes 76808 | tf_op jit(solution)/shard_map/ppermute | solution.py:24
  48.1 29.8 %all-to-all-start.2 = ((f32[4,4,64,128]{3,1,0,2:T(4,128)}), f32[4,4,64,128]{3,1,0,2:T(4,128)}, u32[]{:S(2)}, u32[]{:S(2)}) async-start(f32[4,4,64,128]{3,1,0,2:T(4,128)} %copy.126), calls=%async_computation.2 | async-start | bytes 1048576 | tf_op jit(solution)/shard_map/all_to_all | solution.py:128
  109.1 6.9 %collective-permute-start.2 = (bf16[2,5,32,16]{3,2,1,0:T(8,128)(2,1)S(1)}, bf16[2,5,32,16]{3,2,1,0:T(8,128)(2,1)S(1)}, u32[]{:S(2)}, u32[]{:S(2)}) collective-permute-start(bf16[2,5,32,16]{3,2,1,0:T(8,128)(2,1)S(1)} %get-tuple-element.13), channel_id=1, source_target_pairs={{0,64},{64,128},{128,192},{1,65},{65,129},{129,193},{2,66},{66,130... | collective-permute-start | bytes 30728 | tf_op jit(solution)/shard_map/ppermute | solution.py:21
  110.4 6.4 %collective-permute-start.3 = (bf16[2,5,32,16]{3,2,1,0:T(8,128)(2,1)S(1)}, bf16[2,5,32,16]{3,2,1,0:T(8,128)(2,1)S(1)}, u32[]{:S(2)}, u32[]{:S(2)}) collective-permute-start(bf16[2,5,32,16]{3,2,1,0:T(8,128)(2,1)S(1)} %get-tuple-element.14), channel_id=1, source_target_pairs={{64,0},{128,64},{192,128},{65,1},{129,65},{193,129},{66,2},{130,66... | collective-permute-start | bytes 30728 | tf_op jit(solution)/shard_map/ppermute | solution.py:24
  117.0 8.2 %collective-permute-start.4 = (bf16[2,5,16,160]{3,2,1,0:T(8,128)(2,1)S(1)}, bf16[2,5,16,160]{3,2,1,0:T(8,128)(2,1)S(1)}, u32[]{:S(2)}, u32[]{:S(2)}) collective-permute-start(bf16[2,5,16,160]{3,2,1,0:T(8,128)(2,1)S(1)} %get-tuple-element.12), channel_id=1, source_target_pairs={{0,1},{1,2},{2,3},{3,4},{4,5},{5,6},{6,7},{7,8},{8,9},{9,10},{10,1... | collective-permute-start | bytes 153608 | tf_op jit(solution)/shard_map/ppermute | solution.py:21
  122.0 9.7 %collective-permute-start.5 = (bf16[2,5,16,160]{3,2,1,0:T(8,128)(2,1)S(1)}, bf16[2,5,16,160]{3,2,1,0:T(8,128)(2,1)S(1)}, u32[]{:S(2)}, u32[]{:S(2)}) collective-permute-start(bf16[2,5,16,160]{3,2,1,0:T(8,128)(2,1)S(1)} %get-tuple-element.11), channel_id=1, source_target_pairs={{1,0},{2,1},{3,2},{4,3},{5,4},{6,5},{7,6},{8,7},{9,8},{10,9},{11,1... | collective-permute-start | bytes 153608 | tf_op jit(solution)/shard_map/ppermute | solution.py:24
  133.6 11.7 %copy-start.1 = (f32[16,32,512]{2,1,0:T(8,128)S(1)}, f32[16,32,512]{2,1,0:T(8,128)}, u32[]{:S(2)}) copy-start(f32[16,32,512]{2,1,0:T(8,128)} %param.10) | copy-start | bytes 3145732
  133.6 11.7 %copy-start.9 = (f32[16]{0:T(128)S(1)}, f32[16]{0:T(128)}, u32[]{:S(2)}) copy-start(f32[16]{0:T(128)} %param.11) | copy-start | bytes 196

commit v3 on v2

--- a/solution.py
+++ b/solution.py
@@ -125,12 +125,9 @@
     packet = jnp.concatenate(
         [codes[None], weights[None], weights[None] * gal_shape], axis=0
     )
+    devices = packet.shape[1] * packet.shape[2]
     arrived = lax.all_to_all(
-        lax.all_to_all(packet, "shell", split_axis=1, concat_axis=1, tiled=True),
-        "tile",
-        split_axis=2,
-        concat_axis=2,
-        tiled=True,
+        packet.reshape(4, devices, -1), ("shell", "tile"), split_axis=1, concat_axis=1, tiled=True
     )
     sums = deposit_sums(arrived.reshape(4, -1), NBIN * height, columns)
     sums = sums.reshape(3, NBIN, height, columns)

time: 149 us -> 138 us (0.926)
  the two profiles are of different devices: /device:TPU:31 before, /device:TPU:124 now
where the time goes in v3:
time: 138 us; the launch traced here: 137 us
  starting transfers between devices  39.5 us (29%)
  other arithmetic  24 us (17%)
  Pallas kernels  23.9 us (17%)
  waiting for transfers between devices  22.3 us (16%)
  matrix products  10.9 us (8%)
  blocking collectives  8.13 us (6%)
  local copies, waits for them, and re-layouts  7.25 us (5%)
    pallas_call x1, Pallas kernels, deposit_sums(): pl.pallas_call(functools.partial(scatter_kernel, rows, columns), out_shap...  23.9 us
    unnamed x32, other arithmetic  20.8 us
    ppermute x3, starting transfers between devices, extended(): lax.ppermute(lax.slice_in_dim(block, block.shape[dim] - width, None, axis...  15.7 us
    all_to_all x1, starting transfers between devices, per_device(): lax.all_to_all(packet.reshape(4, devices, -1), ('shell', 'tile'), split_a...  14.8 us
    ppermute x3, waiting for transfers between devices, extended(): lax.ppermute(lax.slice_in_dim(block, 0, width, axis=dim), axis, backward)  11.8 us
    all_to_all x1, waiting for transfers between devices, per_device(): lax.all_to_all(windows, 'shell', split_axis=0, concat_axis=0, tiled=True)  8.51 us
    all_gather x1, blocking collectives, per_device(): full_grad = lax.all_gather(bin_grad, 'shell', axis=2, tiled=True)  8.13 us
    ppermute x3, starting transfers between devices, extended(): lax.ppermute(lax.slice_in_dim(block, 0, width, axis=dim), axis, backward)  5.31 us
  transfers between devices with their start and end apart: 8, of which 4 were waited for; matrix products, arithmetic and copies ran while one was open for 19% of the time, Pallas kernels for 0%

profile of v3, /device:TPU:124, one launch (start us, length us, event | category | flops | bytes accessed | tf_op | source)
XLA Modules:
  0.0 136.6 jit_solution(10920590474981178453)
XLA Ops:
  0.7 2.6 %convolution_bitcast_fusion.1 = f32[5,32,512]{2,0,1:T(8,128)S(1)} fusion(f32[16,32,512]{2,1,0:T(8,128)} %param.10, f32[16]{0:T(128)S(1)} %multiply_multiply_fusion, f32[16]{0:T(128)} %param.11, f32[5,16]{1,0:T(8,128)S(1)} %copy-done), kind=kOutput, calls=%fused_computation.13 | convolution fusion | flops 16515072 | bytes 1376704 | tf_op jit(solution)/shard_map/bs,srw->brw/dot_general | solution.py:139
  3.8 1.0 copy.85
  4.8 3.6 %all-to-all-start = ((f32[4,5,32,160]{3,2,1,0:T(8,128)}), f32[4,5,32,160]{3,2,1,0:T(8,128)S(1)}, u32[]{:S(2)}, u32[]{:S(2)}) async-start(f32[4,5,32,160]{3,2,1,0:T(8,128)} %copy.85), calls=%async_computation | async-start | bytes 1310720 | tf_op jit(solution)/shard_map/all_to_all | solution.py:150
  9.0 1.1 pad_maximum_fusion.1
  10.1 8.5 %all-to-all-done = f32[4,5,32,160]{3,2,1,0:T(8,128)S(1)} async-done(((f32[4,5,32,160]{3,2,1,0:T(8,128)}), f32[4,5,32,160]{3,2,1,0:T(8,128)S(1)}, u32[]{:S(2)}, u32[]{:S(2)}) %all-to-all-start) | async-done | bytes 409632 | tf_op jit(solution)/shard_map/all_to_all | solution.py:150
  18.6 14.8 %all-to-all-start.1 = ((f32[4,256,128]{2,0,1:T(4,128)}), f32[4,256,128]{2,0,1:T(4,128)}, u32[]{:S(2)}, u32[]{:S(2)}) async-start(f32[4,256,128]{2,0,1:T(4,128)} %pad_maximum_fusion.1), calls=%async_computation.1 | async-start | bytes 1048576 | tf_op jit(solution)/shard_map/all_to_all | solution.py:129
  33.6 4.6 %collective-permute-start = (bf16[5,16,160]{2,1,0:T(8,128)(2,1)S(1)}, bf16[5,16,160]{2,1,0:T(8,128)(2,1)S(1)}, u32[]{:S(2)}, u32[]{:S(2)}) collective-permute-start(bf16[5,16,160]{2,1,0:T(8,128)(2,1)S(1)} %get-tuple-element.16), channel_id=1, source_target_pairs={{0,1},{1,2},{2,3},{3,4},{4,5},{5,6},{6,7},{7,8},{8,9},{9,10},{10,1... | collective-permute-start | bytes 76808 | tf_op jit(solution)/shard_map/ppermute | solution.py:21
  38.2 1.0 convert_bitcast_fusion.1
  39.2 1.9 %collective-permute-start.1 = (bf16[5,16,160]{2,1,0:T(8,128)(2,1)S(1)}, bf16[5,16,160]{2,1,0:T(8,128)(2,1)S(1)}, u32[]{:S(2)}, u32[]{:S(2)}) collective-permute-start(bf16[5,16,160]{2,1,0:T(8,128)(2,1)S(1)} %get-tuple-element.15), channel_id=1, source_target_pairs={{1,0},{2,1},{3,2},{4,3},{5,4},{6,5},{7,6},{8,7},{9,8},{10,9},{11,1... | collective-permute-start | bytes 76808 | tf_op jit(solution)/shard_map/ppermute | solution.py:24
  41.2 2.0 %collective-permute-done = bf16[5,16,160]{2,1,0:T(8,128)(2,1)S(1)} collective-permute-done((bf16[5,16,160]{2,1,0:T(8,128)(2,1)S(1)}, bf16[5,16,160]{2,1,0:T(8,128)(2,1)S(1)}, u32[]{:S(2)}, u32[]{:S(2)}) %collective-permute-start) | collective-permute-done | bytes 25632 | tf_op jit(solution)/shard_map/ppermute | solution.py:21
  65.1 23.9 %shard_map.100 = f32[3,160,128]{2,1,0:T(8,128)} custom-call(f32[4,32768]{1,0:T(4,128)} %bitcast.83.packet_ref), custom_call_target="tpu_custom_call" | custom-call | flops 8053063680 | bytes 770048 | tf_op jit(solution)/shard_map/pallas_call | solution.py:91
  89.0 0.9 slice.440
  90.8 3.0 %fusion.35 = bf16[2,5,32,128]{3,2,1,0:T(8,128)(2,1)S(1)} fusion(f32[2,5,32,128]{3,2,1,0:T(8,128)S(1)} %bitcast.407, bf16[5,33,32,160]{3,2,1,0:T(8,128)(2,1)} %constant_dynamic-update-slice_fusion, bf16[2,33,160,128,1]{3,1,0,2,4:T(8,128)(2,1)S(1)} %convert_bitcast_fusion.1, f32[32,128]{1,0:T(8,128)S(1)} %convert_element_type.43, f32[5,32,128]{2,1,0:T(8,128)S(1)} %bitcast.408), kind=kOutput, calls=%fused_computation.18 | convolution fusion | flops 432701440 | bytes 4737024 | tf_op jit(solution)/shard_map/bdrj,kdjc->kbrc/dot_general | solution.py:154
  94.0 1.6 %collective-permute-start.2 = (bf16[2,5,32,16]{3,2,1,0:T(8,128)(2,1)S(1)}, bf16[2,5,32,16]{3,2,1,0:T(8,128)(2,1)S(1)}, u32[]{:S(2)}, u32[]{:S(2)}) collective-permute-start(bf16[2,5,32,16]{3,2,1,0:T(8,128)(2,1)S(1)} %get-tuple-element.13), channel_id=1, source_target_pairs={{0,64},{64,128},{128,192},{1,65},{65,129},{129,193},{2,66},{66,130... | collective-permute-start | bytes 30728 | tf_op jit(solution)/shard_map/ppermute | solution.py:21
  95.6 1.3 collective-permute-start.3
  97.0 2.9 %collective-permute-done.3 = bf16[2,5,32,16]{3,2,1,0:T(8,128)(2,1)S(1)} collective-permute-done((bf16[2,5,32,16]{3,2,1,0:T(8,128)(2,1)S(1)}, bf16[2,5,32,16]{3,2,1,0:T(8,128)(2,1)S(1)}, u32[]{:S(2)}, u32[]{:S(2)}) %collective-permute-start.3) | collective-permute-done | bytes 10272 | tf_op jit(solution)/shard_map/ppermute | solution.py:24
  100.0 9.5 %collective-permute-start.4 = (bf16[2,5,16,160]{3,2,1,0:T(8,128)(2,1)S(1)}, bf16[2,5,16,160]{3,2,1,0:T(8,128)(2,1)S(1)}, u32[]{:S(2)}, u32[]{:S(2)}) collective-permute-start(bf16[2,5,16,160]{3,2,1,0:T(8,128)(2,1)S(1)} %get-tuple-element.12), channel_id=1, source_target_pairs={{0,1},{1,2},{2,3},{3,4},{4,5},{5,6},{6,7},{7,8},{8,9},{9,10},{10,1... | collective-permute-start | bytes 153608 | tf_op jit(solution)/shard_map/ppermute | solution.py:21
  109.6 2.1 %collective-permute-start.5 = (bf16[2,5,16,160]{3,2,1,0:T(8,128)(2,1)S(1)}, bf16[2,5,16,160]{3,2,1,0:T(8,128)(2,1)S(1)}, u32[]{:S(2)}, u32[]{:S(2)}) collective-permute-start(bf16[2,5,16,160]{3,2,1,0:T(8,128)(2,1)S(1)} %get-tuple-element.11), channel_id=1, source_target_pairs={{1,0},{2,1},{3,2},{4,3},{5,4},{6,5},{7,6},{8,7},{9,8},{10,9},{11,1... | collective-permute-start | bytes 153608 | tf_op jit(solution)/shard_map/ppermute | solution.py:24
  111.7 1.0 convert_bitcast_fusion
  112.7 8.9 %collective-permute-done.5 = bf16[2,5,16,160]{3,2,1,0:T(8,128)(2,1)S(1)} collective-permute-done((bf16[2,5,16,160]{3,2,1,0:T(8,128)(2,1)S(1)}, bf16[2,5,16,160]{3,2,1,0:T(8,128)(2,1)S(1)}, u32[]{:S(2)}, u32[]{:S(2)}) %collective-permute-start.5) | collective-permute-done | bytes 51232 | tf_op jit(solution)/shard_map/ppermute | solution.py:24
  123.6 1.6 %fusion.40 = f32[5,32,128]{2,1,0:T(8,128)S(1)} fusion(bf16[2,5,33,32,160]{4,3,1,0,2:T(8,128)(2,1)S(1)} %fusion.53, bf16[2,33,160,128,1]{3,1,0,2,4:T(8,128)(2,1)S(1)} %convert_bitcast_fusion), kind=kOutput, calls=%fused_computation.19 | convolution fusion | flops 432537600 | bytes 6164480 | tf_op jit(solution)/shard_map/kbdrj,kdjc->brc/dot_general | solution.py:164
  125.1 8.1 %all_gather.3 = f32[5,32,512]{2,1,0:T(8,128)S(1)} all-gather(f32[5,32,128]{2,1,0:T(8,128)S(1)} %fusion.40), channel_id=1, replica_groups=mesh['shell'=4,'tile'=64] {'shell'}, dimensions={2}, use_global_device_ids=true | all-gather | bytes 409600 | tf_op jit(solution)/shard_map/all_gather | solution.py:170
  133.3 1.7 %fusion.14 = f32[16,32,512]{2,0,1:T(8,128)S(1)} fusion(f32[16,32,512]{2,1,0:T(8,128)S(1)} %copy-done.1, f32[5,32,512]{2,1,0:T(8,128)S(1)} %all_gather.3, f32[16]{0:T(128)S(1)} %multiply_multiply_fusion, f32[16]{0:T(128)S(1)} %copy-done.9, f32[5,16]{1,0:T(8,128)S(1)} %copy-done), kind=kOutput, calls=%fused_computation.12 | convolution fusion | flops 16777216 | bytes 2425280 | tf_op jit(solution)/shard_map/bs,brw->srw/dot_general | solution.py:171
  135.0 1.6 %copy.125 = f32[16,32,512]{2,1,0:T(8,128)} copy(f32[16,32,512]{2,0,1:T(8,128)S(1)} %fusion.14) | data formatting | bytes 2097152 | tf_op jit(solution)/shard_map/mul | solution.py:178
  (106 shorter events, 26.6 us)
Async XLA Ops:
  0.0 0.7 copy-start
  3.3 5.2 %copy-start.5 = (f32[4,64,128]{2,1,0:T(8,128)S(1)}, f32[4,64,128]{2,1,0:T(8,128)}, u32[]{:S(2)}) copy-start(f32[4,64,128]{2,1,0:T(8,128)} %param.18) | copy-start | bytes 393220
  3.3 5.2 %copy-start.8 = (s32[4,64]{1,0:T(4,128)S(1)}, s32[4,64]{1,0:T(4,128)}, u32[]{:S(2)}) copy-start(s32[4,64]{1,0:T(4,128)} %param.19) | copy-start | bytes 3076
  3.3 5.3 %copy-start.2 = (f32[2,4,64,128]{3,2,1,0:T(8,128)S(1)}, f32[2,4,64,128]{3,2,1,0:T(8,128)}, u32[]{:S(2)}) copy-start(f32[2,4,64,128]{3,2,1,0:T(8,128)} %param.17) | copy-start | bytes 786436
  3.6 5.2 %copy-start.3 = (s32[4,64,128]{2,1,0:T(8,128)S(1)}, s32[4,64,128]{2,1,0:T(8,128)}, u32[]{:S(2)}) copy-start(s32[4,64,128]{2,1,0:T(8,128)} %param.15) | copy-start | bytes 393220
  3.6 5.2 %copy-start.4 = (s32[4,64,128]{2,1,0:T(8,128)S(1)}, s32[4,64,128]{2,1,0:T(8,128)}, u32[]{:S(2)}) copy-start(s32[4,64,128]{2,1,0:T(8,128)} %param.16) | copy-start | bytes 393220
  4.8 33.4 %copy-start.6 = (bf16[2,33,33]{2,0,1:T(2,128)(2,1)S(1)}, bf16[2,33,33]{2,0,1:T(2,128)(2,1)}, u32[]{:S(2)}) copy-start(bf16[2,33,33]{2,0,1:T(2,128)(2,1)} %param.13) | copy-start | bytes 13072
  4.8 13.8 %all-to-all-start = ((f32[4,5,32,160]{3,2,1,0:T(8,128)}), f32[4,5,32,160]{3,2,1,0:T(8,128)S(1)}, u32[]{:S(2)}, u32[]{:S(2)}) async-start(f32[4,5,32,160]{3,2,1,0:T(8,128)} %copy.85), calls=%async_computation | async-start | bytes 1310720 | tf_op jit(solution)/shard_map/all_to_all | solution.py:150
  8.8 30.4 %copy-start.7 = (s32[32,128]{1,0:T(8,128)S(1)}, s32[32,128]{1,0:T(8,128)}, u32[]{:S(2)}) copy-start(s32[32,128]{1,0:T(8,128)} %param.14) | copy-start | bytes 49156
  18.6 46.5 %all-to-all-start.1 = ((f32[4,256,128]{2,0,1:T(4,128)}), f32[4,256,128]{2,0,1:T(4,128)}, u32[]{:S(2)}, u32[]{:S(2)}) async-start(f32[4,256,128]{2,0,1:T(4,128)} %pad_maximum_fusion.1), calls=%async_computation.1 | async-start | bytes 1048576 | tf_op jit(solution)/shard_map/all_to_all | solution.py:129
  33.6 9.6 %collective-permute-start = (bf16[5,16,160]{2,1,0:T(8,128)(2,1)S(1)}, bf16[5,16,160]{2,1,0:T(8,128)(2,1)S(1)}, u32[]{:S(2)}, u32[]{:S(2)}) collective-permute-start(bf16[5,16,160]{2,1,0:T(8,128)(2,1)S(1)} %get-tuple-element.16), channel_id=1, source_target_pairs={{0,1},{1,2},{2,3},{3,4},{4,5},{5,6},{6,7},{7,8},{8,9},{9,10},{10,1... | collective-permute-start | bytes 76808 | tf_op jit(solution)/shard_map/ppermute | solution.py:21
  39.2 15.2 %collective-permute-start.1 = (bf16[5,16,160]{2,1,0:T(8,128)(2,1)S(1)}, bf16[5,16,160]{2,1,0:T(8,128)(2,1)S(1)}, u32[]{:S(2)}, u32[]{:S(2)}) collective-permute-start(bf16[5,16,160]{2,1,0:T(8,128)(2,1)S(1)} %get-tuple-element.15), channel_id=1, source_target_pairs={{1,0},{2,1},{3,2},{4,3},{5,4},{6,5},{7,6},{8,7},{9,8},{10,9},{11,1... | collective-permute-start | bytes 76808 | tf_op jit(solution)/shard_map/ppermute | solution.py:24
  94.0 3.0 %collective-permute-start.2 = (bf16[2,5,32,16]{3,2,1,0:T(8,128)(2,1)S(1)}, bf16[2,5,32,16]{3,2,1,0:T(8,128)(2,1)S(1)}, u32[]{:S(2)}, u32[]{:S(2)}) collective-permute-start(bf16[2,5,32,16]{3,2,1,0:T(8,128)(2,1)S(1)} %get-tuple-element.13), channel_id=1, source_target_pairs={{0,64},{64,128},{128,192},{1,65},{65,129},{129,193},{2,66},{66,130... | collective-permute-start | bytes 30728 | tf_op jit(solution)/shard_map/ppermute | solution.py:21
  95.6 4.3 %collective-permute-start.3 = (bf16[2,5,32,16]{3,2,1,0:T(8,128)(2,1)S(1)}, bf16[2,5,32,16]{3,2,1,0:T(8,128)(2,1)S(1)}, u32[]{:S(2)}, u32[]{:S(2)}) collective-permute-start(bf16[2,5,32,16]{3,2,1,0:T(8,128)(2,1)S(1)} %get-tuple-element.14), channel_id=1, source_target_pairs={{64,0},{128,64},{192,128},{65,1},{129,65},{193,129},{66,2},{130,66... | collective-permute-start | bytes 30728 | tf_op jit(solution)/shard_map/ppermute | solution.py:24
  100.0 12.7 %collective-permute-start.4 = (bf16[2,5,16,160]{3,2,1,0:T(8,128)(2,1)S(1)}, bf16[2,5,16,160]{3,2,1,0:T(8,128)(2,1)S(1)}, u32[]{:S(2)}, u32[]{:S(2)}) collective-permute-start(bf16[2,5,16,160]{3,2,1,0:T(8,128)(2,1)S(1)} %get-tuple-element.12), channel_id=1, source_target_pairs={{0,1},{1,2},{2,3},{3,4},{4,5},{5,6},{6,7},{7,8},{8,9},{9,10},{10,1... | collective-permute-start | bytes 153608 | tf_op jit(solution)/shard_map/ppermute | solution.py:21
  109.6 12.1 %collective-permute-start.5 = (bf16[2,5,16,160]{3,2,1,0:T(8,128)(2,1)S(1)}, bf16[2,5,16,160]{3,2,1,0:T(8,128)(2,1)S(1)}, u32[]{:S(2)}, u32[]{:S(2)}) collective-permute-start(bf16[2,5,16,160]{3,2,1,0:T(8,128)(2,1)S(1)} %get-tuple-element.11), channel_id=1, source_target_pairs={{1,0},{2,1},{3,2},{4,3},{5,4},{6,5},{7,6},{8,7},{9,8},{10,9},{11,1... | collective-permute-start | bytes 153608 | tf_op jit(solution)/shard_map/ppermute | solution.py:24
  123.5 9.7 %copy-start.1 = (f32[16,32,512]{2,1,0:T(8,128)S(1)}, f32[16,32,512]{2,1,0:T(8,128)}, u32[]{:S(2)}) copy-start(f32[16,32,512]{2,1,0:T(8,128)} %param.10) | copy-start | bytes 3145732
  123.6 9.7 %copy-start.9 = (f32[16]{0:T(128)S(1)}, f32[16]{0:T(128)}, u32[]{:S(2)}) copy-start(f32[16]{0:T(128)} %param.11) | copy-start | bytes 196

commit v4 on v3

--- a/solution.py
+++ b/solution.py
@@ -10,7 +10,7 @@
 NBIN = 5
 KER = 33
 HALF = 16
-CHUNK = 1024
+CHUNK = 8192
 
 
 def extended(block, sides, width):
@@ -60,18 +60,16 @@
         row_hot = (lax.broadcasted_iota(jnp.int32, (rows, CHUNK), 0) == row_of).astype(
             jnp.bfloat16
         )
-        col_hot = lax.broadcasted_iota(jnp.int32, (columns, CHUNK), 0) == col_of
-        zero = jnp.zeros((columns, CHUNK), jnp.bfloat16)
+        col_hot = (lax.broadcasted_iota(jnp.int32, (columns, CHUNK), 0) == col_of).astype(
+            jnp.bfloat16
+        )
         pieces = [split_bf16(block[field : field + 1]) for field in (1, 2, 3)]
-        parts = [
-            jnp.where(col_hot, jnp.broadcast_to(piece[half], (columns, CHUNK)), zero)
-            for half in (0, 1)
-            for piece in pieces
-        ]
-        spread = jnp.concatenate(parts, axis=0)
+        spread = jnp.concatenate(
+            [col_hot * piece[half] for half in (0, 1) for piece in pieces], axis=0
+        )
         acc_ref[...] += lax.dot_general(
+            spread,
             row_hot,
-            spread,
             (((1,), (1,)), ((), ())),
             preferred_element_type=jnp.float32,
         )
@@ -80,9 +78,9 @@
     lax.fori_loop(0, steps, body, 0)
     for field in range(3):
         out_ref[field] = (
-            acc_ref[:, field * columns : (field + 1) * columns]
-            + acc_ref[:, (field + 3) * columns : (field + 4) * columns]
-        )
+            acc_ref[field * columns : (field + 1) * columns, :]
+            + acc_ref[(field + 3) * columns : (field + 4) * columns, :]
+        ).T
 
 
 def deposit_sums(packet, rows, columns):
@@ -93,7 +91,7 @@
         out_shape=jax.ShapeDtypeStruct((3, rows, columns), jnp.float32),
         in_specs=[pl.BlockSpec(memory_space=pltpu.VMEM)],
         out_specs=pl.BlockSpec(memory_space=pltpu.VMEM),
-        scratch_shapes=[pltpu.VMEM((rows, 6 * columns), jnp.float32)],
+        scratch_shapes=[pltpu.VMEM((6 * columns, rows), jnp.float32)],
         cost_estimate=pl.CostEstimate(
             flops=flops, bytes_accessed=packet.size * 4 + rows * 3 * columns * 4, transcendentals=0
         ),

time: 138 us -> 130 us (0.942)
  Pallas kernels: 23.9 us -> 15.6 us
    pallas_call x1, Pallas kernels: 23.9 us -> 15.6 us  [deposit_sums(): pl.pallas_call(functools.partial(scatter_kernel, rows, columns), out_shap...]
  transfers between devices with their start and end apart: 8 -> 8, of which waited for: 4 -> 4; matrix products, arithmetic and copies ran while one was open for 19% -> 20% of each run, Pallas kernels for 0% -> 0%
where the time goes in v4:
time: 130 us; the launch traced here: 128 us
  starting transfers between devices  39.5 us (30%)
  other arithmetic  24 us (18%)
  waiting for transfers between devices  22.3 us (17%)
  Pallas kernels  15.6 us (12%)
  matrix products  10.9 us (8%)
  blocking collectives  8.13 us (6%)
  local copies, waits for them, and re-layouts  7.25 us (6%)
    unnamed x32, other arithmetic  20.8 us
    ppermute x3, starting transfers between devices, extended(): lax.ppermute(lax.slice_in_dim(block, block.shape[dim] - width, None, axis...  15.7 us
    pallas_call x1, Pallas kernels, deposit_sums(): pl.pallas_call(functools.partial(scatter_kernel, rows, columns), out_shap...  15.6 us
    all_to_all x1, starting transfers between devices, per_device(): lax.all_to_all(packet.reshape(4, devices, -1), ('shell', 'tile'), split_a...  14.8 us
    ppermute x3, waiting for transfers between devices, extended(): lax.ppermute(lax.slice_in_dim(block, 0, width, axis=dim), axis, backward)  11.8 us
    all_to_all x1, waiting for transfers between devices, per_device(): lax.all_to_all(windows, 'shell', split_axis=0, concat_axis=0, tiled=True)  8.51 us
    all_gather x1, blocking collectives, per_device(): full_grad = lax.all_gather(bin_grad, 'shell', axis=2, tiled=True)  8.13 us
    ppermute x3, starting transfers between devices, extended(): lax.ppermute(lax.slice_in_dim(block, 0, width, axis=dim), axis, backward)  5.31 us
  transfers between devices with their start and end apart: 8, of which 4 were waited for; matrix products, arithmetic and copies ran while one was open for 20% of the time, Pallas kernels for 0%

profile of v4, /device:TPU:124, one launch (start us, length us, event | category | flops | bytes accessed | tf_op | source)
XLA Modules:
  0.0 128.3 jit_solution(5507468730616745635)
XLA Ops:
  0.7 2.6 %convolution_bitcast_fusion.1 = f32[5,32,512]{2,0,1:T(8,128)S(1)} fusion(f32[16,32,512]{2,1,0:T(8,128)} %param.10, f32[16]{0:T(128)S(1)} %multiply_multiply_fusion, f32[16]{0:T(128)} %param.11, f32[5,16]{1,0:T(8,128)S(1)} %copy-done), kind=kOutput, calls=%fused_computation.13 | convolution fusion | flops 16515072 | bytes 1376704 | tf_op jit(solution)/shard_map/bs,srw->brw/dot_general | solution.py:137
  3.8 1.0 copy.85
  4.8 3.6 %all-to-all-start = ((f32[4,5,32,160]{3,2,1,0:T(8,128)}), f32[4,5,32,160]{3,2,1,0:T(8,128)S(1)}, u32[]{:S(2)}, u32[]{:S(2)}) async-start(f32[4,5,32,160]{3,2,1,0:T(8,128)} %copy.85), calls=%async_computation | async-start | bytes 1310720 | tf_op jit(solution)/shard_map/all_to_all | solution.py:148
  9.0 1.1 pad_maximum_fusion.1
  10.1 8.5 %all-to-all-done = f32[4,5,32,160]{3,2,1,0:T(8,128)S(1)} async-done(((f32[4,5,32,160]{3,2,1,0:T(8,128)}), f32[4,5,32,160]{3,2,1,0:T(8,128)S(1)}, u32[]{:S(2)}, u32[]{:S(2)}) %all-to-all-start) | async-done | bytes 409632 | tf_op jit(solution)/shard_map/all_to_all | solution.py:148
  18.6 14.8 %all-to-all-start.1 = ((f32[4,256,128]{2,0,1:T(4,128)}), f32[4,256,128]{2,0,1:T(4,128)}, u32[]{:S(2)}, u32[]{:S(2)}) async-start(f32[4,256,128]{2,0,1:T(4,128)} %pad_maximum_fusion.1), calls=%async_computation.1 | async-start | bytes 1048576 | tf_op jit(solution)/shard_map/all_to_all | solution.py:127
  33.6 4.6 %collective-permute-start = (bf16[5,16,160]{2,1,0:T(8,128)(2,1)S(1)}, bf16[5,16,160]{2,1,0:T(8,128)(2,1)S(1)}, u32[]{:S(2)}, u32[]{:S(2)}) collective-permute-start(bf16[5,16,160]{2,1,0:T(8,128)(2,1)S(1)} %get-tuple-element.16), channel_id=1, source_target_pairs={{0,1},{1,2},{2,3},{3,4},{4,5},{5,6},{6,7},{7,8},{8,9},{9,10},{10,1... | collective-permute-start | bytes 76808 | tf_op jit(solution)/shard_map/ppermute | solution.py:21
  38.2 1.0 convert_bitcast_fusion.1
  39.2 1.9 %collective-permute-start.1 = (bf16[5,16,160]{2,1,0:T(8,128)(2,1)S(1)}, bf16[5,16,160]{2,1,0:T(8,128)(2,1)S(1)}, u32[]{:S(2)}, u32[]{:S(2)}) collective-permute-start(bf16[5,16,160]{2,1,0:T(8,128)(2,1)S(1)} %get-tuple-element.15), channel_id=1, source_target_pairs={{1,0},{2,1},{3,2},{4,3},{5,4},{6,5},{7,6},{8,7},{9,8},{10,9},{11,1... | collective-permute-start | bytes 76808 | tf_op jit(solution)/shard_map/ppermute | solution.py:24
  41.2 2.0 %collective-permute-done = bf16[5,16,160]{2,1,0:T(8,128)(2,1)S(1)} collective-permute-done((bf16[5,16,160]{2,1,0:T(8,128)(2,1)S(1)}, bf16[5,16,160]{2,1,0:T(8,128)(2,1)S(1)}, u32[]{:S(2)}, u32[]{:S(2)}) %collective-permute-start) | collective-permute-done | bytes 25632 | tf_op jit(solution)/shard_map/ppermute | solution.py:21
  65.1 15.6 %shard_map.100 = f32[3,160,128]{2,1,0:T(8,128)} custom-call(f32[4,32768]{1,0:T(4,128)} %bitcast.83.packet_ref), custom_call_target="tpu_custom_call" | custom-call | flops 8053063680 | bytes 770048 | tf_op jit(solution)/shard_map/pallas_call | solution.py:89
  80.7 0.9 slice.440
  82.6 3.0 %fusion.35 = bf16[2,5,32,128]{3,2,1,0:T(8,128)(2,1)S(1)} fusion(f32[2,5,32,128]{3,2,1,0:T(8,128)S(1)} %bitcast.407, bf16[5,33,32,160]{3,2,1,0:T(8,128)(2,1)} %constant_dynamic-update-slice_fusion, bf16[2,33,160,128,1]{3,1,0,2,4:T(8,128)(2,1)S(1)} %convert_bitcast_fusion.1, f32[32,128]{1,0:T(8,128)S(1)} %convert_element_type.43, f32[5,32,128]{2,1,0:T(8,128)S(1)} %bitcast.408), kind=kOutput, calls=%fused_computation.18 | convolution fusion | flops 432701440 | bytes 4737024 | tf_op jit(solution)/shard_map/bdrj,kdjc->kbrc/dot_general | solution.py:152
  85.7 1.6 %collective-permute-start.2 = (bf16[2,5,32,16]{3,2,1,0:T(8,128)(2,1)S(1)}, bf16[2,5,32,16]{3,2,1,0:T(8,128)(2,1)S(1)}, u32[]{:S(2)}, u32[]{:S(2)}) collective-permute-start(bf16[2,5,32,16]{3,2,1,0:T(8,128)(2,1)S(1)} %get-tuple-element.13), channel_id=1, source_target_pairs={{0,64},{64,128},{128,192},{1,65},{65,129},{129,193},{2,66},{66,130... | collective-permute-start | bytes 30728 | tf_op jit(solution)/shard_map/ppermute | solution.py:21
  87.3 1.3 %collective-permute-start.3 = (bf16[2,5,32,16]{3,2,1,0:T(8,128)(2,1)S(1)}, bf16[2,5,32,16]{3,2,1,0:T(8,128)(2,1)S(1)}, u32[]{:S(2)}, u32[]{:S(2)}) collective-permute-start(bf16[2,5,32,16]{3,2,1,0:T(8,128)(2,1)S(1)} %get-tuple-element.14), channel_id=1, source_target_pairs={{64,0},{128,64},{192,128},{65,1},{129,65},{193,129},{66,2},{130,66... | collective-permute-start | bytes 30728 | tf_op jit(solution)/shard_map/ppermute | solution.py:24
  88.7 2.9 %collective-permute-done.3 = bf16[2,5,32,16]{3,2,1,0:T(8,128)(2,1)S(1)} collective-permute-done((bf16[2,5,32,16]{3,2,1,0:T(8,128)(2,1)S(1)}, bf16[2,5,32,16]{3,2,1,0:T(8,128)(2,1)S(1)}, u32[]{:S(2)}, u32[]{:S(2)}) %collective-permute-start.3) | collective-permute-done | bytes 10272 | tf_op jit(solution)/shard_map/ppermute | solution.py:24
  91.8 9.5 %collective-permute-start.4 = (bf16[2,5,16,160]{3,2,1,0:T(8,128)(2,1)S(1)}, bf16[2,5,16,160]{3,2,1,0:T(8,128)(2,1)S(1)}, u32[]{:S(2)}, u32[]{:S(2)}) collective-permute-start(bf16[2,5,16,160]{3,2,1,0:T(8,128)(2,1)S(1)} %get-tuple-element.12), channel_id=1, source_target_pairs={{0,1},{1,2},{2,3},{3,4},{4,5},{5,6},{6,7},{7,8},{8,9},{9,10},{10,1... | collective-permute-start | bytes 153608 | tf_op jit(solution)/shard_map/ppermute | solution.py:21
  101.3 2.1 %collective-permute-start.5 = (bf16[2,5,16,160]{3,2,1,0:T(8,128)(2,1)S(1)}, bf16[2,5,16,160]{3,2,1,0:T(8,128)(2,1)S(1)}, u32[]{:S(2)}, u32[]{:S(2)}) collective-permute-start(bf16[2,5,16,160]{3,2,1,0:T(8,128)(2,1)S(1)} %get-tuple-element.11), channel_id=1, source_target_pairs={{1,0},{2,1},{3,2},{4,3},{5,4},{6,5},{7,6},{8,7},{9,8},{10,9},{11,1... | collective-permute-start | bytes 153608 | tf_op jit(solution)/shard_map/ppermute | solution.py:24
  103.4 1.0 convert_bitcast_fusion
  104.5 8.9 %collective-permute-done.5 = bf16[2,5,16,160]{3,2,1,0:T(8,128)(2,1)S(1)} collective-permute-done((bf16[2,5,16,160]{3,2,1,0:T(8,128)(2,1)S(1)}, bf16[2,5,16,160]{3,2,1,0:T(8,128)(2,1)S(1)}, u32[]{:S(2)}, u32[]{:S(2)}) %collective-permute-start.5) | collective-permute-done | bytes 51232 | tf_op jit(solution)/shard_map/ppermute | solution.py:24
  115.3 1.6 %fusion.40 = f32[5,32,128]{2,1,0:T(8,128)S(1)} fusion(bf16[2,5,33,32,160]{4,3,1,0,2:T(8,128)(2,1)S(1)} %fusion.53, bf16[2,33,160,128,1]{3,1,0,2,4:T(8,128)(2,1)S(1)} %convert_bitcast_fusion), kind=kOutput, calls=%fused_computation.19 | convolution fusion | flops 432537600 | bytes 6164480 | tf_op jit(solution)/shard_map/kbdrj,kdjc->brc/dot_general | solution.py:162
  116.9 8.1 %all_gather.3 = f32[5,32,512]{2,1,0:T(8,128)S(1)} all-gather(f32[5,32,128]{2,1,0:T(8,128)S(1)} %fusion.40), channel_id=1, replica_groups=mesh['shell'=4,'tile'=64] {'shell'}, dimensions={2}, use_global_device_ids=true | all-gather | bytes 409600 | tf_op jit(solution)/shard_map/all_gather | solution.py:168
  125.0 1.7 %fusion.14 = f32[16,32,512]{2,0,1:T(8,128)S(1)} fusion(f32[16,32,512]{2,1,0:T(8,128)S(1)} %copy-done.1, f32[5,32,512]{2,1,0:T(8,128)S(1)} %all_gather.3, f32[16]{0:T(128)S(1)} %multiply_multiply_fusion, f32[16]{0:T(128)S(1)} %copy-done.9, f32[5,16]{1,0:T(8,128)S(1)} %copy-done), kind=kOutput, calls=%fused_computation.12 | convolution fusion | flops 16777216 | bytes 2425280 | tf_op jit(solution)/shard_map/bs,brw->srw/dot_general | solution.py:169
  126.7 1.6 %copy.125 = f32[16,32,512]{2,1,0:T(8,128)} copy(f32[16,32,512]{2,0,1:T(8,128)S(1)} %fusion.14) | data formatting | bytes 2097152 | tf_op jit(solution)/shard_map/mul | solution.py:176
  (106 shorter events, 26.6 us)
Async XLA Ops:
  0.0 0.7 copy-start
  3.3 5.2 %copy-start.5 = (f32[4,64,128]{2,1,0:T(8,128)S(1)}, f32[4,64,128]{2,1,0:T(8,128)}, u32[]{:S(2)}) copy-start(f32[4,64,128]{2,1,0:T(8,128)} %param.18) | copy-start | bytes 393220
  3.3 5.2 %copy-start.8 = (s32[4,64]{1,0:T(4,128)S(1)}, s32[4,64]{1,0:T(4,128)}, u32[]{:S(2)}) copy-start(s32[4,64]{1,0:T(4,128)} %param.19) | copy-start | bytes 3076
  3.3 5.3 %copy-start.2 = (f32[2,4,64,128]{3,2,1,0:T(8,128)S(1)}, f32[2,4,64,128]{3,2,1,0:T(8,128)}, u32[]{:S(2)}) copy-start(f32[2,4,64,128]{3,2,1,0:T(8,128)} %param.17) | copy-start | bytes 786436
  3.6 5.2 %copy-start.3 = (s32[4,64,128]{2,1,0:T(8,128)S(1)}, s32[4,64,128]{2,1,0:T(8,128)}, u32[]{:S(2)}) copy-start(s32[4,64,128]{2,1,0:T(8,128)} %param.15) | copy-start | bytes 393220
  3.6 5.2 %copy-start.4 = (s32[4,64,128]{2,1,0:T(8,128)S(1)}, s32[4,64,128]{2,1,0:T(8,128)}, u32[]{:S(2)}) copy-start(s32[4,64,128]{2,1,0:T(8,128)} %param.16) | copy-start | bytes 393220
  4.8 33.4 %copy-start.6 = (bf16[2,33,33]{2,0,1:T(2,128)(2,1)S(1)}, bf16[2,33,33]{2,0,1:T(2,128)(2,1)}, u32[]{:S(2)}) copy-start(bf16[2,33,33]{2,0,1:T(2,128)(2,1)} %param.13) | copy-start | bytes 13072
  4.8 13.8 %all-to-all-start = ((f32[4,5,32,160]{3,2,1,0:T(8,128)}), f32[4,5,32,160]{3,2,1,0:T(8,128)S(1)}, u32[]{:S(2)}, u32[]{:S(2)}) async-start(f32[4,5,32,160]{3,2,1,0:T(8,128)} %copy.85), calls=%async_computation | async-start | bytes 1310720 | tf_op jit(solution)/shard_map/all_to_all | solution.py:148
  8.8 30.4 %copy-start.7 = (s32[32,128]{1,0:T(8,128)S(1)}, s32[32,128]{1,0:T(8,128)}, u32[]{:S(2)}) copy-start(s32[32,128]{1,0:T(8,128)} %param.14) | copy-start | bytes 49156
  18.6 46.5 %all-to-all-start.1 = ((f32[4,256,128]{2,0,1:T(4,128)}), f32[4,256,128]{2,0,1:T(4,128)}, u32[]{:S(2)}, u32[]{:S(2)}) async-start(f32[4,256,128]{2,0,1:T(4,128)} %pad_maximum_fusion.1), calls=%async_computation.1 | async-start | bytes 1048576 | tf_op jit(solution)/shard_map/all_to_all | solution.py:127
  33.6 9.6 %collective-permute-start = (bf16[5,16,160]{2,1,0:T(8,128)(2,1)S(1)}, bf16[5,16,160]{2,1,0:T(8,128)(2,1)S(1)}, u32[]{:S(2)}, u32[]{:S(2)}) collective-permute-start(bf16[5,16,160]{2,1,0:T(8,128)(2,1)S(1)} %get-tuple-element.16), channel_id=1, source_target_pairs={{0,1},{1,2},{2,3},{3,4},{4,5},{5,6},{6,7},{7,8},{8,9},{9,10},{10,1... | collective-permute-start | bytes 76808 | tf_op jit(solution)/shard_map/ppermute | solution.py:21
  39.2 15.2 %collective-permute-start.1 = (bf16[5,16,160]{2,1,0:T(8,128)(2,1)S(1)}, bf16[5,16,160]{2,1,0:T(8,128)(2,1)S(1)}, u32[]{:S(2)}, u32[]{:S(2)}) collective-permute-start(bf16[5,16,160]{2,1,0:T(8,128)(2,1)S(1)} %get-tuple-element.15), channel_id=1, source_target_pairs={{1,0},{2,1},{3,2},{4,3},{5,4},{6,5},{7,6},{8,7},{9,8},{10,9},{11,1... | collective-permute-start | bytes 76808 | tf_op jit(solution)/shard_map/ppermute | solution.py:24
  85.7 3.0 %collective-permute-start.2 = (bf16[2,5,32,16]{3,2,1,0:T(8,128)(2,1)S(1)}, bf16[2,5,32,16]{3,2,1,0:T(8,128)(2,1)S(1)}, u32[]{:S(2)}, u32[]{:S(2)}) collective-permute-start(bf16[2,5,32,16]{3,2,1,0:T(8,128)(2,1)S(1)} %get-tuple-element.13), channel_id=1, source_target_pairs={{0,64},{64,128},{128,192},{1,65},{65,129},{129,193},{2,66},{66,130... | collective-permute-start | bytes 30728 | tf_op jit(solution)/shard_map/ppermute | solution.py:21
  87.3 4.3 %collective-permute-start.3 = (bf16[2,5,32,16]{3,2,1,0:T(8,128)(2,1)S(1)}, bf16[2,5,32,16]{3,2,1,0:T(8,128)(2,1)S(1)}, u32[]{:S(2)}, u32[]{:S(2)}) collective-permute-start(bf16[2,5,32,16]{3,2,1,0:T(8,128)(2,1)S(1)} %get-tuple-element.14), channel_id=1, source_target_pairs={{64,0},{128,64},{192,128},{65,1},{129,65},{193,129},{66,2},{130,66... | collective-permute-start | bytes 30728 | tf_op jit(solution)/shard_map/ppermute | solution.py:24
  91.8 12.7 %collective-permute-start.4 = (bf16[2,5,16,160]{3,2,1,0:T(8,128)(2,1)S(1)}, bf16[2,5,16,160]{3,2,1,0:T(8,128)(2,1)S(1)}, u32[]{:S(2)}, u32[]{:S(2)}) collective-permute-start(bf16[2,5,16,160]{3,2,1,0:T(8,128)(2,1)S(1)} %get-tuple-element.12), channel_id=1, source_target_pairs={{0,1},{1,2},{2,3},{3,4},{4,5},{5,6},{6,7},{7,8},{8,9},{9,10},{10,1... | collective-permute-start | bytes 153608 | tf_op jit(solution)/shard_map/ppermute | solution.py:21
  101.3 12.1 %collective-permute-start.5 = (bf16[2,5,16,160]{3,2,1,0:T(8,128)(2,1)S(1)}, bf16[2,5,16,160]{3,2,1,0:T(8,128)(2,1)S(1)}, u32[]{:S(2)}, u32[]{:S(2)}) collective-permute-start(bf16[2,5,16,160]{3,2,1,0:T(8,128)(2,1)S(1)} %get-tuple-element.11), channel_id=1, source_target_pairs={{1,0},{2,1},{3,2},{4,3},{5,4},{6,5},{7,6},{8,7},{9,8},{10,9},{11,1... | collective-permute-start | bytes 153608 | tf_op jit(solution)/shard_map/ppermute | solution.py:24
  115.3 9.7 %copy-start.1 = (f32[16,32,512]{2,1,0:T(8,128)S(1)}, f32[16,32,512]{2,1,0:T(8,128)}, u32[]{:S(2)}) copy-start(f32[16,32,512]{2,1,0:T(8,128)} %param.10) | copy-start | bytes 3145732
  115.3 9.7 %copy-start.9 = (f32[16]{0:T(128)S(1)}, f32[16]{0:T(128)}, u32[]{:S(2)}) copy-start(f32[16]{0:T(128)} %param.11) | copy-start | bytes 196

commit v5 on v4

--- a/solution.py
+++ b/solution.py
@@ -6,6 +6,7 @@
 from jax.experimental import pallas as pl
 from jax.experimental.pallas import tpu as pltpu
 from jax.sharding import PartitionSpec as P
+
 
 NBIN = 5
 KER = 33
@@ -96,6 +97,37 @@
             flops=flops, bytes_accessed=packet.size * 4 + rows * 3 * columns * 4, transcendentals=0
         ),
     )(packet)
+
+
+def correlate_kernel(x_ref, band_ref, out_ref, z_ref):
+    bins, span, width = x_ref.shape
+    height = out_ref.shape[2]
+    x = x_ref[...].reshape(bins * span, width)
+    for k in range(band_ref.shape[0]):
+        total = jnp.zeros(out_ref.shape[1:], jnp.float32)
+        for offset in range(band_ref.shape[1]):
+            z_ref[...] = jnp.dot(
+                x, band_ref[k, offset], preferred_element_type=jnp.float32
+            ).reshape(z_ref.shape)
+            total = total + z_ref[:, offset : offset + height, :]
+        out_ref[k] = total
+
+
+def correlate_forward(padded, bands, height):
+    bins, span, width = padded.shape
+    kinds, offsets, _, columns = bands.shape
+    return pl.pallas_call(
+        correlate_kernel,
+        out_shape=jax.ShapeDtypeStruct((kinds, bins, height, columns), jnp.float32),
+        in_specs=[pl.BlockSpec(memory_space=pltpu.VMEM)] * 2,
+        out_specs=pl.BlockSpec(memory_space=pltpu.VMEM),
+        scratch_shapes=[pltpu.VMEM((bins, span, columns), jnp.float32)],
+        cost_estimate=pl.CostEstimate(
+            flops=2 * kinds * offsets * bins * span * width * columns,
+            bytes_accessed=padded.size * 2 + bands.size * 2 + kinds * bins * height * columns * 4,
+            transcendentals=0,
+        ),
+    )(padded, bands)
 
 
 def per_device(
@@ -149,12 +181,7 @@
     bin_map = jnp.sum(gathered, axis=0).astype(jnp.bfloat16)
     padded = extended(bin_map, (("tile", 1),), HALF)
     forward_bands = build_bands(shear_kernel, columns)
-    shear = jnp.einsum(
-        "bdrj,kdjc->kbrc",
-        stacked_rows(padded, height),
-        forward_bands,
-        preferred_element_type=jnp.float32,
-    )
+    shear = correlate_forward(padded, forward_bands, height)
     shear_grad = shear * weight_sum[None] - shape_sum
     masked = (shear_grad * star_mask.astype(jnp.float32)).astype(jnp.bfloat16)
     rims = extended(masked, (("shell", 3), ("tile", 2)), HALF)

time: 130 us -> 112 us (0.86)
  other arithmetic: 24 us -> 3.49 us
  starting transfers between devices: 39.5 us -> 32.7 us
  Pallas kernels: 15.6 us -> 21.5 us
  waiting for transfers between devices: 22.3 us -> 26.7 us
  matrix products: 10.9 us -> 7.83 us
  local copies, waits for them, and re-layouts: 7.25 us -> 9.63 us
    unnamed x32 -> x1, other arithmetic: 20.8 us -> 0.14 us
    ppermute x3, starting transfers between devices: 15.7 us -> 8.9 us  [extended(): lax.ppermute(lax.slice_in_dim(block, block.shape[dim] - width, None, axis...]
    ppermute x3, waiting for transfers between devices: 11.8 us -> 17.6 us  [extended(): lax.ppermute(lax.slice_in_dim(block, 0, width, axis=dim), axis, backward)]
    pallas_call x0 -> x1, Pallas kernels: none -> 5.85 us  [correlate_forward(): pl.pallas_call(correlate_kernel, out_shape=jax.ShapeDtypeStruct((kinds, b...]
    dot_general x1 -> x0, matrix products: 3.05 us -> none  [per_device(): jnp.einsum('bdrj,kdjc->kbrc', stacked_rows(padded, height), forward_bands...]
    dot_general x0 -> x1, local copies, waits for them, and re-layouts: none -> 2.25 us  [build_bands(): jnp.einsum('kdv,vjc->kdjc', kernel, onehot, preferred_element_type=jnp.fl...]
    ppermute x3, waiting for transfers between devices: 1.99 us -> 0.57 us  [extended(): lax.ppermute(lax.slice_in_dim(block, block.shape[dim] - width, None, axis...]
  transfers between devices with their start and end apart: 8 -> 8, of which waited for: 4 -> 5; matrix products, arithmetic and copies ran while one was open for 20% -> 6% of each run, Pallas kernels for 0% -> 5%
where the time goes in v5:
time: 112 us; the launch traced here: 111 us
  starting transfers between devices  32.7 us (29%)
  waiting for transfers between devices  26.7 us (24%)
  Pallas kernels  21.5 us (19%)
  local copies, waits for them, and re-layouts  9.63 us (9%)
  blocking collectives  8.12 us (7%)
  matrix products  7.83 us (7%)
  other arithmetic  3.49 us (3%)
    ppermute x3, waiting for transfers between devices, extended(): lax.ppermute(lax.slice_in_dim(block, 0, width, axis=dim), axis, backward)  17.6 us
    pallas_call x1, Pallas kernels, deposit_sums(): pl.pallas_call(functools.partial(scatter_kernel, rows, columns), out_shap...  15.7 us
    all_to_all x1, starting transfers between devices, per_device(): lax.all_to_all(packet.reshape(4, devices, -1), ('shell', 'tile'), split_a...  13.9 us
    ppermute x3, starting transfers between devices, extended(): lax.ppermute(lax.slice_in_dim(block, block.shape[dim] - width, None, axis...  8.9 us
    all_to_all x1, waiting for transfers between devices, per_device(): lax.all_to_all(windows, 'shell', split_axis=0, concat_axis=0, tiled=True)  8.52 us
    all_gather x1, blocking collectives, per_device(): full_grad = lax.all_gather(bin_grad, 'shell', axis=2, tiled=True)  8.12 us
    ppermute x3, starting transfers between devices, extended(): lax.ppermute(lax.slice_in_dim(block, 0, width, axis=dim), axis, backward)  6.47 us
    pallas_call x1, Pallas kernels, correlate_forward(): pl.pallas_call(correlate_kernel, out_shape=jax.ShapeDtypeStruct((kinds, b...  5.85 us
  transfers between devices with their start and end apart: 8, of which 5 were waited for; matrix products, arithmetic and copies ran while one was open for 6% of the time, Pallas kernels for 5%

profile of v5, /device:TPU:124, one launch (start us, length us, event | category | flops | bytes accessed | tf_op | source)
XLA Modules:
  0.0 110.6 jit_solution(4338016689841178575)
XLA Ops:
  0.8 2.6 %convolution_bitcast_fusion.1 = f32[5,32,512]{2,0,1:T(8,128)S(1)} fusion(f32[16,32,512]{2,1,0:T(8,128)} %param.10, f32[16]{0:T(128)S(1)} %multiply_multiply_fusion, f32[16]{0:T(128)} %param.11, f32[5,16]{1,0:T(8,128)S(1)} %copy-done), kind=kOutput, calls=%fused_computation.11 | convolution fusion | flops 16515072 | bytes 1376704 | tf_op jit(solution)/shard_map/bs,srw->brw/dot_general | solution.py:169
  3.8 1.0 copy.24
  4.9 3.5 %all-to-all-start = ((f32[4,5,32,160]{3,2,1,0:T(8,128)}), f32[4,5,32,160]{3,2,1,0:T(8,128)S(1)}, u32[]{:S(2)}, u32[]{:S(2)}) async-start(f32[4,5,32,160]{3,2,1,0:T(8,128)} %copy.24), calls=%async_computation | async-start | bytes 1310720 | tf_op jit(solution)/shard_map/all_to_all | solution.py:180
  8.9 1.2 %pad_maximum_fusion.1 = f32[4,256,128]{2,0,1:T(4,128)} fusion(f32[2,256,128]{2,0,1:T(2,128)S(1)} %bitcast.183, f32[1,256,128]{2,0,1:T(1,128)S(1)} %bitcast.182, f32[1,256,128]{2,0,1:T(1,128)S(1)} %bitcast.186), kind=kLoop, calls=%fused_computation.20 | loop fusion | flops 262144 | bytes 1048576 | tf_op jit(solution)/shard_map/concatenate | solution.py:155
  10.0 8.5 %all-to-all-done = f32[4,5,32,160]{3,2,1,0:T(8,128)S(1)} async-done(((f32[4,5,32,160]{3,2,1,0:T(8,128)}), f32[4,5,32,160]{3,2,1,0:T(8,128)S(1)}, u32[]{:S(2)}, u32[]{:S(2)}) %all-to-all-start) | async-done | bytes 409632 | tf_op jit(solution)/shard_map/all_to_all | solution.py:180
  18.5 13.9 %all-to-all-start.1 = ((f32[4,256,128]{2,0,1:T(4,128)}), f32[4,256,128]{2,0,1:T(4,128)S(1)}, u32[]{:S(2)}, u32[]{:S(2)}) async-start(f32[4,256,128]{2,0,1:T(4,128)} %pad_maximum_fusion.1), calls=%async_computation.1 | async-start | bytes 1048576 | tf_op jit(solution)/shard_map/all_to_all | solution.py:159
  32.5 4.6 %collective-permute-start = (bf16[5,16,160]{2,1,0:T(8,128)(2,1)S(1)}, bf16[5,16,160]{2,1,0:T(8,128)(2,1)S(1)}, u32[]{:S(2)}, u32[]{:S(2)}) collective-permute-start(bf16[5,16,160]{2,1,0:T(8,128)(2,1)S(1)} %get-tuple-element.15), channel_id=1, source_target_pairs={{0,1},{1,2},{2,3},{3,4},{4,5},{5,6},{6,7},{7,8},{8,9},{9,10},{10,1... | collective-permute-start | bytes 76808 | tf_op jit(solution)/shard_map/ppermute | solution.py:22
  37.1 2.1 %collective-permute-start.1 = (bf16[5,16,160]{2,1,0:T(8,128)(2,1)S(1)}, bf16[5,16,160]{2,1,0:T(8,128)(2,1)S(1)}, u32[]{:S(2)}, u32[]{:S(2)}) collective-permute-start(bf16[5,16,160]{2,1,0:T(8,128)(2,1)S(1)} %get-tuple-element.16), channel_id=1, source_target_pairs={{1,0},{2,1},{3,2},{4,3},{5,4},{6,5},{7,6},{8,7},{9,8},{10,9},{11,1... | collective-permute-start | bytes 76808 | tf_op jit(solution)/shard_map/ppermute | solution.py:25
  39.2 1.0 fusion.3
  40.2 2.2 %copy.67 = bf16[160,128,2,33]{1,0,3,2:T(8,128)(2,1)} copy(bf16[160,128,2,33]{1,3,2,0:T(8,128)(2,1)S(1)} %fusion.3) | data formatting | bytes 5406720 | tf_op jit(solution)/shard_map/kdv,vjc->kdjc/dot_general | solution.py:37
  43.1 5.7 %collective-permute-done.1 = bf16[5,16,160]{2,1,0:T(8,128)(2,1)S(1)} collective-permute-done((bf16[5,16,160]{2,1,0:T(8,128)(2,1)S(1)}, bf16[5,16,160]{2,1,0:T(8,128)(2,1)S(1)}, u32[]{:S(2)}, u32[]{:S(2)}) %collective-permute-start.1) | collective-permute-done | bytes 25632 | tf_op jit(solution)/shard_map/ppermute | solution.py:25
  49.4 5.8 %shard_map.100 = f32[2,5,32,128]{3,2,1,0:T(8,128)} custom-call(bf16[5,64,160]{2,1,0:T(8,128)(2,1)} %pad_maximum_fusion.3.x_ref, bf16[2,33,160,128]{3,2,1,0:T(8,128)(2,1)} %bitcast.181), custom_call_target="tpu_custom_call" | custom-call | flops 865075200 | bytes 2969600 | tf_op jit(solution)/shard_map/pallas_call | solution.py:119
  56.1 15.7 %shard_map.101 = f32[3,160,128]{2,1,0:T(8,128)} custom-call(f32[4,32768]{1,0:T(4,128)} %bitcast.185), custom_call_target="tpu_custom_call" | custom-call | flops 8053063680 | bytes 770048 | tf_op jit(solution)/shard_map/pallas_call | solution.py:90
  73.7 1.3 %collective-permute-start.2 = (bf16[2,5,32,16]{3,2,1,0:T(8,128)(2,1)S(1)}, bf16[2,5,32,16]{3,2,1,0:T(8,128)(2,1)S(1)}, u32[]{:S(2)}, u32[]{:S(2)}) collective-permute-start(bf16[2,5,32,16]{3,2,1,0:T(8,128)(2,1)S(1)} %get-tuple-element.13), channel_id=1, source_target_pairs={{0,64},{64,128},{128,192},{1,65},{65,129},{129,193},{2,66},{66,130... | collective-permute-start | bytes 30728 | tf_op jit(solution)/shard_map/ppermute | solution.py:22
  75.0 1.3 %collective-permute-start.3 = (bf16[2,5,32,16]{3,2,1,0:T(8,128)(2,1)S(1)}, bf16[2,5,32,16]{3,2,1,0:T(8,128)(2,1)S(1)}, u32[]{:S(2)}, u32[]{:S(2)}) collective-permute-start(bf16[2,5,32,16]{3,2,1,0:T(8,128)(2,1)S(1)} %get-tuple-element.14), channel_id=1, source_target_pairs={{64,0},{128,64},{192,128},{65,1},{129,65},{193,129},{66,2},{130,66... | collective-permute-start | bytes 30728 | tf_op jit(solution)/shard_map/ppermute | solution.py:25
  76.4 4.0 %collective-permute-done.3 = bf16[2,5,32,16]{3,2,1,0:T(8,128)(2,1)S(1)} collective-permute-done((bf16[2,5,32,16]{3,2,1,0:T(8,128)(2,1)S(1)}, bf16[2,5,32,16]{3,2,1,0:T(8,128)(2,1)S(1)}, u32[]{:S(2)}, u32[]{:S(2)}) %collective-permute-start.3) | collective-permute-done | bytes 10272 | tf_op jit(solution)/shard_map/ppermute | solution.py:25
  80.6 3.0 %collective-permute-start.4 = (bf16[2,5,16,160]{3,2,1,0:T(8,128)(2,1)S(1)}, bf16[2,5,16,160]{3,2,1,0:T(8,128)(2,1)S(1)}, u32[]{:S(2)}, u32[]{:S(2)}) collective-permute-start(bf16[2,5,16,160]{3,2,1,0:T(8,128)(2,1)S(1)} %get-tuple-element.12), channel_id=1, source_target_pairs={{0,1},{1,2},{2,3},{3,4},{4,5},{5,6},{6,7},{7,8},{8,9},{9,10},{10,1... | collective-permute-start | bytes 153608 | tf_op jit(solution)/shard_map/ppermute | solution.py:22
  83.6 3.1 %collective-permute-start.5 = (bf16[2,5,16,160]{3,2,1,0:T(8,128)(2,1)S(1)}, bf16[2,5,16,160]{3,2,1,0:T(8,128)(2,1)S(1)}, u32[]{:S(2)}, u32[]{:S(2)}) collective-permute-start(bf16[2,5,16,160]{3,2,1,0:T(8,128)(2,1)S(1)} %get-tuple-element.11), channel_id=1, source_target_pairs={{1,0},{2,1},{3,2},{4,3},{5,4},{6,5},{7,6},{8,7},{9,8},{10,9},{11,1... | collective-permute-start | bytes 153608 | tf_op jit(solution)/shard_map/ppermute | solution.py:25
  86.7 1.0 convert_bitcast_fusion
  87.7 7.9 %collective-permute-done.5 = bf16[2,5,16,160]{3,2,1,0:T(8,128)(2,1)S(1)} collective-permute-done((bf16[2,5,16,160]{3,2,1,0:T(8,128)(2,1)S(1)}, bf16[2,5,16,160]{3,2,1,0:T(8,128)(2,1)S(1)}, u32[]{:S(2)}, u32[]{:S(2)}) %collective-permute-start.5) | collective-permute-done | bytes 51232 | tf_op jit(solution)/shard_map/ppermute | solution.py:25
  97.6 1.6 %fusion.11 = f32[5,32,128]{2,1,0:T(8,128)S(1)} fusion(bf16[2,5,33,32,160]{4,3,1,0,2:T(8,128)(2,1)S(1)} %fusion.24, bf16[2,33,160,128,1]{3,1,0,2,4:T(8,128)(2,1)S(1)} %convert_bitcast_fusion), kind=kOutput, calls=%fused_computation.12 | convolution fusion | flops 432537600 | bytes 6164480 | tf_op jit(solution)/shard_map/kbdrj,kdjc->brc/dot_general | solution.py:189
  99.2 8.1 %all_gather.3 = f32[5,32,512]{2,1,0:T(8,128)S(1)} all-gather(f32[5,32,128]{2,1,0:T(8,128)S(1)} %fusion.11), channel_id=1, replica_groups=mesh['shell'=4,'tile'=64] {'shell'}, dimensions={2}, use_global_device_ids=true | all-gather | bytes 409600 | tf_op jit(solution)/shard_map/all_gather | solution.py:195
  107.3 1.7 %fusion.10 = f32[16,32,512]{2,0,1:T(8,128)S(1)} fusion(f32[16,32,512]{2,1,0:T(8,128)S(1)} %copy-done.1, f32[5,32,512]{2,1,0:T(8,128)S(1)} %all_gather.3, f32[16]{0:T(128)S(1)} %multiply_multiply_fusion, f32[16]{0:T(128)S(1)} %copy-done.11, f32[5,16]{1,0:T(8,128)S(1)} %copy-done), kind=kOutput, calls=%fused_computation.10 | convolution fusion | flops 16777216 | bytes 2425280 | tf_op jit(solution)/shard_map/bs,brw->srw/dot_general | solution.py:196
  109.0 1.6 %copy.33 = f32[16,32,512]{2,1,0:T(8,128)} copy(f32[16,32,512]{2,0,1:T(8,128)S(1)} %fusion.10) | data formatting | bytes 2097152 | tf_op jit(solution)/shard_map/mul | solution.py:203
  (80 shorter events, 7.7 us)
Async XLA Ops:
  0.0 0.8 copy-start
  0.0 8.3 %copy-start.7 = (f32[4,64,128]{2,1,0:T(8,128)S(1)}, f32[4,64,128]{2,1,0:T(8,128)}, u32[]{:S(2)}) copy-start(f32[4,64,128]{2,1,0:T(8,128)} %param.18) | copy-start | bytes 393220
  0.0 8.4 %copy-start.10 = (s32[4,64]{1,0:T(4,128)S(1)}, s32[4,64]{1,0:T(4,128)}, u32[]{:S(2)}) copy-start(s32[4,64]{1,0:T(4,128)} %param.19) | copy-start | bytes 3076
  0.0 8.5 %copy-start.3 = (f32[2,4,64,128]{3,2,1,0:T(8,128)S(1)}, f32[2,4,64,128]{3,2,1,0:T(8,128)}, u32[]{:S(2)}) copy-start(f32[2,4,64,128]{3,2,1,0:T(8,128)} %param.17) | copy-start | bytes 786436
  0.0 8.7 %copy-start.5 = (s32[4,64,128]{2,1,0:T(8,128)S(1)}, s32[4,64,128]{2,1,0:T(8,128)}, u32[]{:S(2)}) copy-start(s32[4,64,128]{2,1,0:T(8,128)} %param.15) | copy-start | bytes 393220
  0.0 8.7 %copy-start.6 = (s32[4,64,128]{2,1,0:T(8,128)S(1)}, s32[4,64,128]{2,1,0:T(8,128)}, u32[]{:S(2)}) copy-start(s32[4,64,128]{2,1,0:T(8,128)} %param.16) | copy-start | bytes 393220
  3.7 35.5 %copy-start.8 = (bf16[2,33,33]{2,0,1:T(2,128)(2,1)S(1)}, bf16[2,33,33]{2,0,1:T(2,128)(2,1)}, u32[]{:S(2)}) copy-start(bf16[2,33,33]{2,0,1:T(2,128)(2,1)} %param.13) | copy-start | bytes 13072
  4.9 13.7 %all-to-all-start = ((f32[4,5,32,160]{3,2,1,0:T(8,128)}), f32[4,5,32,160]{3,2,1,0:T(8,128)S(1)}, u32[]{:S(2)}, u32[]{:S(2)}) async-start(f32[4,5,32,160]{3,2,1,0:T(8,128)} %copy.24), calls=%async_computation | async-start | bytes 1310720 | tf_op jit(solution)/shard_map/all_to_all | solution.py:180
  10.0 32.5 %copy-start.9 = (s32[32,128]{1,0:T(8,128)S(1)}, s32[32,128]{1,0:T(8,128)}, u32[]{:S(2)}) copy-start(s32[32,128]{1,0:T(8,128)} %param.14) | copy-start | bytes 49156
  18.5 36.7 %all-to-all-start.1 = ((f32[4,256,128]{2,0,1:T(4,128)}), f32[4,256,128]{2,0,1:T(4,128)S(1)}, u32[]{:S(2)}, u32[]{:S(2)}) async-start(f32[4,256,128]{2,0,1:T(4,128)} %pad_maximum_fusion.1), calls=%async_computation.1 | async-start | bytes 1048576 | tf_op jit(solution)/shard_map/all_to_all | solution.py:159
  32.5 10.6 %collective-permute-start = (bf16[5,16,160]{2,1,0:T(8,128)(2,1)S(1)}, bf16[5,16,160]{2,1,0:T(8,128)(2,1)S(1)}, u32[]{:S(2)}, u32[]{:S(2)}) collective-permute-start(bf16[5,16,160]{2,1,0:T(8,128)(2,1)S(1)} %get-tuple-element.15), channel_id=1, source_target_pairs={{0,1},{1,2},{2,3},{3,4},{4,5},{5,6},{6,7},{7,8},{8,9},{9,10},{10,1... | collective-permute-start | bytes 76808 | tf_op jit(solution)/shard_map/ppermute | solution.py:22
  37.1 11.6 %collective-permute-start.1 = (bf16[5,16,160]{2,1,0:T(8,128)(2,1)S(1)}, bf16[5,16,160]{2,1,0:T(8,128)(2,1)S(1)}, u32[]{:S(2)}, u32[]{:S(2)}) collective-permute-start(bf16[5,16,160]{2,1,0:T(8,128)(2,1)S(1)} %get-tuple-element.16), channel_id=1, source_target_pairs={{1,0},{2,1},{3,2},{4,3},{5,4},{6,5},{7,6},{8,7},{9,8},{10,9},{11,1... | collective-permute-start | bytes 76808 | tf_op jit(solution)/shard_map/ppermute | solution.py:25
  55.3 0.8 copy-start.2
  56.0 17.5 %copy-start.4 = (f32[2,5,32,128]{3,2,1,0:T(8,128)S(1)}, f32[2,5,32,128]{3,2,1,0:T(8,128)}, u32[]{:S(2)}) copy-start(f32[2,5,32,128]{3,2,1,0:T(8,128)} %shard_map.100) | copy-start | bytes 491524
  73.7 2.7 %collective-permute-start.2 = (bf16[2,5,32,16]{3,2,1,0:T(8,128)(2,1)S(1)}, bf16[2,5,32,16]{3,2,1,0:T(8,128)(2,1)S(1)}, u32[]{:S(2)}, u32[]{:S(2)}) collective-permute-start(bf16[2,5,32,16]{3,2,1,0:T(8,128)(2,1)S(1)} %get-tuple-element.13), channel_id=1, source_target_pairs={{0,64},{64,128},{128,192},{1,65},{65,129},{129,193},{2,66},{66,130... | collective-permute-start | bytes 30728 | tf_op jit(solution)/shard_map/ppermute | solution.py:22
  75.0 5.5 %collective-permute-start.3 = (bf16[2,5,32,16]{3,2,1,0:T(8,128)(2,1)S(1)}, bf16[2,5,32,16]{3,2,1,0:T(8,128)(2,1)S(1)}, u32[]{:S(2)}, u32[]{:S(2)}) collective-permute-start(bf16[2,5,32,16]{3,2,1,0:T(8,128)(2,1)S(1)} %get-tuple-element.14), channel_id=1, source_target_pairs={{64,0},{128,64},{192,128},{65,1},{129,65},{193,129},{66,2},{130,66... | collective-permute-start | bytes 30728 | tf_op jit(solution)/shard_map/ppermute | solution.py:25
  80.6 7.1 %collective-permute-start.4 = (bf16[2,5,16,160]{3,2,1,0:T(8,128)(2,1)S(1)}, bf16[2,5,16,160]{3,2,1,0:T(8,128)(2,1)S(1)}, u32[]{:S(2)}, u32[]{:S(2)}) collective-permute-start(bf16[2,5,16,160]{3,2,1,0:T(8,128)(2,1)S(1)} %get-tuple-element.12), channel_id=1, source_target_pairs={{0,1},{1,2},{2,3},{3,4},{4,5},{5,6},{6,7},{7,8},{8,9},{9,10},{10,1... | collective-permute-start | bytes 153608 | tf_op jit(solution)/shard_map/ppermute | solution.py:22
  83.6 12.1 %collective-permute-start.5 = (bf16[2,5,16,160]{3,2,1,0:T(8,128)(2,1)S(1)}, bf16[2,5,16,160]{3,2,1,0:T(8,128)(2,1)S(1)}, u32[]{:S(2)}, u32[]{:S(2)}) collective-permute-start(bf16[2,5,16,160]{3,2,1,0:T(8,128)(2,1)S(1)} %get-tuple-element.11), channel_id=1, source_target_pairs={{1,0},{2,1},{3,2},{4,3},{5,4},{6,5},{7,6},{8,7},{9,8},{10,9},{11,1... | collective-permute-start | bytes 153608 | tf_op jit(solution)/shard_map/ppermute | solution.py:25
  97.4 9.9 %copy-start.1 = (f32[16,32,512]{2,1,0:T(8,128)S(1)}, f32[16,32,512]{2,1,0:T(8,128)}, u32[]{:S(2)}) copy-start(f32[16,32,512]{2,1,0:T(8,128)} %param.10) | copy-start | bytes 3145732
  97.4 9.9 %copy-start.11 = (f32[16]{0:T(128)S(1)}, f32[16]{0:T(128)}, u32[]{:S(2)}) copy-start(f32[16]{0:T(128)} %param.11) | copy-start | bytes 196

commit v6 on v5

--- a/solution.py
+++ b/solution.py
@@ -177,8 +177,14 @@
     windows = jnp.stack(
         [wide[:, :, owner * columns : owner * columns + columns + 2 * HALF] for owner in range(shell_count)]
     )
-    gathered = lax.all_to_all(windows, "shell", split_axis=0, concat_axis=0, tiled=True)
-    bin_map = jnp.sum(gathered, axis=0).astype(jnp.bfloat16)
+    me = lax.axis_index("shell")
+    total = lax.dynamic_index_in_dim(windows, me, 0, keepdims=False)
+    for shift in range(1, shell_count):
+        outgoing = lax.dynamic_index_in_dim(windows, (me + shift) % shell_count, 0, keepdims=False)
+        total = total + lax.ppermute(
+            outgoing, "shell", [(i, (i + shift) % shell_count) for i in range(shell_count)]
+        )
+    bin_map = total.astype(jnp.bfloat16)
     padded = extended(bin_map, (("tile", 1),), HALF)
     forward_bands = build_bands(shear_kernel, columns)
     shear = correlate_forward(padded, forward_bands, height)

time: 112 us -> 102 us (0.911)
  waiting for transfers between devices: 26.7 us -> 18.2 us
    all_to_all x1 -> x0, waiting for transfers between devices: 8.52 us -> none  [per_device(): lax.all_to_all(windows, 'shell', split_axis=0, concat_axis=0, tiled=True)]
    all_to_all x1 -> x0, starting transfers between devices: 3.48 us -> none  [per_device(): lax.all_to_all(windows, 'shell', split_axis=0, concat_axis=0, tiled=True)]
    ppermute x0 -> x3, starting transfers between devices: none -> 2.89 us  [per_device(): lax.ppermute(outgoing, 'shell', [(i, (i + shift) % shell_count) for i in...]
  transfers between devices with their start and end apart: 8 -> 10, of which waited for: 5 -> 4; matrix products, arithmetic and copies ran while one was open for 6% -> 7% of each run, Pallas kernels for 5% -> 6%
where the time goes in v6:
time: 102 us; the launch traced here: 101 us
  starting transfers between devices  32.1 us (31%)
  Pallas kernels  21.5 us (21%)
  waiting for transfers between devices  18.2 us (18%)
  local copies, waits for them, and re-layouts  8.82 us (9%)
  blocking collectives  8.13 us (8%)
  matrix products  7.83 us (8%)
  other arithmetic  3.54 us (3%)
    ppermute x3, waiting for transfers between devices, extended(): lax.ppermute(lax.slice_in_dim(block, 0, width, axis=dim), axis, backward)  17.6 us
    pallas_call x1, Pallas kernels, deposit_sums(): pl.pallas_call(functools.partial(scatter_kernel, rows, columns), out_shap...  15.7 us
    all_to_all x1, starting transfers between devices, per_device(): lax.all_to_all(packet.reshape(4, devices, -1), ('shell', 'tile'), split_a...  13.9 us
    ppermute x3, starting transfers between devices, extended(): lax.ppermute(lax.slice_in_dim(block, block.shape[dim] - width, None, axis...  8.84 us
    all_gather x1, blocking collectives, per_device(): full_grad = lax.all_gather(bin_grad, 'shell', axis=2, tiled=True)  8.13 us
    ppermute x3, starting transfers between devices, extended(): lax.ppermute(lax.slice_in_dim(block, 0, width, axis=dim), axis, backward)  6.53 us
    pallas_call x1, Pallas kernels, correlate_forward(): pl.pallas_call(correlate_kernel, out_shape=jax.ShapeDtypeStruct((kinds, b...  5.87 us
    ppermute x3, starting transfers between devices, per_device(): lax.ppermute(outgoing, 'shell', [(i, (i + shift) % shell_count) for i in...  2.89 us
  transfers between devices with their start and end apart: 10, of which 4 were waited for; matrix products, arithmetic and copies ran while one was open for 7% of the time, Pallas kernels for 6%

profile of v6, /device:TPU:124, one launch (start us, length us, event | category | flops | bytes accessed | tf_op | source)
XLA Modules:
  0.0 100.8 jit_solution(6806201504544301622)
XLA Ops:
  0.8 2.6 %convolution_bitcast_fusion.1 = f32[5,32,512]{2,0,1:T(8,128)S(1)} fusion(f32[16,32,512]{2,1,0:T(8,128)} %param.10, f32[16]{0:T(128)S(1)} %multiply_multiply_fusion, f32[16]{0:T(128)} %param.11, f32[5,16]{1,0:T(8,128)S(1)} %copy-done), kind=kOutput, calls=%fused_computation.11 | convolution fusion | flops 16515072 | bytes 1376704 | tf_op jit(solution)/shard_map/bs,srw->brw/dot_general | solution.py:169
  4.2 1.3 %collective-permute-start.1 = (f32[5,32,160]{2,1,0:T(8,128)S(1)}, f32[5,32,160]{2,1,0:T(8,128)S(1)}, u32[]{:S(2)}, u32[]{:S(2)}) collective-permute-start(f32[5,32,160]{2,1,0:T(8,128)S(1)} %bitcast.206), channel_id=1, source_target_pairs={{0,128},{64,192},{128,0},{192,64},{1,129},{65,193},{129,1},{193,65... | collective-permute-start | bytes 307208 | tf_op jit(solution)/shard_map/ppermute | solution.py:184
  5.6 1.5 %collective-permute-start.2 = (f32[5,32,160]{2,1,0:T(8,128)S(1)}, f32[5,32,160]{2,1,0:T(8,128)S(1)}, u32[]{:S(2)}, u32[]{:S(2)}) collective-permute-start(f32[5,32,160]{2,1,0:T(8,128)S(1)} %bitcast.207), channel_id=1, source_target_pairs={{0,192},{64,0},{128,64},{192,128},{1,193},{65,1},{129,65},{193,129... | collective-permute-start | bytes 307208 | tf_op jit(solution)/shard_map/ppermute | solution.py:184
  7.6 1.1 %pad_maximum_fusion.1 = f32[4,256,128]{2,0,1:T(4,128)} fusion(f32[2,256,128]{2,0,1:T(2,128)S(1)} %bitcast.200, f32[1,256,128]{2,0,1:T(1,128)S(1)} %bitcast.199, f32[1,256,128]{2,0,1:T(1,128)S(1)} %bitcast.203), kind=kLoop, calls=%fused_computation.20 | loop fusion | flops 262144 | bytes 1048576 | tf_op jit(solution)/shard_map/concatenate | solution.py:155
  8.7 13.9 %all-to-all-start = ((f32[4,256,128]{2,0,1:T(4,128)}), f32[4,256,128]{2,0,1:T(4,128)S(1)}, u32[]{:S(2)}, u32[]{:S(2)}) async-start(f32[4,256,128]{2,0,1:T(4,128)} %pad_maximum_fusion.1), calls=%async_computation | async-start | bytes 1048576 | tf_op jit(solution)/shard_map/all_to_all | solution.py:159
  22.7 4.6 %collective-permute-start.3 = (bf16[5,16,160]{2,1,0:T(8,128)(2,1)S(1)}, bf16[5,16,160]{2,1,0:T(8,128)(2,1)S(1)}, u32[]{:S(2)}, u32[]{:S(2)}) collective-permute-start(bf16[5,16,160]{2,1,0:T(8,128)(2,1)S(1)} %get-tuple-element.19), channel_id=1, source_target_pairs={{0,1},{1,2},{2,3},{3,4},{4,5},{5,6},{6,7},{7,8},{8,9},{9,10},{10,1... | collective-permute-start | bytes 76808 | tf_op jit(solution)/shard_map/ppermute | solution.py:22
  27.3 2.1 %collective-permute-start.4 = (bf16[5,16,160]{2,1,0:T(8,128)(2,1)S(1)}, bf16[5,16,160]{2,1,0:T(8,128)(2,1)S(1)}, u32[]{:S(2)}, u32[]{:S(2)}) collective-permute-start(bf16[5,16,160]{2,1,0:T(8,128)(2,1)S(1)} %get-tuple-element.20), channel_id=1, source_target_pairs={{1,0},{2,1},{3,2},{4,3},{5,4},{6,5},{7,6},{8,7},{9,8},{10,9},{11,1... | collective-permute-start | bytes 76808 | tf_op jit(solution)/shard_map/ppermute | solution.py:25
  29.5 1.0 %fusion.3 = bf16[160,128,2,33]{1,3,2,0:T(8,128)(2,1)S(1)} fusion(bf16[2,33,33]{2,0,1:T(2,128)(2,1)S(1)} %copy-done.8), kind=kOutput, calls=%fused_computation.5 | convolution fusion | flops 90562560 | bytes 2707716 | tf_op jit(solution)/shard_map/kdv,vjc->kdjc/dot_general | solution.py:37
  30.5 2.2 %copy.76 = bf16[160,128,2,33]{1,0,3,2:T(8,128)(2,1)} copy(bf16[160,128,2,33]{1,3,2,0:T(8,128)(2,1)S(1)} %fusion.3) | data formatting | bytes 5406720 | tf_op jit(solution)/shard_map/kdv,vjc->kdjc/dot_general | solution.py:37
  33.2 5.7 %collective-permute-done.4 = bf16[5,16,160]{2,1,0:T(8,128)(2,1)S(1)} collective-permute-done((bf16[5,16,160]{2,1,0:T(8,128)(2,1)S(1)}, bf16[5,16,160]{2,1,0:T(8,128)(2,1)S(1)}, u32[]{:S(2)}, u32[]{:S(2)}) %collective-permute-start.4) | collective-permute-done | bytes 25632 | tf_op jit(solution)/shard_map/ppermute | solution.py:25
  39.6 5.9 %shard_map.100 = f32[2,5,32,128]{3,2,1,0:T(8,128)} custom-call(bf16[5,64,160]{2,1,0:T(8,128)(2,1)} %pad_maximum_fusion.3.x_ref, bf16[2,33,160,128]{3,2,1,0:T(8,128)(2,1)} %bitcast.198), custom_call_target="tpu_custom_call" | custom-call | flops 865075200 | bytes 2969600 | tf_op jit(solution)/shard_map/pallas_call | solution.py:119
  46.3 15.7 %shard_map.101 = f32[3,160,128]{2,1,0:T(8,128)} custom-call(f32[4,32768]{1,0:T(4,128)} %bitcast.202), custom_call_target="tpu_custom_call" | custom-call | flops 8053063680 | bytes 770048 | tf_op jit(solution)/shard_map/pallas_call | solution.py:90
  62.0 0.9 slice.220
  64.0 1.3 %collective-permute-start.5 = (bf16[2,5,32,16]{3,2,1,0:T(8,128)(2,1)S(1)}, bf16[2,5,32,16]{3,2,1,0:T(8,128)(2,1)S(1)}, u32[]{:S(2)}, u32[]{:S(2)}) collective-permute-start(bf16[2,5,32,16]{3,2,1,0:T(8,128)(2,1)S(1)} %get-tuple-element.17), channel_id=1, source_target_pairs={{0,64},{64,128},{128,192},{1,65},{65,129},{129,193},{2,66},{66,130... | collective-permute-start | bytes 30728 | tf_op jit(solution)/shard_map/ppermute | solution.py:22
  65.3 1.3 %collective-permute-start.6 = (bf16[2,5,32,16]{3,2,1,0:T(8,128)(2,1)S(1)}, bf16[2,5,32,16]{3,2,1,0:T(8,128)(2,1)S(1)}, u32[]{:S(2)}, u32[]{:S(2)}) collective-permute-start(bf16[2,5,32,16]{3,2,1,0:T(8,128)(2,1)S(1)} %get-tuple-element.18), channel_id=1, source_target_pairs={{64,0},{128,64},{192,128},{65,1},{129,65},{193,129},{66,2},{130,66... | collective-permute-start | bytes 30728 | tf_op jit(solution)/shard_map/ppermute | solution.py:25
  66.7 4.0 %collective-permute-done.6 = bf16[2,5,32,16]{3,2,1,0:T(8,128)(2,1)S(1)} collective-permute-done((bf16[2,5,32,16]{3,2,1,0:T(8,128)(2,1)S(1)}, bf16[2,5,32,16]{3,2,1,0:T(8,128)(2,1)S(1)}, u32[]{:S(2)}, u32[]{:S(2)}) %collective-permute-start.6) | collective-permute-done | bytes 10272 | tf_op jit(solution)/shard_map/ppermute | solution.py:25
  70.9 2.9 %collective-permute-start.7 = (bf16[2,5,16,160]{3,2,1,0:T(8,128)(2,1)S(1)}, bf16[2,5,16,160]{3,2,1,0:T(8,128)(2,1)S(1)}, u32[]{:S(2)}, u32[]{:S(2)}) collective-permute-start(bf16[2,5,16,160]{3,2,1,0:T(8,128)(2,1)S(1)} %get-tuple-element.16), channel_id=1, source_target_pairs={{0,1},{1,2},{2,3},{3,4},{4,5},{5,6},{6,7},{7,8},{8,9},{9,10},{10,1... | collective-permute-start | bytes 153608 | tf_op jit(solution)/shard_map/ppermute | solution.py:22
  73.8 3.1 %collective-permute-start.8 = (bf16[2,5,16,160]{3,2,1,0:T(8,128)(2,1)S(1)}, bf16[2,5,16,160]{3,2,1,0:T(8,128)(2,1)S(1)}, u32[]{:S(2)}, u32[]{:S(2)}) collective-permute-start(bf16[2,5,16,160]{3,2,1,0:T(8,128)(2,1)S(1)} %get-tuple-element.15), channel_id=1, source_target_pairs={{1,0},{2,1},{3,2},{4,3},{5,4},{6,5},{7,6},{8,7},{9,8},{10,9},{11,1... | collective-permute-start | bytes 153608 | tf_op jit(solution)/shard_map/ppermute | solution.py:25
  77.0 1.0 %convert_bitcast_fusion = bf16[2,33,160,128,1]{3,1,0,2,4:T(8,128)(2,1)S(1)} fusion(bf16[2,33,33]{2,0,1:T(2,128)(2,1)S(1)} %rev.4), kind=kOutput, calls=%fused_computation.1 | convolution fusion | flops 91914240 | bytes 2707716 | tf_op jit(solution)/shard_map/kdv,vjc->kdjc/dot_general | solution.py:37
  78.0 7.9 %collective-permute-done.8 = bf16[2,5,16,160]{3,2,1,0:T(8,128)(2,1)S(1)} collective-permute-done((bf16[2,5,16,160]{3,2,1,0:T(8,128)(2,1)S(1)}, bf16[2,5,16,160]{3,2,1,0:T(8,128)(2,1)S(1)}, u32[]{:S(2)}, u32[]{:S(2)}) %collective-permute-start.8) | collective-permute-done | bytes 51232 | tf_op jit(solution)/shard_map/ppermute | solution.py:25
  87.8 1.6 %fusion.11 = f32[5,32,128]{2,1,0:T(8,128)S(1)} fusion(bf16[2,5,33,32,160]{4,3,1,0,2:T(8,128)(2,1)S(1)} %fusion.24, bf16[2,33,160,128,1]{3,1,0,2,4:T(8,128)(2,1)S(1)} %convert_bitcast_fusion), kind=kOutput, calls=%fused_computation.12 | convolution fusion | flops 432537600 | bytes 6164480 | tf_op jit(solution)/shard_map/kbdrj,kdjc->brc/dot_general | solution.py:195
  89.4 8.1 %all_gather.3 = f32[5,32,512]{2,1,0:T(8,128)S(1)} all-gather(f32[5,32,128]{2,1,0:T(8,128)S(1)} %fusion.11), channel_id=1, replica_groups=mesh['shell'=4,'tile'=64] {'shell'}, dimensions={2}, use_global_device_ids=true | all-gather | bytes 409600 | tf_op jit(solution)/shard_map/all_gather | solution.py:201
  97.5 1.7 %fusion.10 = f32[16,32,512]{2,0,1:T(8,128)S(1)} fusion(f32[16,32,512]{2,1,0:T(8,128)S(1)} %copy-done.1, f32[5,32,512]{2,1,0:T(8,128)S(1)} %all_gather.3, f32[16]{0:T(128)S(1)} %multiply_multiply_fusion, f32[16]{0:T(128)S(1)} %copy-done.11, f32[5,16]{1,0:T(8,128)S(1)} %copy-done), kind=kOutput, calls=%fused_computation.10 | convolution fusion | flops 16777216 | bytes 2425280 | tf_op jit(solution)/shard_map/bs,brw->srw/dot_general | solution.py:202
  99.2 1.6 %copy.39 = f32[16,32,512]{2,1,0:T(8,128)} copy(f32[16,32,512]{2,0,1:T(8,128)S(1)} %fusion.10) | data formatting | bytes 2097152 | tf_op jit(solution)/shard_map/mul | solution.py:209
  (87 shorter events, 7.1 us)
Async XLA Ops:
  0.0 0.8 copy-start
  0.0 7.1 %copy-start.7 = (f32[4,64,128]{2,1,0:T(8,128)S(1)}, f32[4,64,128]{2,1,0:T(8,128)}, u32[]{:S(2)}) copy-start(f32[4,64,128]{2,1,0:T(8,128)} %param.18) | copy-start | bytes 393220
  0.0 7.1 %copy-start.10 = (s32[4,64]{1,0:T(4,128)S(1)}, s32[4,64]{1,0:T(4,128)}, u32[]{:S(2)}) copy-start(s32[4,64]{1,0:T(4,128)} %param.19) | copy-start | bytes 3076
  0.0 7.2 %copy-start.3 = (f32[2,4,64,128]{3,2,1,0:T(8,128)S(1)}, f32[2,4,64,128]{3,2,1,0:T(8,128)}, u32[]{:S(2)}) copy-start(f32[2,4,64,128]{3,2,1,0:T(8,128)} %param.17) | copy-start | bytes 786436
  0.0 7.4 %copy-start.5 = (s32[4,64,128]{2,1,0:T(8,128)S(1)}, s32[4,64,128]{2,1,0:T(8,128)}, u32[]{:S(2)}) copy-start(s32[4,64,128]{2,1,0:T(8,128)} %param.15) | copy-start | bytes 393220
  0.0 7.4 %copy-start.6 = (s32[4,64,128]{2,1,0:T(8,128)S(1)}, s32[4,64,128]{2,1,0:T(8,128)}, u32[]{:S(2)}) copy-start(s32[4,64,128]{2,1,0:T(8,128)} %param.16) | copy-start | bytes 393220
  3.7 25.7 %copy-start.8 = (bf16[2,33,33]{2,0,1:T(2,128)(2,1)S(1)}, bf16[2,33,33]{2,0,1:T(2,128)(2,1)}, u32[]{:S(2)}) copy-start(bf16[2,33,33]{2,0,1:T(2,128)(2,1)} %param.13) | copy-start | bytes 13072
  4.1 18.5 %collective-permute-start = (f32[5,32,160]{2,1,0:T(8,128)S(1)}, f32[5,32,160]{2,1,0:T(8,128)S(1)}, u32[]{:S(2)}, u32[]{:S(2)}) collective-permute-start(f32[5,32,160]{2,1,0:T(8,128)S(1)} %bitcast.205), channel_id=1, source_target_pairs={{0,64},{64,128},{128,192},{192,0},{1,65},{65,129},{129,193},{193,1... | collective-permute-start | bytes 307208 | tf_op jit(solution)/shard_map/ppermute | solution.py:184
  4.2 18.4 %collective-permute-start.1 = (f32[5,32,160]{2,1,0:T(8,128)S(1)}, f32[5,32,160]{2,1,0:T(8,128)S(1)}, u32[]{:S(2)}, u32[]{:S(2)}) collective-permute-start(f32[5,32,160]{2,1,0:T(8,128)S(1)} %bitcast.206), channel_id=1, source_target_pairs={{0,128},{64,192},{128,0},{192,64},{1,129},{65,193},{129,1},{193,65... | collective-permute-start | bytes 307208 | tf_op jit(solution)/shard_map/ppermute | solution.py:184
  5.6 17.1 %collective-permute-start.2 = (f32[5,32,160]{2,1,0:T(8,128)S(1)}, f32[5,32,160]{2,1,0:T(8,128)S(1)}, u32[]{:S(2)}, u32[]{:S(2)}) collective-permute-start(f32[5,32,160]{2,1,0:T(8,128)S(1)} %bitcast.207), channel_id=1, source_target_pairs={{0,192},{64,0},{128,64},{192,128},{1,193},{65,1},{129,65},{193,129... | collective-permute-start | bytes 307208 | tf_op jit(solution)/shard_map/ppermute | solution.py:184
  8.7 24.0 %copy-start.9 = (s32[32,128]{1,0:T(8,128)S(1)}, s32[32,128]{1,0:T(8,128)}, u32[]{:S(2)}) copy-start(s32[32,128]{1,0:T(8,128)} %param.14) | copy-start | bytes 49156
  8.7 36.8 %all-to-all-start = ((f32[4,256,128]{2,0,1:T(4,128)}), f32[4,256,128]{2,0,1:T(4,128)S(1)}, u32[]{:S(2)}, u32[]{:S(2)}) async-start(f32[4,256,128]{2,0,1:T(4,128)} %pad_maximum_fusion.1), calls=%async_computation | async-start | bytes 1048576 | tf_op jit(solution)/shard_map/all_to_all | solution.py:159
  22.7 10.5 %collective-permute-start.3 = (bf16[5,16,160]{2,1,0:T(8,128)(2,1)S(1)}, bf16[5,16,160]{2,1,0:T(8,128)(2,1)S(1)}, u32[]{:S(2)}, u32[]{:S(2)}) collective-permute-start(bf16[5,16,160]{2,1,0:T(8,128)(2,1)S(1)} %get-tuple-element.19), channel_id=1, source_target_pairs={{0,1},{1,2},{2,3},{3,4},{4,5},{5,6},{6,7},{7,8},{8,9},{9,10},{10,1... | collective-permute-start | bytes 76808 | tf_op jit(solution)/shard_map/ppermute | solution.py:22
  27.3 11.6 %collective-permute-start.4 = (bf16[5,16,160]{2,1,0:T(8,128)(2,1)S(1)}, bf16[5,16,160]{2,1,0:T(8,128)(2,1)S(1)}, u32[]{:S(2)}, u32[]{:S(2)}) collective-permute-start(bf16[5,16,160]{2,1,0:T(8,128)(2,1)S(1)} %get-tuple-element.20), channel_id=1, source_target_pairs={{1,0},{2,1},{3,2},{4,3},{5,4},{6,5},{7,6},{8,7},{9,8},{10,9},{11,1... | collective-permute-start | bytes 76808 | tf_op jit(solution)/shard_map/ppermute | solution.py:25
  45.5 0.8 copy-start.2
  46.3 17.5 %copy-start.4 = (f32[2,5,32,128]{3,2,1,0:T(8,128)S(1)}, f32[2,5,32,128]{3,2,1,0:T(8,128)}, u32[]{:S(2)}) copy-start(f32[2,5,32,128]{3,2,1,0:T(8,128)} %shard_map.100) | copy-start | bytes 491524
  64.0 2.7 %collective-permute-start.5 = (bf16[2,5,32,16]{3,2,1,0:T(8,128)(2,1)S(1)}, bf16[2,5,32,16]{3,2,1,0:T(8,128)(2,1)S(1)}, u32[]{:S(2)}, u32[]{:S(2)}) collective-permute-start(bf16[2,5,32,16]{3,2,1,0:T(8,128)(2,1)S(1)} %get-tuple-element.17), channel_id=1, source_target_pairs={{0,64},{64,128},{128,192},{1,65},{65,129},{129,193},{2,66},{66,130... | collective-permute-start | bytes 30728 | tf_op jit(solution)/shard_map/ppermute | solution.py:22
  65.3 5.5 %collective-permute-start.6 = (bf16[2,5,32,16]{3,2,1,0:T(8,128)(2,1)S(1)}, bf16[2,5,32,16]{3,2,1,0:T(8,128)(2,1)S(1)}, u32[]{:S(2)}, u32[]{:S(2)}) collective-permute-start(bf16[2,5,32,16]{3,2,1,0:T(8,128)(2,1)S(1)} %get-tuple-element.18), channel_id=1, source_target_pairs={{64,0},{128,64},{192,128},{65,1},{129,65},{193,129},{66,2},{130,66... | collective-permute-start | bytes 30728 | tf_op jit(solution)/shard_map/ppermute | solution.py:25
  70.9 7.1 %collective-permute-start.7 = (bf16[2,5,16,160]{3,2,1,0:T(8,128)(2,1)S(1)}, bf16[2,5,16,160]{3,2,1,0:T(8,128)(2,1)S(1)}, u32[]{:S(2)}, u32[]{:S(2)}) collective-permute-start(bf16[2,5,16,160]{3,2,1,0:T(8,128)(2,1)S(1)} %get-tuple-element.16), channel_id=1, source_target_pairs={{0,1},{1,2},{2,3},{3,4},{4,5},{5,6},{6,7},{7,8},{8,9},{9,10},{10,1... | collective-permute-start | bytes 153608 | tf_op jit(solution)/shard_map/ppermute | solution.py:22
  73.8 12.1 %collective-permute-start.8 = (bf16[2,5,16,160]{3,2,1,0:T(8,128)(2,1)S(1)}, bf16[2,5,16,160]{3,2,1,0:T(8,128)(2,1)S(1)}, u32[]{:S(2)}, u32[]{:S(2)}) collective-permute-start(bf16[2,5,16,160]{3,2,1,0:T(8,128)(2,1)S(1)} %get-tuple-element.15), channel_id=1, source_target_pairs={{1,0},{2,1},{3,2},{4,3},{5,4},{6,5},{7,6},{8,7},{9,8},{10,9},{11,1... | collective-permute-start | bytes 153608 | tf_op jit(solution)/shard_map/ppermute | solution.py:25
  87.6 9.9 %copy-start.1 = (f32[16,32,512]{2,1,0:T(8,128)S(1)}, f32[16,32,512]{2,1,0:T(8,128)}, u32[]{:S(2)}) copy-start(f32[16,32,512]{2,1,0:T(8,128)} %param.10) | copy-start | bytes 3145732
  87.6 9.9 %copy-start.11 = (f32[16]{0:T(128)S(1)}, f32[16]{0:T(128)}, u32[]{:S(2)}) copy-start(f32[16]{0:T(128)} %param.11) | copy-start | bytes 196

commit v7 on v6

--- a/solution.py
+++ b/solution.py
@@ -55,9 +55,8 @@
     def body(step, carry):
         start = pl.multiple_of(step * CHUNK, CHUNK)
         block = packet_ref[:, pl.ds(start, CHUNK)]
-        code = block[0:1].astype(jnp.int32)
-        row_of = code >> 7
-        col_of = code & (columns - 1)
+        row_of = ((block[0:1] + 0.5) * (1.0 / columns)).astype(jnp.int32)
+        col_of = block[0:1].astype(jnp.int32) - row_of * columns
         row_hot = (lax.broadcasted_iota(jnp.int32, (rows, CHUNK), 0) == row_of).astype(
             jnp.bfloat16
         )
@@ -159,7 +158,8 @@
     arrived = lax.all_to_all(
         packet.reshape(4, devices, -1), ("shell", "tile"), split_axis=1, concat_axis=1, tiled=True
     )
-    sums = deposit_sums(arrived.reshape(4, -1), NBIN * height, columns)
+    sum_rows = 256
+    sums = deposit_sums(arrived.reshape(4, -1), sum_rows, NBIN * pixels // sum_rows)
     sums = sums.reshape(3, NBIN, height, columns)
     weight_sum = sums[0]
     shape_sum = sums[1:]

time: 102 us -> 97.7 us (0.958)
  Pallas kernels: 21.5 us -> 16.9 us
    pallas_call x1, Pallas kernels: 15.7 us -> 11 us  [deposit_sums(): pl.pallas_call(functools.partial(scatter_kernel, rows, columns), out_shap...]
where the time goes in v7:
time: 97.7 us; the launch traced here: 96.5 us
  starting transfers between devices  32.1 us (33%)
  waiting for transfers between devices  18.2 us (19%)
  Pallas kernels  16.9 us (17%)
  local copies, waits for them, and re-layouts  9.2 us (9%)
  blocking collectives  8.13 us (8%)
  matrix products  7.83 us (8%)
  other arithmetic  3.53 us (4%)
    ppermute x3, waiting for transfers between devices, extended(): lax.ppermute(lax.slice_in_dim(block, 0, width, axis=dim), axis, backward)  17.6 us
    all_to_all x1, starting transfers between devices, per_device(): lax.all_to_all(packet.reshape(4, devices, -1), ('shell', 'tile'), split_a...  13.9 us
    pallas_call x1, Pallas kernels, deposit_sums(): pl.pallas_call(functools.partial(scatter_kernel, rows, columns), out_shap...  11 us
    ppermute x3, starting transfers between devices, extended(): lax.ppermute(lax.slice_in_dim(block, block.shape[dim] - width, None, axis...  8.84 us
    all_gather x1, blocking collectives, per_device(): full_grad = lax.all_gather(bin_grad, 'shell', axis=2, tiled=True)  8.13 us
    ppermute x3, starting transfers between devices, extended(): lax.ppermute(lax.slice_in_dim(block, 0, width, axis=dim), axis, backward)  6.53 us
    pallas_call x1, Pallas kernels, correlate_forward(): pl.pallas_call(correlate_kernel, out_shape=jax.ShapeDtypeStruct((kinds, b...  5.87 us
    ppermute x3, starting transfers between devices, per_device(): lax.ppermute(outgoing, 'shell', [(i, (i + shift) % shell_count) for i in...  2.89 us
  transfers between devices with their start and end apart: 10, of which 4 were waited for; matrix products, arithmetic and copies ran while one was open for 7% of the time, Pallas kernels for 6%

profile of v7, /device:TPU:124, one launch (start us, length us, event | category | flops | bytes accessed | tf_op | source)
XLA Modules:
  0.0 96.5 jit_solution(12454183318684985451)
XLA Ops:
  0.8 2.6 %convolution_bitcast_fusion.1 = f32[5,32,512]{2,0,1:T(8,128)S(1)} fusion(f32[16,32,512]{2,1,0:T(8,128)} %param.10, f32[16]{0:T(128)S(1)} %multiply_multiply_fusion, f32[16]{0:T(128)} %param.11, f32[5,16]{1,0:T(8,128)S(1)} %copy-done), kind=kOutput, calls=%fused_computation.11 | convolution fusion | flops 16515072 | bytes 1376704 | tf_op jit(solution)/shard_map/bs,srw->brw/dot_general | solution.py:169
  4.2 1.3 %collective-permute-start.1 = (f32[5,32,160]{2,1,0:T(8,128)S(1)}, f32[5,32,160]{2,1,0:T(8,128)S(1)}, u32[]{:S(2)}, u32[]{:S(2)}) collective-permute-start(f32[5,32,160]{2,1,0:T(8,128)S(1)} %bitcast.202), channel_id=1, source_target_pairs={{0,128},{64,192},{128,0},{192,64},{1,129},{65,193},{129,1},{193,65... | collective-permute-start | bytes 307208 | tf_op jit(solution)/shard_map/ppermute | solution.py:184
  5.6 1.5 %collective-permute-start.2 = (f32[5,32,160]{2,1,0:T(8,128)S(1)}, f32[5,32,160]{2,1,0:T(8,128)S(1)}, u32[]{:S(2)}, u32[]{:S(2)}) collective-permute-start(f32[5,32,160]{2,1,0:T(8,128)S(1)} %bitcast.203), channel_id=1, source_target_pairs={{0,192},{64,0},{128,64},{192,128},{1,193},{65,1},{129,65},{193,129... | collective-permute-start | bytes 307208 | tf_op jit(solution)/shard_map/ppermute | solution.py:184
  7.6 1.1 %pad_maximum_fusion.1 = f32[4,256,128]{2,0,1:T(4,128)} fusion(f32[2,256,128]{2,0,1:T(2,128)S(1)} %bitcast.198, f32[1,256,128]{2,0,1:T(1,128)S(1)} %bitcast.197, f32[1,256,128]{2,0,1:T(1,128)S(1)} %bitcast.200), kind=kLoop, calls=%fused_computation.20 | loop fusion | flops 262144 | bytes 1048576 | tf_op jit(solution)/shard_map/concatenate | solution.py:154
  8.7 13.9 %all-to-all-start = ((f32[4,256,128]{2,0,1:T(4,128)}), f32[4,256,128]{2,0,1:T(4,128)S(1)}, u32[]{:S(2)}, u32[]{:S(2)}) async-start(f32[4,256,128]{2,0,1:T(4,128)} %pad_maximum_fusion.1), calls=%async_computation | async-start | bytes 1048576 | tf_op jit(solution)/shard_map/all_to_all | solution.py:158
  22.7 4.6 %collective-permute-start.3 = (bf16[5,16,160]{2,1,0:T(8,128)(2,1)S(1)}, bf16[5,16,160]{2,1,0:T(8,128)(2,1)S(1)}, u32[]{:S(2)}, u32[]{:S(2)}) collective-permute-start(bf16[5,16,160]{2,1,0:T(8,128)(2,1)S(1)} %get-tuple-element.19), channel_id=1, source_target_pairs={{0,1},{1,2},{2,3},{3,4},{4,5},{5,6},{6,7},{7,8},{8,9},{9,10},{10,1... | collective-permute-start | bytes 76808 | tf_op jit(solution)/shard_map/ppermute | solution.py:22
  27.3 2.1 %collective-permute-start.4 = (bf16[5,16,160]{2,1,0:T(8,128)(2,1)S(1)}, bf16[5,16,160]{2,1,0:T(8,128)(2,1)S(1)}, u32[]{:S(2)}, u32[]{:S(2)}) collective-permute-start(bf16[5,16,160]{2,1,0:T(8,128)(2,1)S(1)} %get-tuple-element.20), channel_id=1, source_target_pairs={{1,0},{2,1},{3,2},{4,3},{5,4},{6,5},{7,6},{8,7},{9,8},{10,9},{11,1... | collective-permute-start | bytes 76808 | tf_op jit(solution)/shard_map/ppermute | solution.py:25
  29.5 1.0 %fusion.3 = bf16[160,128,2,33]{1,3,2,0:T(8,128)(2,1)S(1)} fusion(bf16[2,33,33]{2,0,1:T(2,128)(2,1)S(1)} %copy-done.8), kind=kOutput, calls=%fused_computation.5 | convolution fusion | flops 90562560 | bytes 2707716 | tf_op jit(solution)/shard_map/kdv,vjc->kdjc/dot_general | solution.py:37
  30.5 2.2 %copy.75 = bf16[160,128,2,33]{1,0,3,2:T(8,128)(2,1)} copy(bf16[160,128,2,33]{1,3,2,0:T(8,128)(2,1)S(1)} %fusion.3) | data formatting | bytes 5406720 | tf_op jit(solution)/shard_map/kdv,vjc->kdjc/dot_general | solution.py:37
  33.2 5.7 %collective-permute-done.4 = bf16[5,16,160]{2,1,0:T(8,128)(2,1)S(1)} collective-permute-done((bf16[5,16,160]{2,1,0:T(8,128)(2,1)S(1)}, bf16[5,16,160]{2,1,0:T(8,128)(2,1)S(1)}, u32[]{:S(2)}, u32[]{:S(2)}) %collective-permute-start.4) | collective-permute-done | bytes 25632 | tf_op jit(solution)/shard_map/ppermute | solution.py:25
  39.6 5.9 %shard_map.100 = f32[2,5,32,128]{3,2,1,0:T(8,128)} custom-call(bf16[5,64,160]{2,1,0:T(8,128)(2,1)} %pad_maximum_fusion.3.x_ref, bf16[2,33,160,128]{3,2,1,0:T(8,128)(2,1)} %bitcast.196), custom_call_target="tpu_custom_call" | custom-call | flops 865075200 | bytes 2969600 | tf_op jit(solution)/shard_map/pallas_call | solution.py:118
  46.3 11.0 %shard_map.101 = f32[3,256,80]{2,1,0:T(8,128)} custom-call(f32[4,32768]{1,0:T(4,128)} %bitcast.199), custom_call_target="tpu_custom_call" | custom-call | flops 8053063680 | bytes 770048 | tf_op jit(solution)/shard_map/pallas_call | solution.py:89
  57.3 1.0 %slice.220 = f32[2,256,80]{2,1,0:T(8,128)S(1)} slice(f32[3,256,80]{2,1,0:T(8,128)} %shard_map.101), slice={[1:3], [0:256], [0:80]} | slice | bytes 327680 | tf_op jit(solution)/shard_map/slice | solution.py:165
  59.7 1.3 %collective-permute-start.5 = (bf16[2,5,32,16]{3,2,1,0:T(8,128)(2,1)S(1)}, bf16[2,5,32,16]{3,2,1,0:T(8,128)(2,1)S(1)}, u32[]{:S(2)}, u32[]{:S(2)}) collective-permute-start(bf16[2,5,32,16]{3,2,1,0:T(8,128)(2,1)S(1)} %get-tuple-element.17), channel_id=1, source_target_pairs={{0,64},{64,128},{128,192},{1,65},{65,129},{129,193},{2,66},{66,130... | collective-permute-start | bytes 30728 | tf_op jit(solution)/shard_map/ppermute | solution.py:22
  61.0 1.3 %collective-permute-start.6 = (bf16[2,5,32,16]{3,2,1,0:T(8,128)(2,1)S(1)}, bf16[2,5,32,16]{3,2,1,0:T(8,128)(2,1)S(1)}, u32[]{:S(2)}, u32[]{:S(2)}) collective-permute-start(bf16[2,5,32,16]{3,2,1,0:T(8,128)(2,1)S(1)} %get-tuple-element.18), channel_id=1, source_target_pairs={{64,0},{128,64},{192,128},{65,1},{129,65},{193,129},{66,2},{130,66... | collective-permute-start | bytes 30728 | tf_op jit(solution)/shard_map/ppermute | solution.py:25
  62.4 4.0 %collective-permute-done.6 = bf16[2,5,32,16]{3,2,1,0:T(8,128)(2,1)S(1)} collective-permute-done((bf16[2,5,32,16]{3,2,1,0:T(8,128)(2,1)S(1)}, bf16[2,5,32,16]{3,2,1,0:T(8,128)(2,1)S(1)}, u32[]{:S(2)}, u32[]{:S(2)}) %collective-permute-start.6) | collective-permute-done | bytes 10272 | tf_op jit(solution)/shard_map/ppermute | solution.py:25
  66.6 2.9 %collective-permute-start.7 = (bf16[2,5,16,160]{3,2,1,0:T(8,128)(2,1)S(1)}, bf16[2,5,16,160]{3,2,1,0:T(8,128)(2,1)S(1)}, u32[]{:S(2)}, u32[]{:S(2)}) collective-permute-start(bf16[2,5,16,160]{3,2,1,0:T(8,128)(2,1)S(1)} %get-tuple-element.16), channel_id=1, source_target_pairs={{0,1},{1,2},{2,3},{3,4},{4,5},{5,6},{6,7},{7,8},{8,9},{9,10},{10,1... | collective-permute-start | bytes 153608 | tf_op jit(solution)/shard_map/ppermute | solution.py:22
  69.6 3.1 %collective-permute-start.8 = (bf16[2,5,16,160]{3,2,1,0:T(8,128)(2,1)S(1)}, bf16[2,5,16,160]{3,2,1,0:T(8,128)(2,1)S(1)}, u32[]{:S(2)}, u32[]{:S(2)}) collective-permute-start(bf16[2,5,16,160]{3,2,1,0:T(8,128)(2,1)S(1)} %get-tuple-element.15), channel_id=1, source_target_pairs={{1,0},{2,1},{3,2},{4,3},{5,4},{6,5},{7,6},{8,7},{9,8},{10,9},{11,1... | collective-permute-start | bytes 153608 | tf_op jit(solution)/shard_map/ppermute | solution.py:25
  72.7 1.0 %convert_bitcast_fusion = bf16[2,33,160,128,1]{3,1,0,2,4:T(8,128)(2,1)S(1)} fusion(bf16[2,33,33]{2,0,1:T(2,128)(2,1)S(1)} %rev.4), kind=kOutput, calls=%fused_computation.1 | convolution fusion | flops 91914240 | bytes 2707716 | tf_op jit(solution)/shard_map/kdv,vjc->kdjc/dot_general | solution.py:37
  73.7 7.9 %collective-permute-done.8 = bf16[2,5,16,160]{3,2,1,0:T(8,128)(2,1)S(1)} collective-permute-done((bf16[2,5,16,160]{3,2,1,0:T(8,128)(2,1)S(1)}, bf16[2,5,16,160]{3,2,1,0:T(8,128)(2,1)S(1)}, u32[]{:S(2)}, u32[]{:S(2)}) %collective-permute-start.8) | collective-permute-done | bytes 51232 | tf_op jit(solution)/shard_map/ppermute | solution.py:25
  83.6 1.6 %fusion.11 = f32[5,32,128]{2,1,0:T(8,128)S(1)} fusion(bf16[2,5,33,32,160]{4,3,1,0,2:T(8,128)(2,1)S(1)} %fusion.24, bf16[2,33,160,128,1]{3,1,0,2,4:T(8,128)(2,1)S(1)} %convert_bitcast_fusion), kind=kOutput, calls=%fused_computation.12 | convolution fusion | flops 432537600 | bytes 6164480 | tf_op jit(solution)/shard_map/kbdrj,kdjc->brc/dot_general | solution.py:195
  85.1 8.1 %all_gather.3 = f32[5,32,512]{2,1,0:T(8,128)S(1)} all-gather(f32[5,32,128]{2,1,0:T(8,128)S(1)} %fusion.11), channel_id=1, replica_groups=mesh['shell'=4,'tile'=64] {'shell'}, dimensions={2}, use_global_device_ids=true | all-gather | bytes 409600 | tf_op jit(solution)/shard_map/all_gather | solution.py:201
  93.3 1.7 %fusion.10 = f32[16,32,512]{2,0,1:T(8,128)S(1)} fusion(f32[16,32,512]{2,1,0:T(8,128)S(1)} %copy-done.1, f32[5,32,512]{2,1,0:T(8,128)S(1)} %all_gather.3, f32[16]{0:T(128)S(1)} %multiply_multiply_fusion, f32[16]{0:T(128)S(1)} %copy-done.11, f32[5,16]{1,0:T(8,128)S(1)} %copy-done), kind=kOutput, calls=%fused_computation.10 | convolution fusion | flops 16777216 | bytes 2425280 | tf_op jit(solution)/shard_map/bs,brw->srw/dot_general | solution.py:202
  95.0 1.6 %copy.38 = f32[16,32,512]{2,1,0:T(8,128)} copy(f32[16,32,512]{2,0,1:T(8,128)S(1)} %fusion.10) | data formatting | bytes 2097152 | tf_op jit(solution)/shard_map/mul | solution.py:209
  (89 shorter events, 7.4 us)
Async XLA Ops:
  0.0 0.8 copy-start
  0.0 7.1 %copy-start.7 = (f32[4,64,128]{2,1,0:T(8,128)S(1)}, f32[4,64,128]{2,1,0:T(8,128)}, u32[]{:S(2)}) copy-start(f32[4,64,128]{2,1,0:T(8,128)} %param.18) | copy-start | bytes 393220
  0.0 7.1 %copy-start.10 = (s32[4,64]{1,0:T(4,128)S(1)}, s32[4,64]{1,0:T(4,128)}, u32[]{:S(2)}) copy-start(s32[4,64]{1,0:T(4,128)} %param.19) | copy-start | bytes 3076
  0.0 7.2 %copy-start.3 = (f32[2,4,64,128]{3,2,1,0:T(8,128)S(1)}, f32[2,4,64,128]{3,2,1,0:T(8,128)}, u32[]{:S(2)}) copy-start(f32[2,4,64,128]{3,2,1,0:T(8,128)} %param.17) | copy-start | bytes 786436
  0.0 7.4 %copy-start.5 = (s32[4,64,128]{2,1,0:T(8,128)S(1)}, s32[4,64,128]{2,1,0:T(8,128)}, u32[]{:S(2)}) copy-start(s32[4,64,128]{2,1,0:T(8,128)} %param.15) | copy-start | bytes 393220
  0.0 7.4 %copy-start.6 = (s32[4,64,128]{2,1,0:T(8,128)S(1)}, s32[4,64,128]{2,1,0:T(8,128)}, u32[]{:S(2)}) copy-start(s32[4,64,128]{2,1,0:T(8,128)} %param.16) | copy-start | bytes 393220
  3.7 25.7 %copy-start.8 = (bf16[2,33,33]{2,0,1:T(2,128)(2,1)S(1)}, bf16[2,33,33]{2,0,1:T(2,128)(2,1)}, u32[]{:S(2)}) copy-start(bf16[2,33,33]{2,0,1:T(2,128)(2,1)} %param.13) | copy-start | bytes 13072
  4.1 18.5 %collective-permute-start = (f32[5,32,160]{2,1,0:T(8,128)S(1)}, f32[5,32,160]{2,1,0:T(8,128)S(1)}, u32[]{:S(2)}, u32[]{:S(2)}) collective-permute-start(f32[5,32,160]{2,1,0:T(8,128)S(1)} %bitcast.201), channel_id=1, source_target_pairs={{0,64},{64,128},{128,192},{192,0},{1,65},{65,129},{129,193},{193,1... | collective-permute-start | bytes 307208 | tf_op jit(solution)/shard_map/ppermute | solution.py:184
  4.2 18.4 %collective-permute-start.1 = (f32[5,32,160]{2,1,0:T(8,128)S(1)}, f32[5,32,160]{2,1,0:T(8,128)S(1)}, u32[]{:S(2)}, u32[]{:S(2)}) collective-permute-start(f32[5,32,160]{2,1,0:T(8,128)S(1)} %bitcast.202), channel_id=1, source_target_pairs={{0,128},{64,192},{128,0},{192,64},{1,129},{65,193},{129,1},{193,65... | collective-permute-start | bytes 307208 | tf_op jit(solution)/shard_map/ppermute | solution.py:184
  5.6 17.1 %collective-permute-start.2 = (f32[5,32,160]{2,1,0:T(8,128)S(1)}, f32[5,32,160]{2,1,0:T(8,128)S(1)}, u32[]{:S(2)}, u32[]{:S(2)}) collective-permute-start(f32[5,32,160]{2,1,0:T(8,128)S(1)} %bitcast.203), channel_id=1, source_target_pairs={{0,192},{64,0},{128,64},{192,128},{1,193},{65,1},{129,65},{193,129... | collective-permute-start | bytes 307208 | tf_op jit(solution)/shard_map/ppermute | solution.py:184
  8.7 24.0 %copy-start.9 = (s32[32,128]{1,0:T(8,128)S(1)}, s32[32,128]{1,0:T(8,128)}, u32[]{:S(2)}) copy-start(s32[32,128]{1,0:T(8,128)} %param.14) | copy-start | bytes 49156
  8.7 36.8 %all-to-all-start = ((f32[4,256,128]{2,0,1:T(4,128)}), f32[4,256,128]{2,0,1:T(4,128)S(1)}, u32[]{:S(2)}, u32[]{:S(2)}) async-start(f32[4,256,128]{2,0,1:T(4,128)} %pad_maximum_fusion.1), calls=%async_computation | async-start | bytes 1048576 | tf_op jit(solution)/shard_map/all_to_all | solution.py:158
  22.7 10.5 %collective-permute-start.3 = (bf16[5,16,160]{2,1,0:T(8,128)(2,1)S(1)}, bf16[5,16,160]{2,1,0:T(8,128)(2,1)S(1)}, u32[]{:S(2)}, u32[]{:S(2)}) collective-permute-start(bf16[5,16,160]{2,1,0:T(8,128)(2,1)S(1)} %get-tuple-element.19), channel_id=1, source_target_pairs={{0,1},{1,2},{2,3},{3,4},{4,5},{5,6},{6,7},{7,8},{8,9},{9,10},{10,1... | collective-permute-start | bytes 76808 | tf_op jit(solution)/shard_map/ppermute | solution.py:22
  27.3 11.6 %collective-permute-start.4 = (bf16[5,16,160]{2,1,0:T(8,128)(2,1)S(1)}, bf16[5,16,160]{2,1,0:T(8,128)(2,1)S(1)}, u32[]{:S(2)}, u32[]{:S(2)}) collective-permute-start(bf16[5,16,160]{2,1,0:T(8,128)(2,1)S(1)} %get-tuple-element.20), channel_id=1, source_target_pairs={{1,0},{2,1},{3,2},{4,3},{5,4},{6,5},{7,6},{8,7},{9,8},{10,9},{11,1... | collective-permute-start | bytes 76808 | tf_op jit(solution)/shard_map/ppermute | solution.py:25
  45.5 0.8 copy-start.2
  46.3 13.2 %copy-start.4 = (f32[2,5,32,128]{3,2,1,0:T(8,128)S(1)}, f32[2,5,32,128]{3,2,1,0:T(8,128)}, u32[]{:S(2)}) copy-start(f32[2,5,32,128]{3,2,1,0:T(8,128)} %shard_map.100) | copy-start | bytes 491524
  59.7 2.7 %collective-permute-start.5 = (bf16[2,5,32,16]{3,2,1,0:T(8,128)(2,1)S(1)}, bf16[2,5,32,16]{3,2,1,0:T(8,128)(2,1)S(1)}, u32[]{:S(2)}, u32[]{:S(2)}) collective-permute-start(bf16[2,5,32,16]{3,2,1,0:T(8,128)(2,1)S(1)} %get-tuple-element.17), channel_id=1, source_target_pairs={{0,64},{64,128},{128,192},{1,65},{65,129},{129,193},{2,66},{66,130... | collective-permute-start | bytes 30728 | tf_op jit(solution)/shard_map/ppermute | solution.py:22
  61.0 5.5 %collective-permute-start.6 = (bf16[2,5,32,16]{3,2,1,0:T(8,128)(2,1)S(1)}, bf16[2,5,32,16]{3,2,1,0:T(8,128)(2,1)S(1)}, u32[]{:S(2)}, u32[]{:S(2)}) collective-permute-start(bf16[2,5,32,16]{3,2,1,0:T(8,128)(2,1)S(1)} %get-tuple-element.18), channel_id=1, source_target_pairs={{64,0},{128,64},{192,128},{65,1},{129,65},{193,129},{66,2},{130,66... | collective-permute-start | bytes 30728 | tf_op jit(solution)/shard_map/ppermute | solution.py:25
  66.6 7.1 %collective-permute-start.7 = (bf16[2,5,16,160]{3,2,1,0:T(8,128)(2,1)S(1)}, bf16[2,5,16,160]{3,2,1,0:T(8,128)(2,1)S(1)}, u32[]{:S(2)}, u32[]{:S(2)}) collective-permute-start(bf16[2,5,16,160]{3,2,1,0:T(8,128)(2,1)S(1)} %get-tuple-element.16), channel_id=1, source_target_pairs={{0,1},{1,2},{2,3},{3,4},{4,5},{5,6},{6,7},{7,8},{8,9},{9,10},{10,1... | collective-permute-start | bytes 153608 | tf_op jit(solution)/shard_map/ppermute | solution.py:22
  69.6 12.1 %collective-permute-start.8 = (bf16[2,5,16,160]{3,2,1,0:T(8,128)(2,1)S(1)}, bf16[2,5,16,160]{3,2,1,0:T(8,128)(2,1)S(1)}, u32[]{:S(2)}, u32[]{:S(2)}) collective-permute-start(bf16[2,5,16,160]{3,2,1,0:T(8,128)(2,1)S(1)} %get-tuple-element.15), channel_id=1, source_target_pairs={{1,0},{2,1},{3,2},{4,3},{5,4},{6,5},{7,6},{8,7},{9,8},{10,9},{11,1... | collective-permute-start | bytes 153608 | tf_op jit(solution)/shard_map/ppermute | solution.py:25
  83.4 9.9 %copy-start.1 = (f32[16,32,512]{2,1,0:T(8,128)S(1)}, f32[16,32,512]{2,1,0:T(8,128)}, u32[]{:S(2)}) copy-start(f32[16,32,512]{2,1,0:T(8,128)} %param.10) | copy-start | bytes 3145732
  83.4 9.9 %copy-start.11 = (f32[16]{0:T(128)S(1)}, f32[16]{0:T(128)}, u32[]{:S(2)}) copy-start(f32[16]{0:T(128)} %param.11) | copy-start | bytes 196

commit v8 on v7

--- a/solution.py
+++ b/solution.py
@@ -25,6 +25,33 @@
         high = lax.ppermute(lax.slice_in_dim(block, 0, width, axis=dim), axis, backward)
         block = jnp.concatenate([low, block, high], axis=dim)
     return block
+
+
+def neighbourhood(block, width):
+    shells = lax.axis_size("shell")
+    tiles = lax.axis_size("tile")
+    rows, cols = block.shape[-2], block.shape[-1]
+    row_parts = {-1: slice(rows - width, rows), 0: slice(0, rows), 1: slice(0, width)}
+    col_parts = {-1: slice(cols - width, cols), 0: slice(0, cols), 1: slice(0, width)}
+    pieces = {}
+    for dt in (-1, 0, 1):
+        for ds in (-1, 0, 1):
+            part = block[..., row_parts[dt], col_parts[ds]]
+            if dt == 0 and ds == 0:
+                pieces[(dt, ds)] = part
+                continue
+            pairs = [
+                (s * tiles + t, (s - ds) * tiles + (t - dt))
+                for s in range(shells)
+                for t in range(tiles)
+                if 0 <= s - ds < shells and 0 <= t - dt < tiles
+            ]
+            pieces[(dt, ds)] = lax.ppermute(part, ("shell", "tile"), pairs)
+    bands = [
+        jnp.concatenate([pieces[(dt, -1)], pieces[(dt, 0)], pieces[(dt, 1)]], axis=-1)
+        for dt in (-1, 0, 1)
+    ]
+    return jnp.concatenate(bands, axis=-2)
 
 
 def build_bands(kernel, columns):
@@ -166,13 +193,13 @@
 
     sigma = shell_sigma[:, None, None]
     growth = jnp.exp(sigma * latent - 0.5 * sigma * sigma)
-    partial_bins = jnp.einsum(
-        "bs,srw->brw",
+    shells = latent.shape[0]
+    partial_bins = jnp.dot(
         lens_weight,
-        growth - 1.0,
+        (growth - 1.0).reshape(shells, height * width),
         precision=lax.Precision.HIGHEST,
         preferred_element_type=jnp.float32,
-    )
+    ).reshape(NBIN, height, width)
     wide = jnp.pad(partial_bins, ((0, 0), (0, 0), (HALF, HALF)))
     windows = jnp.stack(
         [wide[:, :, owner * columns : owner * columns + columns + 2 * HALF] for owner in range(shell_count)]
@@ -190,7 +217,7 @@
     shear = correlate_forward(padded, forward_bands, height)
     shear_grad = shear * weight_sum[None] - shape_sum
     masked = (shear_grad * star_mask.astype(jnp.float32)).astype(jnp.bfloat16)
-    rims = extended(masked, (("shell", 3), ("tile", 2)), HALF)
+    rims = neighbourhood(masked, HALF)
     back_bands = build_bands(jnp.flip(shear_kernel, (1, 2)), columns)
     bin_grad = jnp.einsum(
         "kbdrj,kdjc->brc",
@@ -198,14 +225,23 @@
         back_bands,
         preferred_element_type=jnp.float32,
     )
-    full_grad = lax.all_gather(bin_grad, "shell", axis=2, tiled=True)
-    mixed = jnp.einsum(
-        "bs,brw->srw",
-        lens_weight,
+    received = [bin_grad]
+    for shift in range(1, shell_count):
+        received.append(
+            lax.ppermute(
+                bin_grad, "shell", [(i, (i + shift) % shell_count) for i in range(shell_count)]
+            )
+        )
+    by_offset = jnp.stack([received[(-j) % shell_count] for j in range(shell_count)])
+    twice = jnp.concatenate([by_offset, by_offset], axis=0)
+    blocks = lax.dynamic_slice_in_dim(twice, (shell_count - me) % shell_count, shell_count, 0)
+    full_grad = jnp.transpose(blocks, (1, 2, 0, 3)).reshape(NBIN, height * width)
+    mixed = jnp.dot(
+        lens_weight.T,
         full_grad,
         precision=lax.Precision.HIGHEST,
         preferred_element_type=jnp.float32,
-    )
+    ).reshape(shells, height, width)
     return sigma * growth * mixed
 
 

time: 97.7 us -> 115 us (1.18)
  the two profiles are of different devices: /device:TPU:124 before, /device:TPU:130 now
where the time goes in v8:
time: 115 us
  starting transfers between devices  62.8 us (55%)
  Pallas kernels  16.8 us (15%)
  waiting for transfers between devices  13.8 us (12%)
  local copies, waits for them, and re-layouts  9.08 us (8%)
  other arithmetic  6.2 us (5%)
  matrix products  5.28 us (5%)
    ppermute x8, starting transfers between devices, neighbourhood(): pieces[dt, ds] = lax.ppermute(part, ('shell', 'tile'), pairs)  31.9 us
    all_to_all x1, starting transfers between devices, per_device(): lax.all_to_all(packet.reshape(4, devices, -1), ('shell', 'tile'), split_a...  15.5 us
    pallas_call x1, Pallas kernels, deposit_sums(): pl.pallas_call(functools.partial(scatter_kernel, rows, columns), out_shap...  11 us
    ppermute x8, waiting for transfers between devices, neighbourhood(): pieces[dt, ds] = lax.ppermute(part, ('shell', 'tile'), pairs)  8.79 us
    ppermute x1, starting transfers between devices, extended(): lax.ppermute(lax.slice_in_dim(block, 0, width, axis=dim), axis, backward)  8.31 us
    pallas_call x1, Pallas kernels, correlate_forward(): pl.pallas_call(correlate_kernel, out_shape=jax.ShapeDtypeStruct((kinds, b...  5.86 us
    ppermute x3, waiting for transfers between devices, per_device(): lax.ppermute(bin_grad, 'shell', [(i, (i + shift) % shell_count) for i in...  5.03 us
    ppermute x1, starting transfers between devices, extended(): lax.ppermute(lax.slice_in_dim(block, block.shape[dim] - width, None, axis...  3.43 us
  transfers between devices with their start and end apart: 17, of which 4 were waited for; matrix products, arithmetic and copies ran while one was open for 6% of the time, Pallas kernels for 5%

profile of v8, /device:TPU:130, one launch (start us, length us, event | category | flops | bytes accessed | tf_op | source)
XLA Modules:
  0.0 114.8 jit_solution(17383817366266806451)
XLA Ops:
  0.8 1.5 %fusion.10 = f32[16,32,512]{2,1,0:T(8,128)S(1)} fusion(f32[16,32,512]{2,1,0:T(8,128)} %param.10, f32[16]{0:T(128)S(1)} %multiply_multiply_fusion, f32[16]{0:T(128)} %param.11), kind=kLoop, calls=%fused_computation.11 | loop fusion | flops 786432 | bytes 2097280 | tf_op jit(solution)/shard_map/sub | solution.py:199
  4.9 1.4 %collective-permute-start.2 = (f32[5,32,160]{2,1,0:T(8,128)S(1)}, f32[5,32,160]{2,1,0:T(8,128)S(1)}, u32[]{:S(2)}, u32[]{:S(2)}) collective-permute-start(f32[5,32,160]{2,1,0:T(8,128)S(1)} %get-tuple-element.6), channel_id=1, source_target_pairs={{0,192},{64,0},{128,64},{192,128},{1,193},{65,1},{129,65},{193,129... | collective-permute-start | bytes 307208 | tf_op jit(solution)/shard_map/ppermute | solution.py:211
  6.8 1.1 pad_maximum_fusion.1
  8.0 15.5 %all-to-all-start = ((f32[4,256,128]{2,0,1:T(4,128)}), f32[4,256,128]{2,0,1:T(4,128)}, u32[]{:S(2)}, u32[]{:S(2)}) async-start(f32[4,256,128]{2,0,1:T(4,128)} %pad_maximum_fusion.1), calls=%async_computation | async-start | bytes 1048576 | tf_op jit(solution)/shard_map/all_to_all | solution.py:185
  24.1 3.4 %collective-permute-start.3 = (bf16[5,16,160]{2,1,0:T(8,128)(2,1)}, bf16[5,16,160]{2,1,0:T(8,128)(2,1)S(1)}, u32[]{:S(2)}, u32[]{:S(2)}) collective-permute-start(bf16[5,16,160]{2,1,0:T(8,128)(2,1)} %get-tuple-element.22), channel_id=1, source_target_pairs={{0,1},{1,2},{2,3},{3,4},{4,5},{5,6},{6,7},{7,8},{8,9},{9,10},{10,1... | collective-permute-start | bytes 76808 | tf_op jit(solution)/shard_map/ppermute | solution.py:22
  27.6 8.3 %collective-permute-start.4 = (bf16[5,16,160]{2,1,0:T(8,128)(2,1)S(1)}, bf16[5,16,160]{2,1,0:T(8,128)(2,1)S(1)}, u32[]{:S(2)}, u32[]{:S(2)}) collective-permute-start(bf16[5,16,160]{2,1,0:T(8,128)(2,1)S(1)} %get-tuple-element.23), channel_id=1, source_target_pairs={{1,0},{2,1},{3,2},{4,3},{5,4},{6,5},{7,6},{8,7},{9,8},{10,9},{11,1... | collective-permute-start | bytes 76808 | tf_op jit(solution)/shard_map/ppermute | solution.py:25
  37.1 2.2 %copy.48 = bf16[160,128,2,33]{1,0,3,2:T(8,128)(2,1)} copy(bf16[160,128,2,33]{1,3,2,0:T(8,128)(2,1)S(1)} %fusion.3) | data formatting | bytes 5406720 | tf_op jit(solution)/shard_map/kdv,vjc->kdjc/dot_general | solution.py:64
  40.0 5.9 %shard_map.100 = f32[2,5,32,128]{3,2,1,0:T(8,128)} custom-call(bf16[5,64,160]{2,1,0:T(8,128)(2,1)} %pad_maximum_fusion.2.x_ref, bf16[2,33,160,128]{3,2,1,0:T(8,128)(2,1)} %bitcast.217), custom_call_target="tpu_custom_call" | custom-call | flops 865075200 | bytes 2969600 | tf_op jit(solution)/shard_map/pallas_call | solution.py:145
  45.9 11.0 %shard_map.101 = f32[3,256,80]{2,1,0:T(8,128)} custom-call(f32[4,32768]{1,0:T(4,128)} %bitcast.16.packet_ref), custom_call_target="tpu_custom_call" | custom-call | flops 8053063680 | bytes 770048 | tf_op jit(solution)/shard_map/pallas_call | solution.py:116
  59.3 6.3 %collective-permute-start.10 = (bf16[2,5,16,16]{3,2,1,0:T(8,128)(2,1)S(1)}, bf16[2,5,16,16]{3,2,1,0:T(8,128)(2,1)S(1)}, u32[]{:S(2)}, u32[]{:S(2)}) collective-permute-start(bf16[2,5,16,16]{3,2,1,0:T(8,128)(2,1)S(1)} %get-tuple-element.14), channel_id=1, source_target_pairs={{1,64},{2,65},{3,66},{4,67},{5,68},{6,69},{7,70},{8,71},{9,72},{10... | collective-permute-start | bytes 15368 | tf_op jit(solution)/shard_map/ppermute | solution.py:49
  65.6 1.9 %collective-permute-start.12 = (bf16[2,5,16,16]{3,2,1,0:T(8,128)(2,1)S(1)}, bf16[2,5,16,16]{3,2,1,0:T(8,128)(2,1)S(1)}, u32[]{:S(2)}, u32[]{:S(2)}) collective-permute-start(bf16[2,5,16,16]{3,2,1,0:T(8,128)(2,1)S(1)} %get-tuple-element.15), channel_id=1, source_target_pairs={{65,0},{66,1},{67,2},{68,3},{69,4},{70,5},{71,6},{72,7},{73,8},{74... | collective-permute-start | bytes 15368 | tf_op jit(solution)/shard_map/ppermute | solution.py:49
  67.6 3.6 %collective-permute-start.5 = (bf16[2,5,16,16]{3,2,1,0:T(8,128)(2,1)S(1)}, bf16[2,5,16,16]{3,2,1,0:T(8,128)(2,1)S(1)}, u32[]{:S(2)}, u32[]{:S(2)}) collective-permute-start(bf16[2,5,16,16]{3,2,1,0:T(8,128)(2,1)S(1)} %get-tuple-element.17), channel_id=1, source_target_pairs={{0,65},{1,66},{2,67},{3,68},{4,69},{5,70},{6,71},{7,72},{8,73},{9,... | collective-permute-start | bytes 15368 | tf_op jit(solution)/shard_map/ppermute | solution.py:49
  71.2 1.9 %collective-permute-start.8 = (bf16[2,5,32,16]{3,2,1,0:T(8,128)(2,1)S(1)}, bf16[2,5,32,16]{3,2,1,0:T(8,128)(2,1)S(1)}, u32[]{:S(2)}, u32[]{:S(2)}) collective-permute-start(bf16[2,5,32,16]{3,2,1,0:T(8,128)(2,1)S(1)} %get-tuple-element.20), channel_id=1, source_target_pairs={{0,64},{1,65},{2,66},{3,67},{4,68},{5,69},{6,70},{7,71},{8,72},{9,... | collective-permute-start | bytes 30728 | tf_op jit(solution)/shard_map/ppermute | solution.py:49
  73.2 5.4 %collective-permute-start.9 = (bf16[2,5,32,16]{3,2,1,0:T(8,128)(2,1)S(1)}, bf16[2,5,32,16]{3,2,1,0:T(8,128)(2,1)S(1)}, u32[]{:S(2)}, u32[]{:S(2)}) collective-permute-start(bf16[2,5,32,16]{3,2,1,0:T(8,128)(2,1)S(1)} %get-tuple-element.21), channel_id=1, source_target_pairs={{64,0},{65,1},{66,2},{67,3},{68,4},{69,5},{70,6},{71,7},{72,8},{73... | collective-permute-start | bytes 30728 | tf_op jit(solution)/shard_map/ppermute | solution.py:49
  78.6 1.9 %collective-permute-start.7 = (bf16[2,5,16,16]{3,2,1,0:T(8,128)(2,1)S(1)}, bf16[2,5,16,16]{3,2,1,0:T(8,128)(2,1)S(1)}, u32[]{:S(2)}, u32[]{:S(2)}) collective-permute-start(bf16[2,5,16,16]{3,2,1,0:T(8,128)(2,1)S(1)} %get-tuple-element.16), channel_id=1, source_target_pairs={{64,1},{65,2},{66,3},{67,4},{68,5},{69,6},{70,7},{71,8},{72,9},{73... | collective-permute-start | bytes 15368 | tf_op jit(solution)/shard_map/ppermute | solution.py:49
  80.5 8.7 %collective-permute-start.11 = (bf16[2,5,16,128]{3,2,1,0:T(8,128)(2,1)S(1)}, bf16[2,5,16,128]{3,2,1,0:T(8,128)(2,1)S(1)}, u32[]{:S(2)}, u32[]{:S(2)}) collective-permute-start(bf16[2,5,16,128]{3,2,1,0:T(8,128)(2,1)S(1)} %get-tuple-element.18), channel_id=1, source_target_pairs={{1,0},{2,1},{3,2},{4,3},{5,4},{6,5},{7,6},{8,7},{9,8},{10,9},{11,1... | collective-permute-start | bytes 122888 | tf_op jit(solution)/shard_map/ppermute | solution.py:49
  89.2 2.1 %collective-permute-start.6 = (bf16[2,5,16,128]{3,2,1,0:T(8,128)(2,1)S(1)}, bf16[2,5,16,128]{3,2,1,0:T(8,128)(2,1)S(1)}, u32[]{:S(2)}, u32[]{:S(2)}) collective-permute-start(bf16[2,5,16,128]{3,2,1,0:T(8,128)(2,1)S(1)} %get-tuple-element.19), channel_id=1, source_target_pairs={{0,1},{1,2},{2,3},{3,4},{4,5},{5,6},{6,7},{7,8},{8,9},{9,10},{10,1... | collective-permute-start | bytes 122888 | tf_op jit(solution)/shard_map/ppermute | solution.py:49
  92.4 8.8 %collective-permute-done.6 = bf16[2,5,16,128]{3,2,1,0:T(8,128)(2,1)S(1)} collective-permute-done((bf16[2,5,16,128]{3,2,1,0:T(8,128)(2,1)S(1)}, bf16[2,5,16,128]{3,2,1,0:T(8,128)(2,1)S(1)}, u32[]{:S(2)}, u32[]{:S(2)}) %collective-permute-start.6) | collective-permute-done | bytes 40992 | tf_op jit(solution)/shard_map/ppermute | solution.py:49
  103.2 1.6 %constant_dynamic-update-slice_fusion.7 = (f32[8,5,32,128]{3,2,1,0:T(8,128)S(1)}, f32[5,32,128,1,1]{2,1,0,4,3:T(8,128)S(1)}) fusion(bf16[2,5,33,32,160]{4,3,1,0,2:T(8,128)(2,1)S(1)} %fusion.13, bf16[2,33,160,128,1]{3,1,0,2,4:T(8,128)(2,1)S(1)} %convert_bitcast_fusion), kind=kOutput, calls=%fused_computation.110 | convolution fusion | flops 432537600 | bytes 6246400 | tf_op jit(solution)/shard_map/kbdrj,kdjc->brc/dot_general | solution.py:222
  104.9 1.4 %collective-permute-start.14 = (f32[5,32,128]{2,1,0:T(8,128)S(1)}, f32[5,32,128]{2,1,0:T(8,128)S(1)}, u32[]{:S(2)}, u32[]{:S(2)}) collective-permute-start(f32[5,32,128]{2,1,0:T(8,128)S(1)} %bitcast.223), channel_id=1, source_target_pairs={{0,128},{64,192},{128,0},{192,64},{1,129},{65,193},{129,1},{193,65... | collective-permute-start | bytes 245768 | tf_op jit(solution)/shard_map/ppermute | solution.py:231
  106.4 1.2 %collective-permute-done.13 = f32[5,32,128]{2,1,0:T(8,128)S(1)} collective-permute-done((f32[5,32,128]{2,1,0:T(8,128)S(1)}, f32[5,32,128]{2,1,0:T(8,128)S(1)}, u32[]{:S(2)}, u32[]{:S(2)}) %collective-permute-start.13) | collective-permute-done | bytes 81952 | tf_op jit(solution)/shard_map/ppermute | solution.py:231
  107.6 3.8 %collective-permute-done.14 = f32[5,32,128]{2,1,0:T(8,128)S(1)} collective-permute-done((f32[5,32,128]{2,1,0:T(8,128)S(1)}, f32[5,32,128]{2,1,0:T(8,128)S(1)}, u32[]{:S(2)}, u32[]{:S(2)}) %collective-permute-start.14) | collective-permute-done | bytes 81952 | tf_op jit(solution)/shard_map/ppermute | solution.py:231
  111.9 1.0 fusion.59
  113.6 1.3 %bitcast_multiply_fusion = f32[16,32,512]{2,1,0:T(8,128)} fusion(f32[2,8,32,512]{3,2,1,0:T(8,128)S(1)} %copy.31, f32[16,32,512]{2,1,0:T(8,128)S(1)} %copy-done.1, f32[16]{0:T(128)S(1)} %multiply_multiply_fusion, f32[16]{0:T(128)S(1)} %copy-done.10), kind=kLoop, calls=%fused_computation.9 | loop fusion | flops 1048576 | bytes 3145856 | tf_op jit(solution)/shard_map/mul | solution.py:245
  (111 shorter events, 12.7 us)
Async XLA Ops:
  0.0 6.3 %copy-start.9 = (s32[4,64]{1,0:T(4,128)S(1)}, s32[4,64]{1,0:T(4,128)}, u32[]{:S(2)}) copy-start(s32[4,64]{1,0:T(4,128)} %param.19) | copy-start | bytes 3076
  0.0 6.4 %copy-start.2 = (f32[2,4,64,128]{3,2,1,0:T(8,128)S(1)}, f32[2,4,64,128]{3,2,1,0:T(8,128)}, u32[]{:S(2)}) copy-start(f32[2,4,64,128]{3,2,1,0:T(8,128)} %param.17) | copy-start | bytes 786436
  3.0 32.9 %copy-start.7 = (bf16[2,33,33]{2,0,1:T(2,128)(2,1)S(1)}, bf16[2,33,33]{2,0,1:T(2,128)(2,1)}, u32[]{:S(2)}) copy-start(bf16[2,33,33]{2,0,1:T(2,128)(2,1)} %param.13) | copy-start | bytes 13072
  4.2 19.2 %collective-permute-start = (f32[5,32,160]{2,1,0:T(8,128)S(1)}, f32[5,32,160]{2,1,0:T(8,128)S(1)}, u32[]{:S(2)}, u32[]{:S(2)}) collective-permute-start(f32[5,32,160]{2,1,0:T(8,128)S(1)} %get-tuple-element.5), channel_id=1, source_target_pairs={{0,64},{64,128},{128,192},{192,0},{1,65},{65,129},{129,193},{193,1... | collective-permute-start | bytes 307208 | tf_op jit(solution)/shard_map/ppermute | solution.py:211
  4.3 19.1 %collective-permute-start.1 = (f32[5,32,160]{2,1,0:T(8,128)S(1)}, f32[5,32,160]{2,1,0:T(8,128)S(1)}, u32[]{:S(2)}, u32[]{:S(2)}) collective-permute-start(f32[5,32,160]{2,1,0:T(8,128)S(1)} %get-tuple-element.7), channel_id=1, source_target_pairs={{0,128},{64,192},{128,0},{192,64},{1,129},{65,193},{129,1},{193,65... | collective-permute-start | bytes 307208 | tf_op jit(solution)/shard_map/ppermute | solution.py:211
  4.9 18.5 %collective-permute-start.2 = (f32[5,32,160]{2,1,0:T(8,128)S(1)}, f32[5,32,160]{2,1,0:T(8,128)S(1)}, u32[]{:S(2)}, u32[]{:S(2)}) collective-permute-start(f32[5,32,160]{2,1,0:T(8,128)S(1)} %get-tuple-element.6), channel_id=1, source_target_pairs={{0,192},{64,0},{128,64},{192,128},{1,193},{65,1},{129,65},{193,129... | collective-permute-start | bytes 307208 | tf_op jit(solution)/shard_map/ppermute | solution.py:211
  8.0 31.3 %copy-start.8 = (s32[32,128]{1,0:T(8,128)S(1)}, s32[32,128]{1,0:T(8,128)}, u32[]{:S(2)}) copy-start(s32[32,128]{1,0:T(8,128)} %param.14) | copy-start | bytes 49156
  8.0 37.9 %all-to-all-start = ((f32[4,256,128]{2,0,1:T(4,128)}), f32[4,256,128]{2,0,1:T(4,128)}, u32[]{:S(2)}, u32[]{:S(2)}) async-start(f32[4,256,128]{2,0,1:T(4,128)} %pad_maximum_fusion.1), calls=%async_computation | async-start | bytes 1048576 | tf_op jit(solution)/shard_map/all_to_all | solution.py:185
  24.1 15.1 %collective-permute-start.3 = (bf16[5,16,160]{2,1,0:T(8,128)(2,1)}, bf16[5,16,160]{2,1,0:T(8,128)(2,1)S(1)}, u32[]{:S(2)}, u32[]{:S(2)}) collective-permute-start(bf16[5,16,160]{2,1,0:T(8,128)(2,1)} %get-tuple-element.22), channel_id=1, source_target_pairs={{0,1},{1,2},{2,3},{3,4},{4,5},{5,6},{6,7},{7,8},{8,9},{9,10},{10,1... | collective-permute-start | bytes 76808 | tf_op jit(solution)/shard_map/ppermute | solution.py:22
  27.6 11.7 %collective-permute-start.4 = (bf16[5,16,160]{2,1,0:T(8,128)(2,1)S(1)}, bf16[5,16,160]{2,1,0:T(8,128)(2,1)S(1)}, u32[]{:S(2)}, u32[]{:S(2)}) collective-permute-start(bf16[5,16,160]{2,1,0:T(8,128)(2,1)S(1)} %get-tuple-element.23), channel_id=1, source_target_pairs={{1,0},{2,1},{3,2},{4,3},{5,4},{6,5},{7,6},{8,7},{9,8},{10,9},{11,1... | collective-permute-start | bytes 76808 | tf_op jit(solution)/shard_map/ppermute | solution.py:25
  45.9 13.2 %copy-start.3 = (f32[2,5,32,128]{3,2,1,0:T(8,128)S(1)}, f32[2,5,32,128]{3,2,1,0:T(8,128)}, u32[]{:S(2)}) copy-start(f32[2,5,32,128]{3,2,1,0:T(8,128)} %shard_map.100) | copy-start | bytes 491524
  59.3 19.3 %collective-permute-start.10 = (bf16[2,5,16,16]{3,2,1,0:T(8,128)(2,1)S(1)}, bf16[2,5,16,16]{3,2,1,0:T(8,128)(2,1)S(1)}, u32[]{:S(2)}, u32[]{:S(2)}) collective-permute-start(bf16[2,5,16,16]{3,2,1,0:T(8,128)(2,1)S(1)} %get-tuple-element.14), channel_id=1, source_target_pairs={{1,64},{2,65},{3,66},{4,67},{5,68},{6,69},{7,70},{8,71},{9,72},{10... | collective-permute-start | bytes 15368 | tf_op jit(solution)/shard_map/ppermute | solution.py:49
  65.6 14.9 %collective-permute-start.12 = (bf16[2,5,16,16]{3,2,1,0:T(8,128)(2,1)S(1)}, bf16[2,5,16,16]{3,2,1,0:T(8,128)(2,1)S(1)}, u32[]{:S(2)}, u32[]{:S(2)}) collective-permute-start(bf16[2,5,16,16]{3,2,1,0:T(8,128)(2,1)S(1)} %get-tuple-element.15), channel_id=1, source_target_pairs={{65,0},{66,1},{67,2},{68,3},{69,4},{70,5},{71,6},{72,7},{73,8},{74... | collective-permute-start | bytes 15368 | tf_op jit(solution)/shard_map/ppermute | solution.py:49
  67.6 21.6 %collective-permute-start.5 = (bf16[2,5,16,16]{3,2,1,0:T(8,128)(2,1)S(1)}, bf16[2,5,16,16]{3,2,1,0:T(8,128)(2,1)S(1)}, u32[]{:S(2)}, u32[]{:S(2)}) collective-permute-start(bf16[2,5,16,16]{3,2,1,0:T(8,128)(2,1)S(1)} %get-tuple-element.17), channel_id=1, source_target_pairs={{0,65},{1,66},{2,67},{3,68},{4,69},{5,70},{6,71},{7,72},{8,73},{9,... | collective-permute-start | bytes 15368 | tf_op jit(solution)/shard_map/ppermute | solution.py:49
  71.2 21.2 %collective-permute-start.8 = (bf16[2,5,32,16]{3,2,1,0:T(8,128)(2,1)S(1)}, bf16[2,5,32,16]{3,2,1,0:T(8,128)(2,1)S(1)}, u32[]{:S(2)}, u32[]{:S(2)}) collective-permute-start(bf16[2,5,32,16]{3,2,1,0:T(8,128)(2,1)S(1)} %get-tuple-element.20), channel_id=1, source_target_pairs={{0,64},{1,65},{2,66},{3,67},{4,68},{5,69},{6,70},{7,71},{8,72},{9,... | collective-permute-start | bytes 30728 | tf_op jit(solution)/shard_map/ppermute | solution.py:49
  73.2 19.2 %collective-permute-start.9 = (bf16[2,5,32,16]{3,2,1,0:T(8,128)(2,1)S(1)}, bf16[2,5,32,16]{3,2,1,0:T(8,128)(2,1)S(1)}, u32[]{:S(2)}, u32[]{:S(2)}) collective-permute-start(bf16[2,5,32,16]{3,2,1,0:T(8,128)(2,1)S(1)} %get-tuple-element.21), channel_id=1, source_target_pairs={{64,0},{65,1},{66,2},{67,3},{68,4},{69,5},{70,6},{71,7},{72,8},{73... | collective-permute-start | bytes 30728 | tf_op jit(solution)/shard_map/ppermute | solution.py:49
  78.6 13.8 %collective-permute-start.7 = (bf16[2,5,16,16]{3,2,1,0:T(8,128)(2,1)S(1)}, bf16[2,5,16,16]{3,2,1,0:T(8,128)(2,1)S(1)}, u32[]{:S(2)}, u32[]{:S(2)}) collective-permute-start(bf16[2,5,16,16]{3,2,1,0:T(8,128)(2,1)S(1)} %get-tuple-element.16), channel_id=1, source_target_pairs={{64,1},{65,2},{66,3},{67,4},{68,5},{69,6},{70,7},{71,8},{72,9},{73... | collective-permute-start | bytes 15368 | tf_op jit(solution)/shard_map/ppermute | solution.py:49
  80.5 11.9 %collective-permute-start.11 = (bf16[2,5,16,128]{3,2,1,0:T(8,128)(2,1)S(1)}, bf16[2,5,16,128]{3,2,1,0:T(8,128)(2,1)S(1)}, u32[]{:S(2)}, u32[]{:S(2)}) collective-permute-start(bf16[2,5,16,128]{3,2,1,0:T(8,128)(2,1)S(1)} %get-tuple-element.18), channel_id=1, source_target_pairs={{1,0},{2,1},{3,2},{4,3},{5,4},{6,5},{7,6},{8,7},{9,8},{10,9},{11,1... | collective-permute-start | bytes 122888 | tf_op jit(solution)/shard_map/ppermute | solution.py:49
  89.2 12.0 %collective-permute-start.6 = (bf16[2,5,16,128]{3,2,1,0:T(8,128)(2,1)S(1)}, bf16[2,5,16,128]{3,2,1,0:T(8,128)(2,1)S(1)}, u32[]{:S(2)}, u32[]{:S(2)}) collective-permute-start(bf16[2,5,16,128]{3,2,1,0:T(8,128)(2,1)S(1)} %get-tuple-element.19), channel_id=1, source_target_pairs={{0,1},{1,2},{2,3},{3,4},{4,5},{5,6},{6,7},{7,8},{8,9},{9,10},{10,1... | collective-permute-start | bytes 122888 | tf_op jit(solution)/shard_map/ppermute | solution.py:49
  104.8 8.8 %copy-start.1 = (f32[16,32,512]{2,1,0:T(8,128)S(1)}, f32[16,32,512]{2,1,0:T(8,128)}, u32[]{:S(2)}) copy-start(f32[16,32,512]{2,1,0:T(8,128)} %param.10) | copy-start | bytes 3145732
  104.8 8.8 %copy-start.10 = (f32[16]{0:T(128)S(1)}, f32[16]{0:T(128)}, u32[]{:S(2)}) copy-start(f32[16]{0:T(128)} %param.11) | copy-start | bytes 196
  104.8 2.7 %collective-permute-start.13 = (f32[5,32,128]{2,1,0:T(8,128)S(1)}, f32[5,32,128]{2,1,0:T(8,128)S(1)}, u32[]{:S(2)}, u32[]{:S(2)}) collective-permute-start(f32[5,32,128]{2,1,0:T(8,128)S(1)} %bitcast.222), channel_id=1, source_target_pairs={{0,192},{64,0},{128,64},{192,128},{1,193},{65,1},{129,65},{193,129... | collective-permute-start | bytes 245768 | tf_op jit(solution)/shard_map/ppermute | solution.py:231
  104.9 6.4 %collective-permute-start.14 = (f32[5,32,128]{2,1,0:T(8,128)S(1)}, f32[5,32,128]{2,1,0:T(8,128)S(1)}, u32[]{:S(2)}, u32[]{:S(2)}) collective-permute-start(f32[5,32,128]{2,1,0:T(8,128)S(1)} %bitcast.223), channel_id=1, source_target_pairs={{0,128},{64,192},{128,0},{192,64},{1,129},{65,193},{129,1},{193,65... | collective-permute-start | bytes 245768 | tf_op jit(solution)/shard_map/ppermute | solution.py:231
  106.4 5.0 %collective-permute-start.15 = (f32[5,32,128]{2,1,0:T(8,128)S(1)}, f32[5,32,128]{2,1,0:T(8,128)S(1)}, u32[]{:S(2)}, u32[]{:S(2)}) collective-permute-start(f32[5,32,128]{2,1,0:T(8,128)S(1)} %bitcast.224), channel_id=1, source_target_pairs={{0,64},{64,128},{128,192},{192,0},{1,65},{65,129},{129,193},{193,1... | collective-permute-start | bytes 245768 | tf_op jit(solution)/shard_map/ppermute | solution.py:231
  (4 other events, 21.0 us)

commit v9 on v8

--- a/solution.py
+++ b/solution.py
@@ -25,33 +25,6 @@
         high = lax.ppermute(lax.slice_in_dim(block, 0, width, axis=dim), axis, backward)
         block = jnp.concatenate([low, block, high], axis=dim)
     return block
-
-
-def neighbourhood(block, width):
-    shells = lax.axis_size("shell")
-    tiles = lax.axis_size("tile")
-    rows, cols = block.shape[-2], block.shape[-1]
-    row_parts = {-1: slice(rows - width, rows), 0: slice(0, rows), 1: slice(0, width)}
-    col_parts = {-1: slice(cols - width, cols), 0: slice(0, cols), 1: slice(0, width)}
-    pieces = {}
-    for dt in (-1, 0, 1):
-        for ds in (-1, 0, 1):
-            part = block[..., row_parts[dt], col_parts[ds]]
-            if dt == 0 and ds == 0:
-                pieces[(dt, ds)] = part
-                continue
-            pairs = [
-                (s * tiles + t, (s - ds) * tiles + (t - dt))
-                for s in range(shells)
-                for t in range(tiles)
-                if 0 <= s - ds < shells and 0 <= t - dt < tiles
-            ]
-            pieces[(dt, ds)] = lax.ppermute(part, ("shell", "tile"), pairs)
-    bands = [
-        jnp.concatenate([pieces[(dt, -1)], pieces[(dt, 0)], pieces[(dt, 1)]], axis=-1)
-        for dt in (-1, 0, 1)
-    ]
-    return jnp.concatenate(bands, axis=-2)
 
 
 def build_bands(kernel, columns):
@@ -195,7 +168,7 @@
     growth = jnp.exp(sigma * latent - 0.5 * sigma * sigma)
     shells = latent.shape[0]
     partial_bins = jnp.dot(
-        lens_weight,
+    lens_weight,
         (growth - 1.0).reshape(shells, height * width),
         precision=lax.Precision.HIGHEST,
         preferred_element_type=jnp.float32,
@@ -217,7 +190,7 @@
     shear = correlate_forward(padded, forward_bands, height)
     shear_grad = shear * weight_sum[None] - shape_sum
     masked = (shear_grad * star_mask.astype(jnp.float32)).astype(jnp.bfloat16)
-    rims = neighbourhood(masked, HALF)
+    rims = extended(masked, (("shell", 3), ("tile", 2)), HALF)
     back_bands = build_bands(jnp.flip(shear_kernel, (1, 2)), columns)
     bin_grad = jnp.einsum(
         "kbdrj,kdjc->brc",

time: 115 us -> 97.5 us (0.85)
  the two profiles are of different devices: /device:TPU:130 before, /device:TPU:124 now
where the time goes in v9:
time: 97.5 us; the launch traced here: 97 us
  starting transfers between devices  35.8 us (37%)
  waiting for transfers between devices  22.8 us (23%)
  Pallas kernels  16.9 us (17%)
  local copies, waits for them, and re-layouts  9.18 us (9%)
  other arithmetic  6.22 us (6%)
  matrix products  5.33 us (5%)
    ppermute x3, waiting for transfers between devices, extended(): lax.ppermute(lax.slice_in_dim(block, 0, width, axis=dim), axis, backward)  17.6 us
    all_to_all x1, starting transfers between devices, per_device(): lax.all_to_all(packet.reshape(4, devices, -1), ('shell', 'tile'), split_a...  13.9 us
    pallas_call x1, Pallas kernels, deposit_sums(): pl.pallas_call(functools.partial(scatter_kernel, rows, columns), out_shap...  11 us
    ppermute x3, starting transfers between devices, extended(): lax.ppermute(lax.slice_in_dim(block, block.shape[dim] - width, None, axis...  8.87 us
    ppermute x3, starting transfers between devices, extended(): lax.ppermute(lax.slice_in_dim(block, 0, width, axis=dim), axis, backward)  6.49 us
    pallas_call x1, Pallas kernels, correlate_forward(): pl.pallas_call(correlate_kernel, out_shape=jax.ShapeDtypeStruct((kinds, b...  5.87 us
    ppermute x3, waiting for transfers between devices, per_device(): lax.ppermute(bin_grad, 'shell', [(i, (i + shift) % shell_count) for i in...  4.63 us
    ppermute x3, starting transfers between devices, per_device(): lax.ppermute(bin_grad, 'shell', [(i, (i + shift) % shell_count) for i in...  3.8 us
  transfers between devices with their start and end apart: 13, of which 5 were waited for; matrix products, arithmetic and copies ran while one was open for 7% of the time, Pallas kernels for 6%

profile of v9, /device:TPU:124, one launch (start us, length us, event | category | flops | bytes accessed | tf_op | source)
XLA Modules:
  0.0 97.0 jit_solution(7766898182463106545)
XLA Ops:
  0.8 1.5 %fusion.10 = f32[16,32,512]{2,1,0:T(8,128)S(1)} fusion(f32[16,32,512]{2,1,0:T(8,128)} %param.10, f32[16]{0:T(128)S(1)} %multiply_multiply_fusion, f32[16]{0:T(128)} %param.11), kind=kLoop, calls=%fused_computation.11 | loop fusion | flops 786432 | bytes 2097280 | tf_op jit(solution)/shard_map/sub | solution.py:172
  4.3 1.3 %collective-permute-start.1 = (f32[5,32,160]{2,1,0:T(8,128)S(1)}, f32[5,32,160]{2,1,0:T(8,128)S(1)}, u32[]{:S(2)}, u32[]{:S(2)}) collective-permute-start(f32[5,32,160]{2,1,0:T(8,128)S(1)} %get-tuple-element.7), channel_id=1, source_target_pairs={{0,128},{64,192},{128,0},{192,64},{1,129},{65,193},{129,1},{193,65... | collective-permute-start | bytes 307208 | tf_op jit(solution)/shard_map/ppermute | solution.py:184
  5.6 1.4 %collective-permute-start.2 = (f32[5,32,160]{2,1,0:T(8,128)S(1)}, f32[5,32,160]{2,1,0:T(8,128)S(1)}, u32[]{:S(2)}, u32[]{:S(2)}) collective-permute-start(f32[5,32,160]{2,1,0:T(8,128)S(1)} %get-tuple-element.6), channel_id=1, source_target_pairs={{0,192},{64,0},{128,64},{192,128},{1,193},{65,1},{129,65},{193,129... | collective-permute-start | bytes 307208 | tf_op jit(solution)/shard_map/ppermute | solution.py:184
  7.5 1.1 %pad_maximum_fusion.1 = f32[4,256,128]{2,0,1:T(4,128)} fusion(f32[2,256,128]{2,0,1:T(2,128)S(1)} %bitcast.218, f32[1,256,128]{2,0,1:T(1,128)S(1)} %bitcast.217, f32[1,256,128]{2,0,1:T(1,128)S(1)} %bitcast.220), kind=kLoop, calls=%fused_computation.13 | loop fusion | flops 262144 | bytes 1048576 | tf_op jit(solution)/shard_map/concatenate | solution.py:154
  8.6 13.9 %all-to-all-start = ((f32[4,256,128]{2,0,1:T(4,128)}), f32[4,256,128]{2,0,1:T(4,128)S(1)}, u32[]{:S(2)}, u32[]{:S(2)}) async-start(f32[4,256,128]{2,0,1:T(4,128)} %pad_maximum_fusion.1), calls=%async_computation | async-start | bytes 1048576 | tf_op jit(solution)/shard_map/all_to_all | solution.py:158
  22.6 4.6 %collective-permute-start.3 = (bf16[5,16,160]{2,1,0:T(8,128)(2,1)S(1)}, bf16[5,16,160]{2,1,0:T(8,128)(2,1)S(1)}, u32[]{:S(2)}, u32[]{:S(2)}) collective-permute-start(bf16[5,16,160]{2,1,0:T(8,128)(2,1)S(1)} %get-tuple-element.18), channel_id=1, source_target_pairs={{0,1},{1,2},{2,3},{3,4},{4,5},{5,6},{6,7},{7,8},{8,9},{9,10},{10,1... | collective-permute-start | bytes 76808 | tf_op jit(solution)/shard_map/ppermute | solution.py:22
  27.2 2.1 %collective-permute-start.4 = (bf16[5,16,160]{2,1,0:T(8,128)(2,1)S(1)}, bf16[5,16,160]{2,1,0:T(8,128)(2,1)S(1)}, u32[]{:S(2)}, u32[]{:S(2)}) collective-permute-start(bf16[5,16,160]{2,1,0:T(8,128)(2,1)S(1)} %get-tuple-element.19), channel_id=1, source_target_pairs={{1,0},{2,1},{3,2},{4,3},{5,4},{6,5},{7,6},{8,7},{9,8},{10,9},{11,1... | collective-permute-start | bytes 76808 | tf_op jit(solution)/shard_map/ppermute | solution.py:25
  29.3 1.0 %fusion.3 = bf16[160,128,2,33]{1,3,2,0:T(8,128)(2,1)S(1)} fusion(bf16[2,33,33]{2,0,1:T(2,128)(2,1)S(1)} %copy-done.8), kind=kOutput, calls=%fused_computation.5 | convolution fusion | flops 90562560 | bytes 2707716 | tf_op jit(solution)/shard_map/kdv,vjc->kdjc/dot_general | solution.py:37
  30.3 2.2 %copy.48 = bf16[160,128,2,33]{1,0,3,2:T(8,128)(2,1)} copy(bf16[160,128,2,33]{1,3,2,0:T(8,128)(2,1)S(1)} %fusion.3) | data formatting | bytes 5406720 | tf_op jit(solution)/shard_map/kdv,vjc->kdjc/dot_general | solution.py:37
  33.1 5.7 %collective-permute-done.4 = bf16[5,16,160]{2,1,0:T(8,128)(2,1)S(1)} collective-permute-done((bf16[5,16,160]{2,1,0:T(8,128)(2,1)S(1)}, bf16[5,16,160]{2,1,0:T(8,128)(2,1)S(1)}, u32[]{:S(2)}, u32[]{:S(2)}) %collective-permute-start.4) | collective-permute-done | bytes 25632 | tf_op jit(solution)/shard_map/ppermute | solution.py:25
  39.5 5.9 %shard_map.100 = f32[2,5,32,128]{3,2,1,0:T(8,128)} custom-call(bf16[5,64,160]{2,1,0:T(8,128)(2,1)} %pad_maximum_fusion.3.x_ref, bf16[2,33,160,128]{3,2,1,0:T(8,128)(2,1)} %bitcast.215), custom_call_target="tpu_custom_call" | custom-call | flops 865075200 | bytes 2969600 | tf_op jit(solution)/shard_map/pallas_call | solution.py:118
  46.2 11.0 %shard_map.101 = f32[3,256,80]{2,1,0:T(8,128)} custom-call(f32[4,32768]{1,0:T(4,128)} %bitcast.219), custom_call_target="tpu_custom_call" | custom-call | flops 8053063680 | bytes 770048 | tf_op jit(solution)/shard_map/pallas_call | solution.py:89
  59.6 1.3 %collective-permute-start.5 = (bf16[2,5,32,16]{3,2,1,0:T(8,128)(2,1)S(1)}, bf16[2,5,32,16]{3,2,1,0:T(8,128)(2,1)S(1)}, u32[]{:S(2)}, u32[]{:S(2)}) collective-permute-start(bf16[2,5,32,16]{3,2,1,0:T(8,128)(2,1)S(1)} %get-tuple-element.16), channel_id=1, source_target_pairs={{0,64},{64,128},{128,192},{1,65},{65,129},{129,193},{2,66},{66,130... | collective-permute-start | bytes 30728 | tf_op jit(solution)/shard_map/ppermute | solution.py:22
  60.9 1.3 %collective-permute-start.6 = (bf16[2,5,32,16]{3,2,1,0:T(8,128)(2,1)S(1)}, bf16[2,5,32,16]{3,2,1,0:T(8,128)(2,1)S(1)}, u32[]{:S(2)}, u32[]{:S(2)}) collective-permute-start(bf16[2,5,32,16]{3,2,1,0:T(8,128)(2,1)S(1)} %get-tuple-element.17), channel_id=1, source_target_pairs={{64,0},{128,64},{192,128},{65,1},{129,65},{193,129},{66,2},{130,66... | collective-permute-start | bytes 30728 | tf_op jit(solution)/shard_map/ppermute | solution.py:25
  62.3 4.0 %collective-permute-done.6 = bf16[2,5,32,16]{3,2,1,0:T(8,128)(2,1)S(1)} collective-permute-done((bf16[2,5,32,16]{3,2,1,0:T(8,128)(2,1)S(1)}, bf16[2,5,32,16]{3,2,1,0:T(8,128)(2,1)S(1)}, u32[]{:S(2)}, u32[]{:S(2)}) %collective-permute-start.6) | collective-permute-done | bytes 10272 | tf_op jit(solution)/shard_map/ppermute | solution.py:25
  66.5 3.0 %collective-permute-start.7 = (bf16[2,5,16,160]{3,2,1,0:T(8,128)(2,1)S(1)}, bf16[2,5,16,160]{3,2,1,0:T(8,128)(2,1)S(1)}, u32[]{:S(2)}, u32[]{:S(2)}) collective-permute-start(bf16[2,5,16,160]{3,2,1,0:T(8,128)(2,1)S(1)} %get-tuple-element.15), channel_id=1, source_target_pairs={{0,1},{1,2},{2,3},{3,4},{4,5},{5,6},{6,7},{7,8},{8,9},{9,10},{10,1... | collective-permute-start | bytes 153608 | tf_op jit(solution)/shard_map/ppermute | solution.py:22
  69.5 3.1 %collective-permute-start.8 = (bf16[2,5,16,160]{3,2,1,0:T(8,128)(2,1)S(1)}, bf16[2,5,16,160]{3,2,1,0:T(8,128)(2,1)S(1)}, u32[]{:S(2)}, u32[]{:S(2)}) collective-permute-start(bf16[2,5,16,160]{3,2,1,0:T(8,128)(2,1)S(1)} %get-tuple-element.14), channel_id=1, source_target_pairs={{1,0},{2,1},{3,2},{4,3},{5,4},{6,5},{7,6},{8,7},{9,8},{10,9},{11,1... | collective-permute-start | bytes 153608 | tf_op jit(solution)/shard_map/ppermute | solution.py:25
  72.6 1.0 %convert_bitcast_fusion = bf16[2,33,160,128,1]{3,1,0,2,4:T(8,128)(2,1)S(1)} fusion(bf16[2,33,33]{2,0,1:T(2,128)(2,1)S(1)} %rev.4), kind=kOutput, calls=%fused_computation.1 | convolution fusion | flops 91914240 | bytes 2707716 | tf_op jit(solution)/shard_map/kdv,vjc->kdjc/dot_general | solution.py:37
  73.6 7.9 %collective-permute-done.8 = bf16[2,5,16,160]{3,2,1,0:T(8,128)(2,1)S(1)} collective-permute-done((bf16[2,5,16,160]{3,2,1,0:T(8,128)(2,1)S(1)}, bf16[2,5,16,160]{3,2,1,0:T(8,128)(2,1)S(1)}, u32[]{:S(2)}, u32[]{:S(2)}) %collective-permute-start.8) | collective-permute-done | bytes 51232 | tf_op jit(solution)/shard_map/ppermute | solution.py:25
  83.4 1.6 %constant_dynamic-update-slice_fusion.7 = (f32[8,5,32,128]{3,2,1,0:T(8,128)S(1)}, f32[5,32,128,1,1]{2,1,0,4,3:T(8,128)S(1)}) fusion(bf16[2,5,33,32,160]{4,3,1,0,2:T(8,128)(2,1)S(1)} %fusion.13, bf16[2,33,160,128,1]{3,1,0,2,4:T(8,128)(2,1)S(1)} %convert_bitcast_fusion), kind=kOutput, calls=%fused_computation.110 | convolution fusion | flops 432537600 | bytes 6246400 | tf_op jit(solution)/shard_map/kbdrj,kdjc->brc/dot_general | solution.py:195
  85.2 3.6 %collective-permute-start.10 = (f32[5,32,128]{2,1,0:T(8,128)S(1)}, f32[5,32,128]{2,1,0:T(8,128)S(1)}, u32[]{:S(2)}, u32[]{:S(2)}) collective-permute-start(f32[5,32,128]{2,1,0:T(8,128)S(1)} %bitcast.222), channel_id=1, source_target_pairs={{0,128},{64,192},{128,0},{192,64},{1,129},{65,193},{129,1},{193,65... | collective-permute-start | bytes 245768 | tf_op jit(solution)/shard_map/ppermute | solution.py:204
  88.9 4.6 %collective-permute-done.10 = f32[5,32,128]{2,1,0:T(8,128)S(1)} collective-permute-done((f32[5,32,128]{2,1,0:T(8,128)S(1)}, f32[5,32,128]{2,1,0:T(8,128)S(1)}, u32[]{:S(2)}, u32[]{:S(2)}) %collective-permute-start.10) | collective-permute-done | bytes 81952 | tf_op jit(solution)/shard_map/ppermute | solution.py:204
  94.1 1.0 %fusion.57 = f32[16384,16]{0,1:T(8,128)S(1)} fusion(f32[5,16384]{1,0:T(8,128)S(1)} %reshape.35, f32[5,16]{1,0:T(8,128)S(1)} %copy-done), kind=kOutput, calls=%fused_computation.120 | convolution fusion | flops 15728640 | bytes 1376576 | tf_op jit(solution)/shard_map/dot_general | solution.py:212
  95.7 1.3 %bitcast_multiply_fusion = f32[16,32,512]{2,1,0:T(8,128)} fusion(f32[2,8,32,512]{3,2,1,0:T(8,128)S(1)} %copy.31, f32[16,32,512]{2,1,0:T(8,128)S(1)} %copy-done.1, f32[16]{0:T(128)S(1)} %multiply_multiply_fusion, f32[16]{0:T(128)S(1)} %copy-done.11), kind=kLoop, calls=%fused_computation.9 | loop fusion | flops 1048576 | bytes 3145856 | tf_op jit(solution)/shard_map/mul | solution.py:218
  (105 shorter events, 10.8 us)
Async XLA Ops:
  0.0 3.0 %copy-start = (f32[5,16]{1,0:T(8,128)S(1)}, f32[5,16]{1,0:T(8,128)}, u32[]{:S(2)}) copy-start(f32[5,16]{1,0:T(8,128)} %param.12) | copy-start | bytes 964
  0.0 7.0 %copy-start.7 = (f32[4,64,128]{2,1,0:T(8,128)S(1)}, f32[4,64,128]{2,1,0:T(8,128)}, u32[]{:S(2)}) copy-start(f32[4,64,128]{2,1,0:T(8,128)} %param.18) | copy-start | bytes 393220
  0.0 7.0 %copy-start.10 = (s32[4,64]{1,0:T(4,128)S(1)}, s32[4,64]{1,0:T(4,128)}, u32[]{:S(2)}) copy-start(s32[4,64]{1,0:T(4,128)} %param.19) | copy-start | bytes 3076
  0.0 7.1 %copy-start.3 = (f32[2,4,64,128]{3,2,1,0:T(8,128)S(1)}, f32[2,4,64,128]{3,2,1,0:T(8,128)}, u32[]{:S(2)}) copy-start(f32[2,4,64,128]{3,2,1,0:T(8,128)} %param.17) | copy-start | bytes 786436
  0.8 6.5 %copy-start.5 = (s32[4,64,128]{2,1,0:T(8,128)S(1)}, s32[4,64,128]{2,1,0:T(8,128)}, u32[]{:S(2)}) copy-start(s32[4,64,128]{2,1,0:T(8,128)} %param.15) | copy-start | bytes 393220
  0.8 6.5 %copy-start.6 = (s32[4,64,128]{2,1,0:T(8,128)S(1)}, s32[4,64,128]{2,1,0:T(8,128)}, u32[]{:S(2)}) copy-start(s32[4,64,128]{2,1,0:T(8,128)} %param.16) | copy-start | bytes 393220
  3.0 26.3 %copy-start.8 = (bf16[2,33,33]{2,0,1:T(2,128)(2,1)S(1)}, bf16[2,33,33]{2,0,1:T(2,128)(2,1)}, u32[]{:S(2)}) copy-start(bf16[2,33,33]{2,0,1:T(2,128)(2,1)} %param.13) | copy-start | bytes 13072
  4.2 18.2 %collective-permute-start = (f32[5,32,160]{2,1,0:T(8,128)S(1)}, f32[5,32,160]{2,1,0:T(8,128)S(1)}, u32[]{:S(2)}, u32[]{:S(2)}) collective-permute-start(f32[5,32,160]{2,1,0:T(8,128)S(1)} %get-tuple-element.5), channel_id=1, source_target_pairs={{0,64},{64,128},{128,192},{192,0},{1,65},{65,129},{129,193},{193,1... | collective-permute-start | bytes 307208 | tf_op jit(solution)/shard_map/ppermute | solution.py:184
  4.3 18.2 %collective-permute-start.1 = (f32[5,32,160]{2,1,0:T(8,128)S(1)}, f32[5,32,160]{2,1,0:T(8,128)S(1)}, u32[]{:S(2)}, u32[]{:S(2)}) collective-permute-start(f32[5,32,160]{2,1,0:T(8,128)S(1)} %get-tuple-element.7), channel_id=1, source_target_pairs={{0,128},{64,192},{128,0},{192,64},{1,129},{65,193},{129,1},{193,65... | collective-permute-start | bytes 307208 | tf_op jit(solution)/shard_map/ppermute | solution.py:184
  5.6 16.9 %collective-permute-start.2 = (f32[5,32,160]{2,1,0:T(8,128)S(1)}, f32[5,32,160]{2,1,0:T(8,128)S(1)}, u32[]{:S(2)}, u32[]{:S(2)}) collective-permute-start(f32[5,32,160]{2,1,0:T(8,128)S(1)} %get-tuple-element.6), channel_id=1, source_target_pairs={{0,192},{64,0},{128,64},{192,128},{1,193},{65,1},{129,65},{193,129... | collective-permute-start | bytes 307208 | tf_op jit(solution)/shard_map/ppermute | solution.py:184
  8.6 24.0 %copy-start.9 = (s32[32,128]{1,0:T(8,128)S(1)}, s32[32,128]{1,0:T(8,128)}, u32[]{:S(2)}) copy-start(s32[32,128]{1,0:T(8,128)} %param.14) | copy-start | bytes 49156
  8.6 36.8 %all-to-all-start = ((f32[4,256,128]{2,0,1:T(4,128)}), f32[4,256,128]{2,0,1:T(4,128)S(1)}, u32[]{:S(2)}, u32[]{:S(2)}) async-start(f32[4,256,128]{2,0,1:T(4,128)} %pad_maximum_fusion.1), calls=%async_computation | async-start | bytes 1048576 | tf_op jit(solution)/shard_map/all_to_all | solution.py:158
  22.6 10.6 %collective-permute-start.3 = (bf16[5,16,160]{2,1,0:T(8,128)(2,1)S(1)}, bf16[5,16,160]{2,1,0:T(8,128)(2,1)S(1)}, u32[]{:S(2)}, u32[]{:S(2)}) collective-permute-start(bf16[5,16,160]{2,1,0:T(8,128)(2,1)S(1)} %get-tuple-element.18), channel_id=1, source_target_pairs={{0,1},{1,2},{2,3},{3,4},{4,5},{5,6},{6,7},{7,8},{8,9},{9,10},{10,1... | collective-permute-start | bytes 76808 | tf_op jit(solution)/shard_map/ppermute | solution.py:22
  27.2 11.6 %collective-permute-start.4 = (bf16[5,16,160]{2,1,0:T(8,128)(2,1)S(1)}, bf16[5,16,160]{2,1,0:T(8,128)(2,1)S(1)}, u32[]{:S(2)}, u32[]{:S(2)}) collective-permute-start(bf16[5,16,160]{2,1,0:T(8,128)(2,1)S(1)} %get-tuple-element.19), channel_id=1, source_target_pairs={{1,0},{2,1},{3,2},{4,3},{5,4},{6,5},{7,6},{8,7},{9,8},{10,9},{11,1... | collective-permute-start | bytes 76808 | tf_op jit(solution)/shard_map/ppermute | solution.py:25
  46.2 13.2 %copy-start.4 = (f32[2,5,32,128]{3,2,1,0:T(8,128)S(1)}, f32[2,5,32,128]{3,2,1,0:T(8,128)}, u32[]{:S(2)}) copy-start(f32[2,5,32,128]{3,2,1,0:T(8,128)} %shard_map.100) | copy-start | bytes 491524
  59.6 2.7 %collective-permute-start.5 = (bf16[2,5,32,16]{3,2,1,0:T(8,128)(2,1)S(1)}, bf16[2,5,32,16]{3,2,1,0:T(8,128)(2,1)S(1)}, u32[]{:S(2)}, u32[]{:S(2)}) collective-permute-start(bf16[2,5,32,16]{3,2,1,0:T(8,128)(2,1)S(1)} %get-tuple-element.16), channel_id=1, source_target_pairs={{0,64},{64,128},{128,192},{1,65},{65,129},{129,193},{2,66},{66,130... | collective-permute-start | bytes 30728 | tf_op jit(solution)/shard_map/ppermute | solution.py:22
  60.9 5.5 %collective-permute-start.6 = (bf16[2,5,32,16]{3,2,1,0:T(8,128)(2,1)S(1)}, bf16[2,5,32,16]{3,2,1,0:T(8,128)(2,1)S(1)}, u32[]{:S(2)}, u32[]{:S(2)}) collective-permute-start(bf16[2,5,32,16]{3,2,1,0:T(8,128)(2,1)S(1)} %get-tuple-element.17), channel_id=1, source_target_pairs={{64,0},{128,64},{192,128},{65,1},{129,65},{193,129},{66,2},{130,66... | collective-permute-start | bytes 30728 | tf_op jit(solution)/shard_map/ppermute | solution.py:25
  66.5 7.1 %collective-permute-start.7 = (bf16[2,5,16,160]{3,2,1,0:T(8,128)(2,1)S(1)}, bf16[2,5,16,160]{3,2,1,0:T(8,128)(2,1)S(1)}, u32[]{:S(2)}, u32[]{:S(2)}) collective-permute-start(bf16[2,5,16,160]{3,2,1,0:T(8,128)(2,1)S(1)} %get-tuple-element.15), channel_id=1, source_target_pairs={{0,1},{1,2},{2,3},{3,4},{4,5},{5,6},{6,7},{7,8},{8,9},{9,10},{10,1... | collective-permute-start | bytes 153608 | tf_op jit(solution)/shard_map/ppermute | solution.py:22
  69.5 12.1 %collective-permute-start.8 = (bf16[2,5,16,160]{3,2,1,0:T(8,128)(2,1)S(1)}, bf16[2,5,16,160]{3,2,1,0:T(8,128)(2,1)S(1)}, u32[]{:S(2)}, u32[]{:S(2)}) collective-permute-start(bf16[2,5,16,160]{3,2,1,0:T(8,128)(2,1)S(1)} %get-tuple-element.14), channel_id=1, source_target_pairs={{1,0},{2,1},{3,2},{4,3},{5,4},{6,5},{7,6},{8,7},{9,8},{10,9},{11,1... | collective-permute-start | bytes 153608 | tf_op jit(solution)/shard_map/ppermute | solution.py:25
  85.1 10.7 %copy-start.1 = (f32[16,32,512]{2,1,0:T(8,128)S(1)}, f32[16,32,512]{2,1,0:T(8,128)}, u32[]{:S(2)}) copy-start(f32[16,32,512]{2,1,0:T(8,128)} %param.10) | copy-start | bytes 3145732
  85.1 10.7 %copy-start.11 = (f32[16]{0:T(128)S(1)}, f32[16]{0:T(128)}, u32[]{:S(2)}) copy-start(f32[16]{0:T(128)} %param.11) | copy-start | bytes 196
  85.1 3.8 %collective-permute-start.9 = (f32[5,32,128]{2,1,0:T(8,128)S(1)}, f32[5,32,128]{2,1,0:T(8,128)S(1)}, u32[]{:S(2)}, u32[]{:S(2)}) collective-permute-start(f32[5,32,128]{2,1,0:T(8,128)S(1)} %bitcast.221), channel_id=1, source_target_pairs={{0,192},{64,0},{128,64},{192,128},{1,193},{65,1},{129,65},{193,129... | collective-permute-start | bytes 245768 | tf_op jit(solution)/shard_map/ppermute | solution.py:204
  85.2 8.4 %collective-permute-start.10 = (f32[5,32,128]{2,1,0:T(8,128)S(1)}, f32[5,32,128]{2,1,0:T(8,128)S(1)}, u32[]{:S(2)}, u32[]{:S(2)}) collective-permute-start(f32[5,32,128]{2,1,0:T(8,128)S(1)} %bitcast.222), channel_id=1, source_target_pairs={{0,128},{64,192},{128,0},{192,64},{1,129},{65,193},{129,1},{193,65... | collective-permute-start | bytes 245768 | tf_op jit(solution)/shard_map/ppermute | solution.py:204
  88.8 4.8 %collective-permute-start.11 = (f32[5,32,128]{2,1,0:T(8,128)S(1)}, f32[5,32,128]{2,1,0:T(8,128)S(1)}, u32[]{:S(2)}, u32[]{:S(2)}) collective-permute-start(f32[5,32,128]{2,1,0:T(8,128)S(1)} %bitcast.223), channel_id=1, source_target_pairs={{0,64},{64,128},{128,192},{192,0},{1,65},{65,129},{129,193},{193,1... | collective-permute-start | bytes 245768 | tf_op jit(solution)/shard_map/ppermute | solution.py:204
  (1 other events, 0.8 us)

commit v10 on v9

--- a/solution.py
+++ b/solution.py
@@ -160,19 +160,13 @@
     )
     sum_rows = 256
     sums = deposit_sums(arrived.reshape(4, -1), sum_rows, NBIN * pixels // sum_rows)
-    sums = sums.reshape(3, NBIN, height, columns)
+    sums = lax.optimization_barrier(sums.reshape(3, NBIN, height, columns))
     weight_sum = sums[0]
     shape_sum = sums[1:]
 
     sigma = shell_sigma[:, None, None]
     growth = jnp.exp(sigma * latent - 0.5 * sigma * sigma)
-    shells = latent.shape[0]
-    partial_bins = jnp.dot(
-    lens_weight,
-        (growth - 1.0).reshape(shells, height * width),
-        precision=lax.Precision.HIGHEST,
-        preferred_element_type=jnp.float32,
-    ).reshape(NBIN, height, width)
+    partial_bins = jnp.sum(lens_weight[:, :, None, None] * (growth - 1.0)[None], axis=1)
     wide = jnp.pad(partial_bins, ((0, 0), (0, 0), (HALF, HALF)))
     windows = jnp.stack(
         [wide[:, :, owner * columns : owner * columns + columns + 2 * HALF] for owner in range(shell_count)]
@@ -190,7 +184,7 @@
     shear = correlate_forward(padded, forward_bands, height)
     shear_grad = shear * weight_sum[None] - shape_sum
     masked = (shear_grad * star_mask.astype(jnp.float32)).astype(jnp.bfloat16)
-    rims = extended(masked, (("shell", 3), ("tile", 2)), HALF)
+    rims = extended(masked, (("tile", 2), ("shell", 3)), HALF)
     back_bands = build_bands(jnp.flip(shear_kernel, (1, 2)), columns)
     bin_grad = jnp.einsum(
         "kbdrj,kdjc->brc",
@@ -208,13 +202,8 @@
     by_offset = jnp.stack([received[(-j) % shell_count] for j in range(shell_count)])
     twice = jnp.concatenate([by_offset, by_offset], axis=0)
     blocks = lax.dynamic_slice_in_dim(twice, (shell_count - me) % shell_count, shell_count, 0)
-    full_grad = jnp.transpose(blocks, (1, 2, 0, 3)).reshape(NBIN, height * width)
-    mixed = jnp.dot(
-        lens_weight.T,
-        full_grad,
-        precision=lax.Precision.HIGHEST,
-        preferred_element_type=jnp.float32,
-    ).reshape(shells, height, width)
+    full_grad = jnp.transpose(blocks, (1, 2, 0, 3)).reshape(NBIN, height, width)
+    mixed = jnp.sum(lens_weight.T[:, :, None, None] * full_grad[None], axis=1)
     return sigma * growth * mixed
 
 

time: 97.5 us -> 97 us (level)
  local copies, waits for them, and re-layouts: 9.18 us -> 6.62 us
  starting transfers between devices: 35.8 us -> 38.1 us
  other arithmetic: 6.22 us -> 7.96 us
  matrix products: 5.33 us -> 3.64 us
    slice x4 -> x0, local copies, waits for them, and re-layouts: 2.09 us -> none  [the longest x2 1.17 us: per_device(): shape_sum = sums[1:]]
    reduce_sum x0 -> x2, other arithmetic: none -> 2.04 us  [the longest x1 1.31 us: per_device(): jnp.sum(lens_weight[:, :, None, None] * (growth - 1.0)[None], axis=1)]
    ppermute x3, starting transfers between devices: 3.8 us -> 5.8 us  [per_device(): lax.ppermute(bin_grad, 'shell', [(i, (i + shift) % shell_count) for i in...]
    dot_general x2 -> x0, matrix products: 1.7 us -> none  [the longest x1 1.03 us: per_device(): jnp.dot(lens_weight.T, full_grad, precision=lax.Precision.HIGHEST, prefer...]
    ppermute x3, starting transfers between devices: 8.87 us -> 10.4 us  [extended(): lax.ppermute(lax.slice_in_dim(block, block.shape[dim] - width, None, axis...]
    unnamed x64 -> x62, local copies, waits for them, and re-layouts: 3.6 us -> 2.19 us
    ppermute x3, starting transfers between devices: 6.49 us -> 5.31 us  [extended(): lax.ppermute(lax.slice_in_dim(block, 0, width, axis=dim), axis, backward)]
    reshape x1, local copies, waits for them, and re-layouts: 0.15 us -> 1.29 us  [per_device(): sums = lax.optimization_barrier(sums.reshape(3, NBIN, height, columns))]
  transfers between devices with their start and end apart: 13 -> 13, of which waited for: 5 -> 6; matrix products, arithmetic and copies ran while one was open for 7% -> 7% of each run, Pallas kernels for 6% -> 6%
where the time goes in v10:
time: 97 us; the launch traced here: 96.5 us
  starting transfers between devices  38.1 us (39%)
  waiting for transfers between devices  22.7 us (23%)
  Pallas kernels  16.8 us (17%)
  other arithmetic  7.96 us (8%)
  local copies, waits for them, and re-layouts  6.62 us (7%)
  matrix products  3.64 us (4%)
    ppermute x3, waiting for transfers between devices, extended(): lax.ppermute(lax.slice_in_dim(block, 0, width, axis=dim), axis, backward)  17.6 us
    all_to_all x1, starting transfers between devices, per_device(): lax.all_to_all(packet.reshape(4, devices, -1), ('shell', 'tile'), split_a...  13.9 us
    pallas_call x1, Pallas kernels, deposit_sums(): pl.pallas_call(functools.partial(scatter_kernel, rows, columns), out_shap...  11 us
    ppermute x3, starting transfers between devices, extended(): lax.ppermute(lax.slice_in_dim(block, block.shape[dim] - width, None, axis...  10.4 us
    pallas_call x1, Pallas kernels, correlate_forward(): pl.pallas_call(correlate_kernel, out_shape=jax.ShapeDtypeStruct((kinds, b...  5.86 us
    ppermute x3, starting transfers between devices, per_device(): lax.ppermute(bin_grad, 'shell', [(i, (i + shift) % shell_count) for i in...  5.8 us
    ppermute x3, starting transfers between devices, extended(): lax.ppermute(lax.slice_in_dim(block, 0, width, axis=dim), axis, backward)  5.31 us
    ppermute x3, waiting for transfers between devices, per_device(): lax.ppermute(bin_grad, 'shell', [(i, (i + shift) % shell_count) for i in...  4.49 us
  transfers between devices with their start and end apart: 13, of which 6 were waited for; matrix products, arithmetic and copies ran while one was open for 7% of the time, Pallas kernels for 6%

profile of v10, /device:TPU:124, one launch (start us, length us, event | category | flops | bytes accessed | tf_op | source)
XLA Modules:
  0.0 96.5 jit_solution(4495296942451520226)
XLA Ops:
  0.8 1.5 %fusion.10 = f32[16,32,512]{2,1,0:T(8,128)S(1)} fusion(f32[16,32,512]{2,1,0:T(8,128)} %param.10, f32[16]{0:T(128)S(1)} %multiply_multiply_fusion.1, f32[16]{0:T(128)} %param.11), kind=kLoop, calls=%fused_computation.13 | loop fusion | flops 786432 | bytes 2097280 | tf_op jit(solution)/shard_map/sub | solution.py:169
  2.3 1.3 %multiply_reduce_fusion.1 = f32[5,32,512]{2,1,0:T(8,128)S(1)} fusion(f32[16,32,512]{2,1,0:T(8,128)S(1)} %fusion.10, f32[5,16]{1,0:T(8,128)} %param.12), kind=kLoop, calls=%fused_computation.2 | loop fusion | flops 2539520 | bytes 1376576 | tf_op jit(solution)/shard_map/reduce_sum | solution.py:169
  4.1 1.3 %collective-permute-start.1 = (f32[5,32,160]{2,1,0:T(8,128)S(1)}, f32[5,32,160]{2,1,0:T(8,128)S(1)}, u32[]{:S(2)}, u32[]{:S(2)}) collective-permute-start(f32[5,32,160]{2,1,0:T(8,128)S(1)} %get-tuple-element.7), channel_id=1, source_target_pairs={{0,128},{64,192},{128,0},{192,64},{1,129},{65,193},{129,1},{193,65... | collective-permute-start | bytes 307208 | tf_op jit(solution)/shard_map/ppermute | solution.py:178
  5.4 1.4 %collective-permute-start.2 = (f32[5,32,160]{2,1,0:T(8,128)S(1)}, f32[5,32,160]{2,1,0:T(8,128)S(1)}, u32[]{:S(2)}, u32[]{:S(2)}) collective-permute-start(f32[5,32,160]{2,1,0:T(8,128)S(1)} %get-tuple-element.6), channel_id=1, source_target_pairs={{0,192},{64,0},{128,64},{192,128},{1,193},{65,1},{129,65},{193,129... | collective-permute-start | bytes 307208 | tf_op jit(solution)/shard_map/ppermute | solution.py:178
  7.2 1.1 %pad_maximum_fusion.1 = f32[4,256,128]{2,0,1:T(4,128)} fusion(f32[2,256,128]{2,0,1:T(2,128)S(1)} %bitcast.207, f32[1,256,128]{2,0,1:T(1,128)S(1)} %bitcast.206, f32[1,256,128]{2,0,1:T(1,128)S(1)} %bitcast.209), kind=kLoop, calls=%fused_computation.15 | loop fusion | flops 262144 | bytes 1048576 | tf_op jit(solution)/shard_map/concatenate | solution.py:154
  8.4 13.9 %all-to-all-start = ((f32[4,256,128]{2,0,1:T(4,128)}), f32[4,256,128]{2,0,1:T(4,128)S(1)}, u32[]{:S(2)}, u32[]{:S(2)}) async-start(f32[4,256,128]{2,0,1:T(4,128)} %pad_maximum_fusion.1), calls=%async_computation | async-start | bytes 1048576 | tf_op jit(solution)/shard_map/all_to_all | solution.py:158
  22.4 4.6 %collective-permute-start.3 = (bf16[5,16,160]{2,1,0:T(8,128)(2,1)S(1)}, bf16[5,16,160]{2,1,0:T(8,128)(2,1)S(1)}, u32[]{:S(2)}, u32[]{:S(2)}) collective-permute-start(bf16[5,16,160]{2,1,0:T(8,128)(2,1)S(1)} %get-tuple-element.16), channel_id=1, source_target_pairs={{0,1},{1,2},{2,3},{3,4},{4,5},{5,6},{6,7},{7,8},{8,9},{9,10},{10,1... | collective-permute-start | bytes 76808 | tf_op jit(solution)/shard_map/ppermute | solution.py:22
  27.0 2.1 %collective-permute-start.4 = (bf16[5,16,160]{2,1,0:T(8,128)(2,1)S(1)}, bf16[5,16,160]{2,1,0:T(8,128)(2,1)S(1)}, u32[]{:S(2)}, u32[]{:S(2)}) collective-permute-start(bf16[5,16,160]{2,1,0:T(8,128)(2,1)S(1)} %get-tuple-element.17), channel_id=1, source_target_pairs={{1,0},{2,1},{3,2},{4,3},{5,4},{6,5},{7,6},{8,7},{9,8},{10,9},{11,1... | collective-permute-start | bytes 76808 | tf_op jit(solution)/shard_map/ppermute | solution.py:25
  29.1 1.0 %fusion.3 = bf16[160,128,2,33]{1,3,2,0:T(8,128)(2,1)S(1)} fusion(bf16[2,33,33]{2,0,1:T(2,128)(2,1)S(1)} %copy-done.7), kind=kOutput, calls=%fused_computation.7 | convolution fusion | flops 90562560 | bytes 2707716 | tf_op jit(solution)/shard_map/kdv,vjc->kdjc/dot_general | solution.py:37
  30.1 2.2 %copy.56 = bf16[160,128,2,33]{1,0,3,2:T(8,128)(2,1)} copy(bf16[160,128,2,33]{1,3,2,0:T(8,128)(2,1)S(1)} %fusion.3) | data formatting | bytes 5406720 | tf_op jit(solution)/shard_map/kdv,vjc->kdjc/dot_general | solution.py:37
  32.9 5.7 %collective-permute-done.4 = bf16[5,16,160]{2,1,0:T(8,128)(2,1)S(1)} collective-permute-done((bf16[5,16,160]{2,1,0:T(8,128)(2,1)S(1)}, bf16[5,16,160]{2,1,0:T(8,128)(2,1)S(1)}, u32[]{:S(2)}, u32[]{:S(2)}) %collective-permute-start.4) | collective-permute-done | bytes 25632 | tf_op jit(solution)/shard_map/ppermute | solution.py:25
  39.3 5.9 %shard_map.100 = f32[2,5,32,128]{3,2,1,0:T(8,128)} custom-call(bf16[5,64,160]{2,1,0:T(8,128)(2,1)} %pad_maximum_fusion.3.x_ref, bf16[2,33,160,128]{3,2,1,0:T(8,128)(2,1)} %bitcast.205), custom_call_target="tpu_custom_call" | custom-call | flops 865075200 | bytes 2969600 | tf_op jit(solution)/shard_map/pallas_call | solution.py:118
  45.9 11.0 %shard_map.101 = f32[3,256,80]{2,1,0:T(8,128)} custom-call(f32[4,32768]{1,0:T(4,128)} %bitcast.208), custom_call_target="tpu_custom_call" | custom-call | flops 8053063680 | bytes 770048 | tf_op jit(solution)/shard_map/pallas_call | solution.py:89
  56.9 1.3 %reshape.24 = f32[3,5,32,128]{3,2,1,0:T(8,128)S(1)} reshape(f32[3,256,80]{2,1,0:T(8,128)} %shard_map.101) | data formatting | bytes 491520 | tf_op jit(solution)/shard_map/reshape | solution.py:163
  58.3 4.5 %collective-permute-start.5 = (bf16[2,5,16,128]{3,2,1,0:T(8,128)(2,1)S(1)}, bf16[2,5,16,128]{3,2,1,0:T(8,128)(2,1)S(1)}, u32[]{:S(2)}, u32[]{:S(2)}) collective-permute-start(bf16[2,5,16,128]{3,2,1,0:T(8,128)(2,1)S(1)} %get-tuple-element.14), channel_id=1, source_target_pairs={{0,1},{1,2},{2,3},{3,4},{4,5},{5,6},{6,7},{7,8},{8,9},{9,10},{10,1... | collective-permute-start | bytes 122888 | tf_op jit(solution)/shard_map/ppermute | solution.py:22
  62.8 1.9 %collective-permute-start.6 = (bf16[2,5,16,128]{3,2,1,0:T(8,128)(2,1)S(1)}, bf16[2,5,16,128]{3,2,1,0:T(8,128)(2,1)S(1)}, u32[]{:S(2)}, u32[]{:S(2)}) collective-permute-start(bf16[2,5,16,128]{3,2,1,0:T(8,128)(2,1)S(1)} %get-tuple-element.15), channel_id=1, source_target_pairs={{1,0},{2,1},{3,2},{4,3},{5,4},{6,5},{7,6},{8,7},{9,8},{10,9},{11,1... | collective-permute-start | bytes 122888 | tf_op jit(solution)/shard_map/ppermute | solution.py:25
  64.9 9.5 %collective-permute-done.6 = bf16[2,5,16,128]{3,2,1,0:T(8,128)(2,1)S(1)} collective-permute-done((bf16[2,5,16,128]{3,2,1,0:T(8,128)(2,1)S(1)}, bf16[2,5,16,128]{3,2,1,0:T(8,128)(2,1)S(1)}, u32[]{:S(2)}, u32[]{:S(2)}) %collective-permute-start.6) | collective-permute-done | bytes 40992 | tf_op jit(solution)/shard_map/ppermute | solution.py:25
  74.5 1.3 %collective-permute-start.7 = (bf16[2,5,64,16]{3,2,1,0:T(8,128)(2,1)S(1)}, bf16[2,5,64,16]{3,2,1,0:T(8,128)(2,1)S(1)}, u32[]{:S(2)}, u32[]{:S(2)}) collective-permute-start(bf16[2,5,64,16]{3,2,1,0:T(8,128)(2,1)S(1)} %get-tuple-element.12), channel_id=1, source_target_pairs={{0,64},{64,128},{128,192},{1,65},{65,129},{129,193},{2,66},{66,130... | collective-permute-start | bytes 61448 | tf_op jit(solution)/shard_map/ppermute | solution.py:22
  75.8 1.3 %collective-permute-start.8 = (bf16[2,5,64,16]{3,2,1,0:T(8,128)(2,1)S(1)}, bf16[2,5,64,16]{3,2,1,0:T(8,128)(2,1)S(1)}, u32[]{:S(2)}, u32[]{:S(2)}) collective-permute-start(bf16[2,5,64,16]{3,2,1,0:T(8,128)(2,1)S(1)} %get-tuple-element.13), channel_id=1, source_target_pairs={{64,0},{128,64},{192,128},{65,1},{129,65},{193,129},{66,2},{130,66... | collective-permute-start | bytes 61448 | tf_op jit(solution)/shard_map/ppermute | solution.py:25
  78.2 2.4 %collective-permute-done.8 = bf16[2,5,64,16]{3,2,1,0:T(8,128)(2,1)S(1)} collective-permute-done((bf16[2,5,64,16]{3,2,1,0:T(8,128)(2,1)S(1)}, bf16[2,5,64,16]{3,2,1,0:T(8,128)(2,1)S(1)}, u32[]{:S(2)}, u32[]{:S(2)}) %collective-permute-start.8) | collective-permute-done | bytes 20512 | tf_op jit(solution)/shard_map/ppermute | solution.py:25
  82.4 1.6 %constant_dynamic-update-slice_fusion.7 = (f32[8,5,32,128]{3,2,1,0:T(8,128)S(1)}, f32[5,32,128,1,1]{2,1,0,4,3:T(8,128)S(1)}) fusion(bf16[2,5,33,32,160]{4,3,1,0,2:T(8,128)(2,1)S(1)} %fusion.13, bf16[2,33,160,128,1]{3,1,0,2,4:T(8,128)(2,1)S(1)} %convert_bitcast_fusion), kind=kOutput, calls=%fused_computation.114 | convolution fusion | flops 432537600 | bytes 6246400 | tf_op jit(solution)/shard_map/kbdrj,kdjc->brc/dot_general | solution.py:189
  84.6 5.3 %collective-permute-start.10 = (f32[5,32,128]{2,1,0:T(8,128)S(1)}, f32[5,32,128]{2,1,0:T(8,128)S(1)}, u32[]{:S(2)}, u32[]{:S(2)}) collective-permute-start(f32[5,32,128]{2,1,0:T(8,128)S(1)} %bitcast.211), channel_id=1, source_target_pairs={{0,128},{64,192},{128,0},{192,64},{1,129},{65,193},{129,1},{193,65... | collective-permute-start | bytes 245768 | tf_op jit(solution)/shard_map/ppermute | solution.py:198
  89.9 4.3 %collective-permute-done.10 = f32[5,32,128]{2,1,0:T(8,128)S(1)} collective-permute-done((f32[5,32,128]{2,1,0:T(8,128)S(1)}, f32[5,32,128]{2,1,0:T(8,128)S(1)}, u32[]{:S(2)}, u32[]{:S(2)}) %collective-permute-start.10) | collective-permute-done | bytes 81952 | tf_op jit(solution)/shard_map/ppermute | solution.py:198
  95.3 1.3 %multiply_multiply_fusion = f32[16,32,512]{2,1,0:T(8,128)} fusion(f32[16,32,512]{2,1,0:T(8,128)S(1)} %multiply_reduce_fusion, f32[16,32,512]{2,1,0:T(8,128)S(1)} %copy-done, f32[16]{0:T(128)S(1)} %multiply_multiply_fusion.1, f32[16]{0:T(128)S(1)} %copy-done.11), kind=kLoop, calls=%fused_computation.11 | loop fusion | flops 1048576 | bytes 3145856 | tf_op jit(solution)/shard_map/mul | solution.py:207
  (99 shorter events, 8.2 us)
Async XLA Ops:
  0.0 6.7 %copy-start.6 = (f32[4,64,128]{2,1,0:T(8,128)S(1)}, f32[4,64,128]{2,1,0:T(8,128)}, u32[]{:S(2)}) copy-start(f32[4,64,128]{2,1,0:T(8,128)} %param.18) | copy-start | bytes 393220
  0.0 6.7 %copy-start.10 = (s32[4,64]{1,0:T(4,128)S(1)}, s32[4,64]{1,0:T(4,128)}, u32[]{:S(2)}) copy-start(s32[4,64]{1,0:T(4,128)} %param.19) | copy-start | bytes 3076
  0.0 6.9 %copy-start.2 = (f32[2,4,64,128]{3,2,1,0:T(8,128)S(1)}, f32[2,4,64,128]{3,2,1,0:T(8,128)}, u32[]{:S(2)}) copy-start(f32[2,4,64,128]{3,2,1,0:T(8,128)} %param.17) | copy-start | bytes 786436
  0.0 7.1 %copy-start.4 = (s32[4,64,128]{2,1,0:T(8,128)S(1)}, s32[4,64,128]{2,1,0:T(8,128)}, u32[]{:S(2)}) copy-start(s32[4,64,128]{2,1,0:T(8,128)} %param.15) | copy-start | bytes 393220
  0.0 7.1 %copy-start.5 = (s32[4,64,128]{2,1,0:T(8,128)S(1)}, s32[4,64,128]{2,1,0:T(8,128)}, u32[]{:S(2)}) copy-start(s32[4,64,128]{2,1,0:T(8,128)} %param.16) | copy-start | bytes 393220
  2.3 26.8 %copy-start.7 = (bf16[2,33,33]{2,0,1:T(2,128)(2,1)S(1)}, bf16[2,33,33]{2,0,1:T(2,128)(2,1)}, u32[]{:S(2)}) copy-start(bf16[2,33,33]{2,0,1:T(2,128)(2,1)} %param.13) | copy-start | bytes 13072
  4.0 18.2 %collective-permute-start = (f32[5,32,160]{2,1,0:T(8,128)S(1)}, f32[5,32,160]{2,1,0:T(8,128)S(1)}, u32[]{:S(2)}, u32[]{:S(2)}) collective-permute-start(f32[5,32,160]{2,1,0:T(8,128)S(1)} %get-tuple-element.5), channel_id=1, source_target_pairs={{0,64},{64,128},{128,192},{192,0},{1,65},{65,129},{129,193},{193,1... | collective-permute-start | bytes 307208 | tf_op jit(solution)/shard_map/ppermute | solution.py:178
  4.1 18.2 %collective-permute-start.1 = (f32[5,32,160]{2,1,0:T(8,128)S(1)}, f32[5,32,160]{2,1,0:T(8,128)S(1)}, u32[]{:S(2)}, u32[]{:S(2)}) collective-permute-start(f32[5,32,160]{2,1,0:T(8,128)S(1)} %get-tuple-element.7), channel_id=1, source_target_pairs={{0,128},{64,192},{128,0},{192,64},{1,129},{65,193},{129,1},{193,65... | collective-permute-start | bytes 307208 | tf_op jit(solution)/shard_map/ppermute | solution.py:178
  5.4 16.9 %collective-permute-start.2 = (f32[5,32,160]{2,1,0:T(8,128)S(1)}, f32[5,32,160]{2,1,0:T(8,128)S(1)}, u32[]{:S(2)}, u32[]{:S(2)}) collective-permute-start(f32[5,32,160]{2,1,0:T(8,128)S(1)} %get-tuple-element.6), channel_id=1, source_target_pairs={{0,192},{64,0},{128,64},{192,128},{1,193},{65,1},{129,65},{193,129... | collective-permute-start | bytes 307208 | tf_op jit(solution)/shard_map/ppermute | solution.py:178
  8.4 24.0 %copy-start.9 = (s32[32,128]{1,0:T(8,128)S(1)}, s32[32,128]{1,0:T(8,128)}, u32[]{:S(2)}) copy-start(s32[32,128]{1,0:T(8,128)} %param.14) | copy-start | bytes 49156
  8.4 36.8 %all-to-all-start = ((f32[4,256,128]{2,0,1:T(4,128)}), f32[4,256,128]{2,0,1:T(4,128)S(1)}, u32[]{:S(2)}, u32[]{:S(2)}) async-start(f32[4,256,128]{2,0,1:T(4,128)} %pad_maximum_fusion.1), calls=%async_computation | async-start | bytes 1048576 | tf_op jit(solution)/shard_map/all_to_all | solution.py:158
  22.4 10.6 %collective-permute-start.3 = (bf16[5,16,160]{2,1,0:T(8,128)(2,1)S(1)}, bf16[5,16,160]{2,1,0:T(8,128)(2,1)S(1)}, u32[]{:S(2)}, u32[]{:S(2)}) collective-permute-start(bf16[5,16,160]{2,1,0:T(8,128)(2,1)S(1)} %get-tuple-element.16), channel_id=1, source_target_pairs={{0,1},{1,2},{2,3},{3,4},{4,5},{5,6},{6,7},{7,8},{8,9},{9,10},{10,1... | collective-permute-start | bytes 76808 | tf_op jit(solution)/shard_map/ppermute | solution.py:22
  27.0 11.6 %collective-permute-start.4 = (bf16[5,16,160]{2,1,0:T(8,128)(2,1)S(1)}, bf16[5,16,160]{2,1,0:T(8,128)(2,1)S(1)}, u32[]{:S(2)}, u32[]{:S(2)}) collective-permute-start(bf16[5,16,160]{2,1,0:T(8,128)(2,1)S(1)} %get-tuple-element.17), channel_id=1, source_target_pairs={{1,0},{2,1},{3,2},{4,3},{5,4},{6,5},{7,6},{8,7},{9,8},{10,9},{11,1... | collective-permute-start | bytes 76808 | tf_op jit(solution)/shard_map/ppermute | solution.py:25
  45.9 12.3 %copy-start.3 = (f32[2,5,32,128]{3,2,1,0:T(8,128)S(1)}, f32[2,5,32,128]{3,2,1,0:T(8,128)}, u32[]{:S(2)}) copy-start(f32[2,5,32,128]{3,2,1,0:T(8,128)} %shard_map.100) | copy-start | bytes 491524
  58.3 6.5 %collective-permute-start.5 = (bf16[2,5,16,128]{3,2,1,0:T(8,128)(2,1)S(1)}, bf16[2,5,16,128]{3,2,1,0:T(8,128)(2,1)S(1)}, u32[]{:S(2)}, u32[]{:S(2)}) collective-permute-start(bf16[2,5,16,128]{3,2,1,0:T(8,128)(2,1)S(1)} %get-tuple-element.14), channel_id=1, source_target_pairs={{0,1},{1,2},{2,3},{3,4},{4,5},{5,6},{6,7},{7,8},{8,9},{9,10},{10,1... | collective-permute-start | bytes 122888 | tf_op jit(solution)/shard_map/ppermute | solution.py:22
  62.8 11.6 %collective-permute-start.6 = (bf16[2,5,16,128]{3,2,1,0:T(8,128)(2,1)S(1)}, bf16[2,5,16,128]{3,2,1,0:T(8,128)(2,1)S(1)}, u32[]{:S(2)}, u32[]{:S(2)}) collective-permute-start(bf16[2,5,16,128]{3,2,1,0:T(8,128)(2,1)S(1)} %get-tuple-element.15), channel_id=1, source_target_pairs={{1,0},{2,1},{3,2},{4,3},{5,4},{6,5},{7,6},{8,7},{9,8},{10,9},{11,1... | collective-permute-start | bytes 122888 | tf_op jit(solution)/shard_map/ppermute | solution.py:25
  74.5 3.6 %collective-permute-start.7 = (bf16[2,5,64,16]{3,2,1,0:T(8,128)(2,1)S(1)}, bf16[2,5,64,16]{3,2,1,0:T(8,128)(2,1)S(1)}, u32[]{:S(2)}, u32[]{:S(2)}) collective-permute-start(bf16[2,5,64,16]{3,2,1,0:T(8,128)(2,1)S(1)} %get-tuple-element.12), channel_id=1, source_target_pairs={{0,64},{64,128},{128,192},{1,65},{65,129},{129,193},{2,66},{66,130... | collective-permute-start | bytes 61448 | tf_op jit(solution)/shard_map/ppermute | solution.py:22
  75.8 4.7 %collective-permute-start.8 = (bf16[2,5,64,16]{3,2,1,0:T(8,128)(2,1)S(1)}, bf16[2,5,64,16]{3,2,1,0:T(8,128)(2,1)S(1)}, u32[]{:S(2)}, u32[]{:S(2)}) collective-permute-start(bf16[2,5,64,16]{3,2,1,0:T(8,128)(2,1)S(1)} %get-tuple-element.13), channel_id=1, source_target_pairs={{64,0},{128,64},{192,128},{65,1},{129,65},{193,129},{66,2},{130,66... | collective-permute-start | bytes 61448 | tf_op jit(solution)/shard_map/ppermute | solution.py:25
  82.1 2.4 %copy-start.8 = (f32[5,16]{1,0:T(8,128)S(1)}, f32[5,16]{1,0:T(8,128)}, u32[]{:S(2)}) copy-start(f32[5,16]{1,0:T(8,128)} %param.12) | copy-start | bytes 964
  82.4 12.9 %copy-start = (f32[16,32,512]{2,1,0:T(8,128)S(1)}, f32[16,32,512]{2,1,0:T(8,128)}, u32[]{:S(2)}) copy-start(f32[16,32,512]{2,1,0:T(8,128)} %param.10) | copy-start | bytes 3145732
  82.4 12.9 %copy-start.11 = (f32[16]{0:T(128)S(1)}, f32[16]{0:T(128)}, u32[]{:S(2)}) copy-start(f32[16]{0:T(128)} %param.11) | copy-start | bytes 196
  84.0 5.9 %collective-permute-start.9 = (f32[5,32,128]{2,1,0:T(8,128)S(1)}, f32[5,32,128]{2,1,0:T(8,128)S(1)}, u32[]{:S(2)}, u32[]{:S(2)}) collective-permute-start(f32[5,32,128]{2,1,0:T(8,128)S(1)} %bitcast.210), channel_id=1, source_target_pairs={{0,192},{64,0},{128,64},{192,128},{1,193},{65,1},{129,65},{193,129... | collective-permute-start | bytes 245768 | tf_op jit(solution)/shard_map/ppermute | solution.py:198
  84.6 9.6 %collective-permute-start.10 = (f32[5,32,128]{2,1,0:T(8,128)S(1)}, f32[5,32,128]{2,1,0:T(8,128)S(1)}, u32[]{:S(2)}, u32[]{:S(2)}) collective-permute-start(f32[5,32,128]{2,1,0:T(8,128)S(1)} %bitcast.211), channel_id=1, source_target_pairs={{0,128},{64,192},{128,0},{192,64},{1,129},{65,193},{129,1},{193,65... | collective-permute-start | bytes 245768 | tf_op jit(solution)/shard_map/ppermute | solution.py:198
  89.9 4.5 %collective-permute-start.11 = (f32[5,32,128]{2,1,0:T(8,128)S(1)}, f32[5,32,128]{2,1,0:T(8,128)S(1)}, u32[]{:S(2)}, u32[]{:S(2)}) collective-permute-start(f32[5,32,128]{2,1,0:T(8,128)S(1)} %bitcast.212), channel_id=1, source_target_pairs={{0,64},{64,128},{128,192},{192,0},{1,65},{65,129},{129,193},{193,1... | collective-permute-start | bytes 245768 | tf_op jit(solution)/shard_map/ppermute | solution.py:198
  (1 other events, 0.8 us)

commit v11 on v10

--- a/solution.py
+++ b/solution.py
@@ -160,12 +160,13 @@
     )
     sum_rows = 256
     sums = deposit_sums(arrived.reshape(4, -1), sum_rows, NBIN * pixels // sum_rows)
-    sums = lax.optimization_barrier(sums.reshape(3, NBIN, height, columns))
+    sums = sums.reshape(3, NBIN, height, columns)
     weight_sum = sums[0]
     shape_sum = sums[1:]
 
     sigma = shell_sigma[:, None, None]
-    growth = jnp.exp(sigma * latent - 0.5 * sigma * sigma)
+    exponent = sigma * latent - 0.5 * sigma * sigma
+    growth = jnp.exp(exponent)
     partial_bins = jnp.sum(lens_weight[:, :, None, None] * (growth - 1.0)[None], axis=1)
     wide = jnp.pad(partial_bins, ((0, 0), (0, 0), (HALF, HALF)))
     windows = jnp.stack(
@@ -184,7 +185,7 @@
     shear = correlate_forward(padded, forward_bands, height)
     shear_grad = shear * weight_sum[None] - shape_sum
     masked = (shear_grad * star_mask.astype(jnp.float32)).astype(jnp.bfloat16)
-    rims = extended(masked, (("tile", 2), ("shell", 3)), HALF)
+    rims = extended(masked, (("shell", 3), ("tile", 2)), HALF)
     back_bands = build_bands(jnp.flip(shear_kernel, (1, 2)), columns)
     bin_grad = jnp.einsum(
         "kbdrj,kdjc->brc",
@@ -204,7 +205,7 @@
     blocks = lax.dynamic_slice_in_dim(twice, (shell_count - me) % shell_count, shell_count, 0)
     full_grad = jnp.transpose(blocks, (1, 2, 0, 3)).reshape(NBIN, height, width)
     mixed = jnp.sum(lens_weight.T[:, :, None, None] * full_grad[None], axis=1)
-    return sigma * growth * mixed
+    return jnp.exp(exponent + jnp.log(sigma)) * mixed
 
 
 def solution(mesh):

time: 97 us -> 96.1 us (level)
  starting transfers between devices: 38.1 us -> 35.8 us
    slice x0 -> x4, local copies, waits for them, and re-layouts: none -> 2.09 us  [the longest x2 1.17 us: per_device(): shape_sum = sums[1:]]
    ppermute x3, starting transfers between devices: 5.8 us -> 3.81 us  [per_device(): lax.ppermute(bin_grad, 'shell', [(i, (i + shift) % shell_count) for i in...]
    ppermute x3, starting transfers between devices: 10.4 us -> 8.86 us  [extended(): lax.ppermute(lax.slice_in_dim(block, block.shape[dim] - width, None, axis...]
    reshape x1 -> x0, local copies, waits for them, and re-layouts: 1.29 us -> none  [per_device(): sums = lax.optimization_barrier(sums.reshape(3, NBIN, height, columns))]
    ppermute x3, starting transfers between devices: 5.31 us -> 6.5 us  [extended(): lax.ppermute(lax.slice_in_dim(block, 0, width, axis=dim), axis, backward)]
    mul x2 -> x1, other arithmetic: 2 us -> 1.3 us  [per_device(): return jnp.exp(exponent + jnp.log(sigma)) * mixed]
    unnamed x62 -> x61, local copies, waits for them, and re-layouts: 2.19 us -> 2.18 us
  transfers between devices with their start and end apart: 13 -> 13, of which waited for: 6 -> 5; matrix products, arithmetic and copies ran while one was open for 7% -> 7% of each run, Pallas kernels for 6% -> 6%
where the time goes in v11:
time: 96.1 us; the launch traced here: 95.6 us
  starting transfers between devices  35.8 us (37%)
  waiting for transfers between devices  22.8 us (24%)
  Pallas kernels  16.9 us (18%)
  other arithmetic  8.24 us (9%)
  local copies, waits for them, and re-layouts  7.49 us (8%)
  matrix products  3.64 us (4%)
    ppermute x3, waiting for transfers between devices, extended(): lax.ppermute(lax.slice_in_dim(block, 0, width, axis=dim), axis, backward)  17.6 us
    all_to_all x1, starting transfers between devices, per_device(): lax.all_to_all(packet.reshape(4, devices, -1), ('shell', 'tile'), split_a...  13.9 us
    pallas_call x1, Pallas kernels, deposit_sums(): pl.pallas_call(functools.partial(scatter_kernel, rows, columns), out_shap...  11 us
    ppermute x3, starting transfers between devices, extended(): lax.ppermute(lax.slice_in_dim(block, block.shape[dim] - width, None, axis...  8.86 us
    ppermute x3, starting transfers between devices, extended(): lax.ppermute(lax.slice_in_dim(block, 0, width, axis=dim), axis, backward)  6.5 us
    pallas_call x1, Pallas kernels, correlate_forward(): pl.pallas_call(correlate_kernel, out_shape=jax.ShapeDtypeStruct((kinds, b...  5.86 us
    ppermute x3, waiting for transfers between devices, per_device(): lax.ppermute(bin_grad, 'shell', [(i, (i + shift) % shell_count) for i in...  4.64 us
    ppermute x3, starting transfers between devices, per_device(): lax.ppermute(bin_grad, 'shell', [(i, (i + shift) % shell_count) for i in...  3.81 us
  transfers between devices with their start and end apart: 13, of which 5 were waited for; matrix products, arithmetic and copies ran while one was open for 7% of the time, Pallas kernels for 6%

profile of v11, /device:TPU:124, one launch (start us, length us, event | category | flops | bytes accessed | tf_op | source)
XLA Modules:
  0.0 95.6 jit_solution(10259906476539286283)
XLA Ops:
  0.8 1.5 %exponential_add_fusion = f32[16,32,512]{2,1,0:T(8,128)S(1)} fusion(f32[16,32,512]{2,1,0:T(8,128)} %param.10, f32[16]{0:T(128)S(1)} %get-tuple-element.21, f32[16]{0:T(128)} %param.11), kind=kLoop, calls=%fused_computation.11 | loop fusion | flops 786432 | bytes 2097280 | tf_op jit(solution)/shard_map/sub | solution.py:170
  2.3 1.3 %multiply_reduce_fusion.1 = f32[5,32,512]{2,1,0:T(8,128)S(1)} fusion(f32[16,32,512]{2,1,0:T(8,128)S(1)} %exponential_add_fusion, f32[5,16]{1,0:T(8,128)} %param.12), kind=kLoop, calls=%fused_computation.2 | loop fusion | flops 2539520 | bytes 1376576 | tf_op jit(solution)/shard_map/reduce_sum | solution.py:170
  4.1 1.3 %collective-permute-start.1 = (f32[5,32,160]{2,1,0:T(8,128)S(1)}, f32[5,32,160]{2,1,0:T(8,128)S(1)}, u32[]{:S(2)}, u32[]{:S(2)}) collective-permute-start(f32[5,32,160]{2,1,0:T(8,128)S(1)} %get-tuple-element.7), channel_id=1, source_target_pairs={{0,128},{64,192},{128,0},{192,64},{1,129},{65,193},{129,1},{193,65... | collective-permute-start | bytes 307208 | tf_op jit(solution)/shard_map/ppermute | solution.py:179
  5.4 1.4 %collective-permute-start.2 = (f32[5,32,160]{2,1,0:T(8,128)S(1)}, f32[5,32,160]{2,1,0:T(8,128)S(1)}, u32[]{:S(2)}, u32[]{:S(2)}) collective-permute-start(f32[5,32,160]{2,1,0:T(8,128)S(1)} %get-tuple-element.6), channel_id=1, source_target_pairs={{0,192},{64,0},{128,64},{192,128},{1,193},{65,1},{129,65},{193,129... | collective-permute-start | bytes 307208 | tf_op jit(solution)/shard_map/ppermute | solution.py:179
  7.2 1.1 %pad_maximum_fusion.1 = f32[4,256,128]{2,0,1:T(4,128)} fusion(f32[2,256,128]{2,0,1:T(2,128)S(1)} %bitcast.203, f32[1,256,128]{2,0,1:T(1,128)S(1)} %bitcast.202, f32[1,256,128]{2,0,1:T(1,128)S(1)} %bitcast.205), kind=kLoop, calls=%fused_computation.15 | loop fusion | flops 262144 | bytes 1048576 | tf_op jit(solution)/shard_map/concatenate | solution.py:154
  8.4 13.9 %all-to-all-start = ((f32[4,256,128]{2,0,1:T(4,128)}), f32[4,256,128]{2,0,1:T(4,128)S(1)}, u32[]{:S(2)}, u32[]{:S(2)}) async-start(f32[4,256,128]{2,0,1:T(4,128)} %pad_maximum_fusion.1), calls=%async_computation | async-start | bytes 1048576 | tf_op jit(solution)/shard_map/all_to_all | solution.py:158
  22.4 4.6 %collective-permute-start.3 = (bf16[5,16,160]{2,1,0:T(8,128)(2,1)S(1)}, bf16[5,16,160]{2,1,0:T(8,128)(2,1)S(1)}, u32[]{:S(2)}, u32[]{:S(2)}) collective-permute-start(bf16[5,16,160]{2,1,0:T(8,128)(2,1)S(1)} %get-tuple-element.18), channel_id=1, source_target_pairs={{0,1},{1,2},{2,3},{3,4},{4,5},{5,6},{6,7},{7,8},{8,9},{9,10},{10,1... | collective-permute-start | bytes 76808 | tf_op jit(solution)/shard_map/ppermute | solution.py:22
  27.0 2.1 %collective-permute-start.4 = (bf16[5,16,160]{2,1,0:T(8,128)(2,1)S(1)}, bf16[5,16,160]{2,1,0:T(8,128)(2,1)S(1)}, u32[]{:S(2)}, u32[]{:S(2)}) collective-permute-start(bf16[5,16,160]{2,1,0:T(8,128)(2,1)S(1)} %get-tuple-element.19), channel_id=1, source_target_pairs={{1,0},{2,1},{3,2},{4,3},{5,4},{6,5},{7,6},{8,7},{9,8},{10,9},{11,1... | collective-permute-start | bytes 76808 | tf_op jit(solution)/shard_map/ppermute | solution.py:25
  29.1 1.0 %fusion.3 = bf16[160,128,2,33]{1,3,2,0:T(8,128)(2,1)S(1)} fusion(bf16[2,33,33]{2,0,1:T(2,128)(2,1)S(1)} %copy-done.7), kind=kOutput, calls=%fused_computation.7 | convolution fusion | flops 90562560 | bytes 2707716 | tf_op jit(solution)/shard_map/kdv,vjc->kdjc/dot_general | solution.py:37
  30.1 2.2 %copy.56 = bf16[160,128,2,33]{1,0,3,2:T(8,128)(2,1)} copy(bf16[160,128,2,33]{1,3,2,0:T(8,128)(2,1)S(1)} %fusion.3) | data formatting | bytes 5406720 | tf_op jit(solution)/shard_map/kdv,vjc->kdjc/dot_general | solution.py:37
  32.9 5.7 %collective-permute-done.4 = bf16[5,16,160]{2,1,0:T(8,128)(2,1)S(1)} collective-permute-done((bf16[5,16,160]{2,1,0:T(8,128)(2,1)S(1)}, bf16[5,16,160]{2,1,0:T(8,128)(2,1)S(1)}, u32[]{:S(2)}, u32[]{:S(2)}) %collective-permute-start.4) | collective-permute-done | bytes 25632 | tf_op jit(solution)/shard_map/ppermute | solution.py:25
  39.3 5.9 %shard_map.100 = f32[2,5,32,128]{3,2,1,0:T(8,128)} custom-call(bf16[5,64,160]{2,1,0:T(8,128)(2,1)} %pad_maximum_fusion.3.x_ref, bf16[2,33,160,128]{3,2,1,0:T(8,128)(2,1)} %bitcast.201), custom_call_target="tpu_custom_call" | custom-call | flops 865075200 | bytes 2969600 | tf_op jit(solution)/shard_map/pallas_call | solution.py:118
  45.9 11.0 %shard_map.101 = f32[3,256,80]{2,1,0:T(8,128)} custom-call(f32[4,32768]{1,0:T(4,128)} %bitcast.204), custom_call_target="tpu_custom_call" | custom-call | flops 8053063680 | bytes 770048 | tf_op jit(solution)/shard_map/pallas_call | solution.py:89
  59.3 1.3 %collective-permute-start.5 = (bf16[2,5,32,16]{3,2,1,0:T(8,128)(2,1)S(1)}, bf16[2,5,32,16]{3,2,1,0:T(8,128)(2,1)S(1)}, u32[]{:S(2)}, u32[]{:S(2)}) collective-permute-start(bf16[2,5,32,16]{3,2,1,0:T(8,128)(2,1)S(1)} %get-tuple-element.16), channel_id=1, source_target_pairs={{0,64},{64,128},{128,192},{1,65},{65,129},{129,193},{2,66},{66,130... | collective-permute-start | bytes 30728 | tf_op jit(solution)/shard_map/ppermute | solution.py:22
  60.6 1.3 %collective-permute-start.6 = (bf16[2,5,32,16]{3,2,1,0:T(8,128)(2,1)S(1)}, bf16[2,5,32,16]{3,2,1,0:T(8,128)(2,1)S(1)}, u32[]{:S(2)}, u32[]{:S(2)}) collective-permute-start(bf16[2,5,32,16]{3,2,1,0:T(8,128)(2,1)S(1)} %get-tuple-element.17), channel_id=1, source_target_pairs={{64,0},{128,64},{192,128},{65,1},{129,65},{193,129},{66,2},{130,66... | collective-permute-start | bytes 30728 | tf_op jit(solution)/shard_map/ppermute | solution.py:25
  62.1 4.0 %collective-permute-done.6 = bf16[2,5,32,16]{3,2,1,0:T(8,128)(2,1)S(1)} collective-permute-done((bf16[2,5,32,16]{3,2,1,0:T(8,128)(2,1)S(1)}, bf16[2,5,32,16]{3,2,1,0:T(8,128)(2,1)S(1)}, u32[]{:S(2)}, u32[]{:S(2)}) %collective-permute-start.6) | collective-permute-done | bytes 10272 | tf_op jit(solution)/shard_map/ppermute | solution.py:25
  66.3 3.0 %collective-permute-start.7 = (bf16[2,5,16,160]{3,2,1,0:T(8,128)(2,1)S(1)}, bf16[2,5,16,160]{3,2,1,0:T(8,128)(2,1)S(1)}, u32[]{:S(2)}, u32[]{:S(2)}) collective-permute-start(bf16[2,5,16,160]{3,2,1,0:T(8,128)(2,1)S(1)} %get-tuple-element.15), channel_id=1, source_target_pairs={{0,1},{1,2},{2,3},{3,4},{4,5},{5,6},{6,7},{7,8},{8,9},{9,10},{10,1... | collective-permute-start | bytes 153608 | tf_op jit(solution)/shard_map/ppermute | solution.py:22
  69.2 3.1 %collective-permute-start.8 = (bf16[2,5,16,160]{3,2,1,0:T(8,128)(2,1)S(1)}, bf16[2,5,16,160]{3,2,1,0:T(8,128)(2,1)S(1)}, u32[]{:S(2)}, u32[]{:S(2)}) collective-permute-start(bf16[2,5,16,160]{3,2,1,0:T(8,128)(2,1)S(1)} %get-tuple-element.14), channel_id=1, source_target_pairs={{1,0},{2,1},{3,2},{4,3},{5,4},{6,5},{7,6},{8,7},{9,8},{10,9},{11,1... | collective-permute-start | bytes 153608 | tf_op jit(solution)/shard_map/ppermute | solution.py:25
  72.3 1.0 %convert_bitcast_fusion = bf16[2,33,160,128,1]{3,1,0,2,4:T(8,128)(2,1)S(1)} fusion(bf16[2,33,33]{2,0,1:T(2,128)(2,1)S(1)} %rev.4), kind=kOutput, calls=%fused_computation.3 | convolution fusion | flops 91914240 | bytes 2707716 | tf_op jit(solution)/shard_map/kdv,vjc->kdjc/dot_general | solution.py:37
  73.4 7.9 %collective-permute-done.8 = bf16[2,5,16,160]{3,2,1,0:T(8,128)(2,1)S(1)} collective-permute-done((bf16[2,5,16,160]{3,2,1,0:T(8,128)(2,1)S(1)}, bf16[2,5,16,160]{3,2,1,0:T(8,128)(2,1)S(1)}, u32[]{:S(2)}, u32[]{:S(2)}) %collective-permute-start.8) | collective-permute-done | bytes 51232 | tf_op jit(solution)/shard_map/ppermute | solution.py:25
  83.2 1.6 %constant_dynamic-update-slice_fusion.7 = (f32[8,5,32,128]{3,2,1,0:T(8,128)S(1)}, f32[5,32,128,1,1]{2,1,0,4,3:T(8,128)S(1)}) fusion(bf16[2,5,33,32,160]{4,3,1,0,2:T(8,128)(2,1)S(1)} %fusion.12, bf16[2,33,160,128,1]{3,1,0,2,4:T(8,128)(2,1)S(1)} %convert_bitcast_fusion), kind=kOutput, calls=%fused_computation.112 | convolution fusion | flops 432537600 | bytes 6246400 | tf_op jit(solution)/shard_map/kbdrj,kdjc->brc/dot_general | solution.py:190
  85.1 3.5 %collective-permute-start.10 = (f32[5,32,128]{2,1,0:T(8,128)S(1)}, f32[5,32,128]{2,1,0:T(8,128)S(1)}, u32[]{:S(2)}, u32[]{:S(2)}) collective-permute-start(f32[5,32,128]{2,1,0:T(8,128)S(1)} %bitcast.207), channel_id=1, source_target_pairs={{0,128},{64,192},{128,0},{192,64},{1,129},{65,193},{129,1},{193,65... | collective-permute-start | bytes 245768 | tf_op jit(solution)/shard_map/ppermute | solution.py:199
  88.8 4.6 %collective-permute-done.10 = f32[5,32,128]{2,1,0:T(8,128)S(1)} collective-permute-done((f32[5,32,128]{2,1,0:T(8,128)S(1)}, f32[5,32,128]{2,1,0:T(8,128)S(1)}, u32[]{:S(2)}, u32[]{:S(2)}) %collective-permute-start.10) | collective-permute-done | bytes 81952 | tf_op jit(solution)/shard_map/ppermute | solution.py:199
  94.3 1.3 %exponential_multiply_fusion = f32[16,32,512]{2,1,0:T(8,128)} fusion(f32[16,32,512]{2,1,0:T(8,128)S(1)} %multiply_reduce_fusion, f32[16,32,512]{2,1,0:T(8,128)S(1)} %copy-done, f32[16]{0:T(128)S(1)} %get-tuple-element.20, f32[16]{0:T(128)S(1)} %get-tuple-element.21, f32[16]{0:T(128)S(1)} %copy-done.11), kind=kLoop, calls=%fused_computation.12 | loop fusion | flops 1048576 | bytes 3145920 | tf_op jit(solution)/shard_map/mul | solution.py:208
  (101 shorter events, 9.2 us)
Async XLA Ops:
  0.0 6.7 %copy-start.6 = (f32[4,64,128]{2,1,0:T(8,128)S(1)}, f32[4,64,128]{2,1,0:T(8,128)}, u32[]{:S(2)}) copy-start(f32[4,64,128]{2,1,0:T(8,128)} %param.18) | copy-start | bytes 393220
  0.0 6.7 %copy-start.10 = (s32[4,64]{1,0:T(4,128)S(1)}, s32[4,64]{1,0:T(4,128)}, u32[]{:S(2)}) copy-start(s32[4,64]{1,0:T(4,128)} %param.19) | copy-start | bytes 3076
  0.0 6.9 %copy-start.2 = (f32[2,4,64,128]{3,2,1,0:T(8,128)S(1)}, f32[2,4,64,128]{3,2,1,0:T(8,128)}, u32[]{:S(2)}) copy-start(f32[2,4,64,128]{3,2,1,0:T(8,128)} %param.17) | copy-start | bytes 786436
  0.0 7.1 %copy-start.4 = (s32[4,64,128]{2,1,0:T(8,128)S(1)}, s32[4,64,128]{2,1,0:T(8,128)}, u32[]{:S(2)}) copy-start(s32[4,64,128]{2,1,0:T(8,128)} %param.15) | copy-start | bytes 393220
  0.0 7.1 %copy-start.5 = (s32[4,64,128]{2,1,0:T(8,128)S(1)}, s32[4,64,128]{2,1,0:T(8,128)}, u32[]{:S(2)}) copy-start(s32[4,64,128]{2,1,0:T(8,128)} %param.16) | copy-start | bytes 393220
  2.3 26.8 %copy-start.7 = (bf16[2,33,33]{2,0,1:T(2,128)(2,1)S(1)}, bf16[2,33,33]{2,0,1:T(2,128)(2,1)}, u32[]{:S(2)}) copy-start(bf16[2,33,33]{2,0,1:T(2,128)(2,1)} %param.13) | copy-start | bytes 13072
  4.0 18.2 %collective-permute-start = (f32[5,32,160]{2,1,0:T(8,128)S(1)}, f32[5,32,160]{2,1,0:T(8,128)S(1)}, u32[]{:S(2)}, u32[]{:S(2)}) collective-permute-start(f32[5,32,160]{2,1,0:T(8,128)S(1)} %get-tuple-element.5), channel_id=1, source_target_pairs={{0,64},{64,128},{128,192},{192,0},{1,65},{65,129},{129,193},{193,1... | collective-permute-start | bytes 307208 | tf_op jit(solution)/shard_map/ppermute | solution.py:179
  4.1 18.2 %collective-permute-start.1 = (f32[5,32,160]{2,1,0:T(8,128)S(1)}, f32[5,32,160]{2,1,0:T(8,128)S(1)}, u32[]{:S(2)}, u32[]{:S(2)}) collective-permute-start(f32[5,32,160]{2,1,0:T(8,128)S(1)} %get-tuple-element.7), channel_id=1, source_target_pairs={{0,128},{64,192},{128,0},{192,64},{1,129},{65,193},{129,1},{193,65... | collective-permute-start | bytes 307208 | tf_op jit(solution)/shard_map/ppermute | solution.py:179
  5.4 16.9 %collective-permute-start.2 = (f32[5,32,160]{2,1,0:T(8,128)S(1)}, f32[5,32,160]{2,1,0:T(8,128)S(1)}, u32[]{:S(2)}, u32[]{:S(2)}) collective-permute-start(f32[5,32,160]{2,1,0:T(8,128)S(1)} %get-tuple-element.6), channel_id=1, source_target_pairs={{0,192},{64,0},{128,64},{192,128},{1,193},{65,1},{129,65},{193,129... | collective-permute-start | bytes 307208 | tf_op jit(solution)/shard_map/ppermute | solution.py:179
  8.4 24.0 %copy-start.9 = (s32[32,128]{1,0:T(8,128)S(1)}, s32[32,128]{1,0:T(8,128)}, u32[]{:S(2)}) copy-start(s32[32,128]{1,0:T(8,128)} %param.14) | copy-start | bytes 49156
  8.4 36.8 %all-to-all-start = ((f32[4,256,128]{2,0,1:T(4,128)}), f32[4,256,128]{2,0,1:T(4,128)S(1)}, u32[]{:S(2)}, u32[]{:S(2)}) async-start(f32[4,256,128]{2,0,1:T(4,128)} %pad_maximum_fusion.1), calls=%async_computation | async-start | bytes 1048576 | tf_op jit(solution)/shard_map/all_to_all | solution.py:158
  22.4 10.6 %collective-permute-start.3 = (bf16[5,16,160]{2,1,0:T(8,128)(2,1)S(1)}, bf16[5,16,160]{2,1,0:T(8,128)(2,1)S(1)}, u32[]{:S(2)}, u32[]{:S(2)}) collective-permute-start(bf16[5,16,160]{2,1,0:T(8,128)(2,1)S(1)} %get-tuple-element.18), channel_id=1, source_target_pairs={{0,1},{1,2},{2,3},{3,4},{4,5},{5,6},{6,7},{7,8},{8,9},{9,10},{10,1... | collective-permute-start | bytes 76808 | tf_op jit(solution)/shard_map/ppermute | solution.py:22
  27.0 11.6 %collective-permute-start.4 = (bf16[5,16,160]{2,1,0:T(8,128)(2,1)S(1)}, bf16[5,16,160]{2,1,0:T(8,128)(2,1)S(1)}, u32[]{:S(2)}, u32[]{:S(2)}) collective-permute-start(bf16[5,16,160]{2,1,0:T(8,128)(2,1)S(1)} %get-tuple-element.19), channel_id=1, source_target_pairs={{1,0},{2,1},{3,2},{4,3},{5,4},{6,5},{7,6},{8,7},{9,8},{10,9},{11,1... | collective-permute-start | bytes 76808 | tf_op jit(solution)/shard_map/ppermute | solution.py:25
  45.9 13.2 %copy-start.3 = (f32[2,5,32,128]{3,2,1,0:T(8,128)S(1)}, f32[2,5,32,128]{3,2,1,0:T(8,128)}, u32[]{:S(2)}) copy-start(f32[2,5,32,128]{3,2,1,0:T(8,128)} %shard_map.100) | copy-start | bytes 491524
  59.3 2.7 %collective-permute-start.5 = (bf16[2,5,32,16]{3,2,1,0:T(8,128)(2,1)S(1)}, bf16[2,5,32,16]{3,2,1,0:T(8,128)(2,1)S(1)}, u32[]{:S(2)}, u32[]{:S(2)}) collective-permute-start(bf16[2,5,32,16]{3,2,1,0:T(8,128)(2,1)S(1)} %get-tuple-element.16), channel_id=1, source_target_pairs={{0,64},{64,128},{128,192},{1,65},{65,129},{129,193},{2,66},{66,130... | collective-permute-start | bytes 30728 | tf_op jit(solution)/shard_map/ppermute | solution.py:22
  60.6 5.5 %collective-permute-start.6 = (bf16[2,5,32,16]{3,2,1,0:T(8,128)(2,1)S(1)}, bf16[2,5,32,16]{3,2,1,0:T(8,128)(2,1)S(1)}, u32[]{:S(2)}, u32[]{:S(2)}) collective-permute-start(bf16[2,5,32,16]{3,2,1,0:T(8,128)(2,1)S(1)} %get-tuple-element.17), channel_id=1, source_target_pairs={{64,0},{128,64},{192,128},{65,1},{129,65},{193,129},{66,2},{130,66... | collective-permute-start | bytes 30728 | tf_op jit(solution)/shard_map/ppermute | solution.py:25
  66.3 7.1 %collective-permute-start.7 = (bf16[2,5,16,160]{3,2,1,0:T(8,128)(2,1)S(1)}, bf16[2,5,16,160]{3,2,1,0:T(8,128)(2,1)S(1)}, u32[]{:S(2)}, u32[]{:S(2)}) collective-permute-start(bf16[2,5,16,160]{3,2,1,0:T(8,128)(2,1)S(1)} %get-tuple-element.15), channel_id=1, source_target_pairs={{0,1},{1,2},{2,3},{3,4},{4,5},{5,6},{6,7},{7,8},{8,9},{9,10},{10,1... | collective-permute-start | bytes 153608 | tf_op jit(solution)/shard_map/ppermute | solution.py:22
  69.2 12.1 %collective-permute-start.8 = (bf16[2,5,16,160]{3,2,1,0:T(8,128)(2,1)S(1)}, bf16[2,5,16,160]{3,2,1,0:T(8,128)(2,1)S(1)}, u32[]{:S(2)}, u32[]{:S(2)}) collective-permute-start(bf16[2,5,16,160]{3,2,1,0:T(8,128)(2,1)S(1)} %get-tuple-element.14), channel_id=1, source_target_pairs={{1,0},{2,1},{3,2},{4,3},{5,4},{6,5},{7,6},{8,7},{9,8},{10,9},{11,1... | collective-permute-start | bytes 153608 | tf_op jit(solution)/shard_map/ppermute | solution.py:25
  83.0 2.0 %copy-start.8 = (f32[5,16]{1,0:T(8,128)S(1)}, f32[5,16]{1,0:T(8,128)}, u32[]{:S(2)}) copy-start(f32[5,16]{1,0:T(8,128)} %param.12) | copy-start | bytes 964
  83.2 11.1 %copy-start = (f32[16,32,512]{2,1,0:T(8,128)S(1)}, f32[16,32,512]{2,1,0:T(8,128)}, u32[]{:S(2)}) copy-start(f32[16,32,512]{2,1,0:T(8,128)} %param.10) | copy-start | bytes 3145732
  83.2 11.1 %copy-start.11 = (f32[16]{0:T(128)S(1)}, f32[16]{0:T(128)}, u32[]{:S(2)}) copy-start(f32[16]{0:T(128)} %param.11) | copy-start | bytes 196
  84.9 3.9 %collective-permute-start.9 = (f32[5,32,128]{2,1,0:T(8,128)S(1)}, f32[5,32,128]{2,1,0:T(8,128)S(1)}, u32[]{:S(2)}, u32[]{:S(2)}) collective-permute-start(f32[5,32,128]{2,1,0:T(8,128)S(1)} %bitcast.206), channel_id=1, source_target_pairs={{0,192},{64,0},{128,64},{192,128},{1,193},{65,1},{129,65},{193,129... | collective-permute-start | bytes 245768 | tf_op jit(solution)/shard_map/ppermute | solution.py:199
  85.1 8.4 %collective-permute-start.10 = (f32[5,32,128]{2,1,0:T(8,128)S(1)}, f32[5,32,128]{2,1,0:T(8,128)S(1)}, u32[]{:S(2)}, u32[]{:S(2)}) collective-permute-start(f32[5,32,128]{2,1,0:T(8,128)S(1)} %bitcast.207), channel_id=1, source_target_pairs={{0,128},{64,192},{128,0},{192,64},{1,129},{65,193},{129,1},{193,65... | collective-permute-start | bytes 245768 | tf_op jit(solution)/shard_map/ppermute | solution.py:199
  88.6 4.8 %collective-permute-start.11 = (f32[5,32,128]{2,1,0:T(8,128)S(1)}, f32[5,32,128]{2,1,0:T(8,128)S(1)}, u32[]{:S(2)}, u32[]{:S(2)}) collective-permute-start(f32[5,32,128]{2,1,0:T(8,128)S(1)} %bitcast.208), channel_id=1, source_target_pairs={{0,64},{64,128},{128,192},{192,0},{1,65},{65,129},{129,193},{193,1... | collective-permute-start | bytes 245768 | tf_op jit(solution)/shard_map/ppermute | solution.py:199
  (1 other events, 0.8 us)

commit v12 on v10

--- a/solution.py
+++ b/solution.py
@@ -11,7 +11,7 @@
 NBIN = 5
 KER = 33
 HALF = 16
-CHUNK = 8192
+CHUNK = 32768
 
 
 def extended(block, sides, width):
@@ -160,7 +160,7 @@
     )
     sum_rows = 256
     sums = deposit_sums(arrived.reshape(4, -1), sum_rows, NBIN * pixels // sum_rows)
-    sums = lax.optimization_barrier(sums.reshape(3, NBIN, height, columns))
+    sums = sums.reshape(3, NBIN, height, columns)
     weight_sum = sums[0]
     shape_sum = sums[1:]
 
@@ -184,7 +184,7 @@
     shear = correlate_forward(padded, forward_bands, height)
     shear_grad = shear * weight_sum[None] - shape_sum
     masked = (shear_grad * star_mask.astype(jnp.float32)).astype(jnp.bfloat16)
-    rims = extended(masked, (("tile", 2), ("shell", 3)), HALF)
+    rims = extended(masked, (("shell", 3), ("tile", 2)), HALF)
     back_bands = build_bands(jnp.flip(shear_kernel, (1, 2)), columns)
     bin_grad = jnp.einsum(
         "kbdrj,kdjc->brc",

time: 97 us -> 95.6 us (0.986)
  starting transfers between devices: 38.1 us -> 35.5 us
    slice x0 -> x4, local copies, waits for them, and re-layouts: none -> 2.09 us  [the longest x2 1.17 us: per_device(): shape_sum = sums[1:]]
    ppermute x3, starting transfers between devices: 5.8 us -> 3.81 us  [per_device(): lax.ppermute(bin_grad, 'shell', [(i, (i + shift) % shell_count) for i in...]
    ppermute x3, starting transfers between devices: 10.4 us -> 8.87 us  [extended(): lax.ppermute(lax.slice_in_dim(block, block.shape[dim] - width, None, axis...]
    reshape x1 -> x0, local copies, waits for them, and re-layouts: 1.29 us -> none  [per_device(): sums = lax.optimization_barrier(sums.reshape(3, NBIN, height, columns))]
    unnamed x62 -> x61, local copies, waits for them, and re-layouts: 2.19 us -> 2.18 us
  transfers between devices with their start and end apart: 13 -> 13, of which waited for: 6 -> 5; matrix products, arithmetic and copies ran while one was open for 7% -> 7% of each run, Pallas kernels for 6% -> 6%
where the time goes in v12:
time: 95.6 us; the launch traced here: 95.1 us
  starting transfers between devices  35.5 us (37%)
  waiting for transfers between devices  23.1 us (24%)
  Pallas kernels  16.3 us (17%)
  other arithmetic  8.22 us (9%)
  local copies, waits for them, and re-layouts  7.5 us (8%)
  matrix products  3.64 us (4%)
    ppermute x3, waiting for transfers between devices, extended(): lax.ppermute(lax.slice_in_dim(block, 0, width, axis=dim), axis, backward)  17.9 us
    all_to_all x1, starting transfers between devices, per_device(): lax.all_to_all(packet.reshape(4, devices, -1), ('shell', 'tile'), split_a...  13.9 us
    pallas_call x1, Pallas kernels, deposit_sums(): pl.pallas_call(functools.partial(scatter_kernel, rows, columns), out_shap...  10.4 us
    ppermute x3, starting transfers between devices, extended(): lax.ppermute(lax.slice_in_dim(block, block.shape[dim] - width, None, axis...  8.87 us
    ppermute x3, starting transfers between devices, extended(): lax.ppermute(lax.slice_in_dim(block, 0, width, axis=dim), axis, backward)  6.27 us
    pallas_call x1, Pallas kernels, correlate_forward(): pl.pallas_call(correlate_kernel, out_shape=jax.ShapeDtypeStruct((kinds, b...  5.86 us
    ppermute x3, waiting for transfers between devices, per_device(): lax.ppermute(bin_grad, 'shell', [(i, (i + shift) % shell_count) for i in...  4.64 us
    ppermute x3, starting transfers between devices, per_device(): lax.ppermute(bin_grad, 'shell', [(i, (i + shift) % shell_count) for i in...  3.81 us
  transfers between devices with their start and end apart: 13, of which 5 were waited for; matrix products, arithmetic and copies ran while one was open for 7% of the time, Pallas kernels for 6%

profile of v12, /device:TPU:124, one launch (start us, length us, event | category | flops | bytes accessed | tf_op | source)
XLA Modules:
  0.0 95.1 jit_solution(7019445914151368530)
XLA Ops:
  0.8 1.5 %fusion.10 = f32[16,32,512]{2,1,0:T(8,128)S(1)} fusion(f32[16,32,512]{2,1,0:T(8,128)} %param.10, f32[16]{0:T(128)S(1)} %multiply_multiply_fusion.1, f32[16]{0:T(128)} %param.11), kind=kLoop, calls=%fused_computation.13 | loop fusion | flops 786432 | bytes 2097280 | tf_op jit(solution)/shard_map/sub | solution.py:169
  2.3 1.3 %multiply_reduce_fusion.1 = f32[5,32,512]{2,1,0:T(8,128)S(1)} fusion(f32[16,32,512]{2,1,0:T(8,128)S(1)} %fusion.10, f32[5,16]{1,0:T(8,128)} %param.12), kind=kLoop, calls=%fused_computation.2 | loop fusion | flops 2539520 | bytes 1376576 | tf_op jit(solution)/shard_map/reduce_sum | solution.py:169
  4.1 1.3 %collective-permute-start.1 = (f32[5,32,160]{2,1,0:T(8,128)S(1)}, f32[5,32,160]{2,1,0:T(8,128)S(1)}, u32[]{:S(2)}, u32[]{:S(2)}) collective-permute-start(f32[5,32,160]{2,1,0:T(8,128)S(1)} %get-tuple-element.7), channel_id=1, source_target_pairs={{0,128},{64,192},{128,0},{192,64},{1,129},{65,193},{129,1},{193,65... | collective-permute-start | bytes 307208 | tf_op jit(solution)/shard_map/ppermute | solution.py:178
  5.4 1.4 %collective-permute-start.2 = (f32[5,32,160]{2,1,0:T(8,128)S(1)}, f32[5,32,160]{2,1,0:T(8,128)S(1)}, u32[]{:S(2)}, u32[]{:S(2)}) collective-permute-start(f32[5,32,160]{2,1,0:T(8,128)S(1)} %get-tuple-element.6), channel_id=1, source_target_pairs={{0,192},{64,0},{128,64},{192,128},{1,193},{65,1},{129,65},{193,129... | collective-permute-start | bytes 307208 | tf_op jit(solution)/shard_map/ppermute | solution.py:178
  7.2 1.1 %pad_maximum_fusion.1 = f32[4,256,128]{2,0,1:T(4,128)} fusion(f32[2,256,128]{2,0,1:T(2,128)S(1)} %bitcast.203, f32[1,256,128]{2,0,1:T(1,128)S(1)} %bitcast.202, f32[1,256,128]{2,0,1:T(1,128)S(1)} %bitcast.205), kind=kLoop, calls=%fused_computation.15 | loop fusion | flops 262144 | bytes 1048576 | tf_op jit(solution)/shard_map/concatenate | solution.py:154
  8.4 13.9 %all-to-all-start = ((f32[4,256,128]{2,0,1:T(4,128)}), f32[4,256,128]{2,0,1:T(4,128)S(1)}, u32[]{:S(2)}, u32[]{:S(2)}) async-start(f32[4,256,128]{2,0,1:T(4,128)} %pad_maximum_fusion.1), calls=%async_computation | async-start | bytes 1048576 | tf_op jit(solution)/shard_map/all_to_all | solution.py:158
  22.4 4.6 %collective-permute-start.3 = (bf16[5,16,160]{2,1,0:T(8,128)(2,1)S(1)}, bf16[5,16,160]{2,1,0:T(8,128)(2,1)S(1)}, u32[]{:S(2)}, u32[]{:S(2)}) collective-permute-start(bf16[5,16,160]{2,1,0:T(8,128)(2,1)S(1)} %get-tuple-element.18), channel_id=1, source_target_pairs={{0,1},{1,2},{2,3},{3,4},{4,5},{5,6},{6,7},{7,8},{8,9},{9,10},{10,1... | collective-permute-start | bytes 76808 | tf_op jit(solution)/shard_map/ppermute | solution.py:22
  27.0 2.1 %collective-permute-start.4 = (bf16[5,16,160]{2,1,0:T(8,128)(2,1)S(1)}, bf16[5,16,160]{2,1,0:T(8,128)(2,1)S(1)}, u32[]{:S(2)}, u32[]{:S(2)}) collective-permute-start(bf16[5,16,160]{2,1,0:T(8,128)(2,1)S(1)} %get-tuple-element.19), channel_id=1, source_target_pairs={{1,0},{2,1},{3,2},{4,3},{5,4},{6,5},{7,6},{8,7},{9,8},{10,9},{11,1... | collective-permute-start | bytes 76808 | tf_op jit(solution)/shard_map/ppermute | solution.py:25
  29.1 1.0 %fusion.3 = bf16[160,128,2,33]{1,3,2,0:T(8,128)(2,1)S(1)} fusion(bf16[2,33,33]{2,0,1:T(2,128)(2,1)S(1)} %copy-done.7), kind=kOutput, calls=%fused_computation.7 | convolution fusion | flops 90562560 | bytes 2707716 | tf_op jit(solution)/shard_map/kdv,vjc->kdjc/dot_general | solution.py:37
  30.1 2.2 %copy.56 = bf16[160,128,2,33]{1,0,3,2:T(8,128)(2,1)} copy(bf16[160,128,2,33]{1,3,2,0:T(8,128)(2,1)S(1)} %fusion.3) | data formatting | bytes 5406720 | tf_op jit(solution)/shard_map/kdv,vjc->kdjc/dot_general | solution.py:37
  32.9 5.7 %collective-permute-done.4 = bf16[5,16,160]{2,1,0:T(8,128)(2,1)S(1)} collective-permute-done((bf16[5,16,160]{2,1,0:T(8,128)(2,1)S(1)}, bf16[5,16,160]{2,1,0:T(8,128)(2,1)S(1)}, u32[]{:S(2)}, u32[]{:S(2)}) %collective-permute-start.4) | collective-permute-done | bytes 25632 | tf_op jit(solution)/shard_map/ppermute | solution.py:25
  39.3 5.9 %shard_map.100 = f32[2,5,32,128]{3,2,1,0:T(8,128)} custom-call(bf16[5,64,160]{2,1,0:T(8,128)(2,1)} %pad_maximum_fusion.3.x_ref, bf16[2,33,160,128]{3,2,1,0:T(8,128)(2,1)} %bitcast.201), custom_call_target="tpu_custom_call" | custom-call | flops 865075200 | bytes 2969600 | tf_op jit(solution)/shard_map/pallas_call | solution.py:118
  46.0 10.4 %shard_map.101 = f32[3,256,80]{2,1,0:T(8,128)} custom-call(f32[4,32768]{1,0:T(4,128)} %bitcast.204), custom_call_target="tpu_custom_call" | custom-call | flops 8053063680 | bytes 770048 | tf_op jit(solution)/shard_map/pallas_call | solution.py:89
  58.8 1.3 %collective-permute-start.5 = (bf16[2,5,32,16]{3,2,1,0:T(8,128)(2,1)S(1)}, bf16[2,5,32,16]{3,2,1,0:T(8,128)(2,1)S(1)}, u32[]{:S(2)}, u32[]{:S(2)}) collective-permute-start(bf16[2,5,32,16]{3,2,1,0:T(8,128)(2,1)S(1)} %get-tuple-element.16), channel_id=1, source_target_pairs={{0,64},{64,128},{128,192},{1,65},{65,129},{129,193},{2,66},{66,130... | collective-permute-start | bytes 30728 | tf_op jit(solution)/shard_map/ppermute | solution.py:22
  60.1 1.3 %collective-permute-start.6 = (bf16[2,5,32,16]{3,2,1,0:T(8,128)(2,1)S(1)}, bf16[2,5,32,16]{3,2,1,0:T(8,128)(2,1)S(1)}, u32[]{:S(2)}, u32[]{:S(2)}) collective-permute-start(bf16[2,5,32,16]{3,2,1,0:T(8,128)(2,1)S(1)} %get-tuple-element.17), channel_id=1, source_target_pairs={{64,0},{128,64},{192,128},{65,1},{129,65},{193,129},{66,2},{130,66... | collective-permute-start | bytes 30728 | tf_op jit(solution)/shard_map/ppermute | solution.py:25
  61.5 4.0 %collective-permute-done.6 = bf16[2,5,32,16]{3,2,1,0:T(8,128)(2,1)S(1)} collective-permute-done((bf16[2,5,32,16]{3,2,1,0:T(8,128)(2,1)S(1)}, bf16[2,5,32,16]{3,2,1,0:T(8,128)(2,1)S(1)}, u32[]{:S(2)}, u32[]{:S(2)}) %collective-permute-start.6) | collective-permute-done | bytes 10272 | tf_op jit(solution)/shard_map/ppermute | solution.py:25
  65.7 3.0 %collective-permute-start.7 = (bf16[2,5,16,160]{3,2,1,0:T(8,128)(2,1)S(1)}, bf16[2,5,16,160]{3,2,1,0:T(8,128)(2,1)S(1)}, u32[]{:S(2)}, u32[]{:S(2)}) collective-permute-start(bf16[2,5,16,160]{3,2,1,0:T(8,128)(2,1)S(1)} %get-tuple-element.15), channel_id=1, source_target_pairs={{0,1},{1,2},{2,3},{3,4},{4,5},{5,6},{6,7},{7,8},{8,9},{9,10},{10,1... | collective-permute-start | bytes 153608 | tf_op jit(solution)/shard_map/ppermute | solution.py:22
  68.7 2.9 %collective-permute-start.8 = (bf16[2,5,16,160]{3,2,1,0:T(8,128)(2,1)S(1)}, bf16[2,5,16,160]{3,2,1,0:T(8,128)(2,1)S(1)}, u32[]{:S(2)}, u32[]{:S(2)}) collective-permute-start(bf16[2,5,16,160]{3,2,1,0:T(8,128)(2,1)S(1)} %get-tuple-element.14), channel_id=1, source_target_pairs={{1,0},{2,1},{3,2},{4,3},{5,4},{6,5},{7,6},{8,7},{9,8},{10,9},{11,1... | collective-permute-start | bytes 153608 | tf_op jit(solution)/shard_map/ppermute | solution.py:25
  71.6 1.0 %convert_bitcast_fusion = bf16[2,33,160,128,1]{3,1,0,2,4:T(8,128)(2,1)S(1)} fusion(bf16[2,33,33]{2,0,1:T(2,128)(2,1)S(1)} %rev.4), kind=kOutput, calls=%fused_computation.3 | convolution fusion | flops 91914240 | bytes 2707716 | tf_op jit(solution)/shard_map/kdv,vjc->kdjc/dot_general | solution.py:37
  72.6 8.1 %collective-permute-done.8 = bf16[2,5,16,160]{3,2,1,0:T(8,128)(2,1)S(1)} collective-permute-done((bf16[2,5,16,160]{3,2,1,0:T(8,128)(2,1)S(1)}, bf16[2,5,16,160]{3,2,1,0:T(8,128)(2,1)S(1)}, u32[]{:S(2)}, u32[]{:S(2)}) %collective-permute-start.8) | collective-permute-done | bytes 51232 | tf_op jit(solution)/shard_map/ppermute | solution.py:25
  82.7 1.6 %constant_dynamic-update-slice_fusion.7 = (f32[8,5,32,128]{3,2,1,0:T(8,128)S(1)}, f32[5,32,128,1,1]{2,1,0,4,3:T(8,128)S(1)}) fusion(bf16[2,5,33,32,160]{4,3,1,0,2:T(8,128)(2,1)S(1)} %fusion.13, bf16[2,33,160,128,1]{3,1,0,2,4:T(8,128)(2,1)S(1)} %convert_bitcast_fusion), kind=kOutput, calls=%fused_computation.112 | convolution fusion | flops 432537600 | bytes 6246400 | tf_op jit(solution)/shard_map/kbdrj,kdjc->brc/dot_general | solution.py:189
  84.5 3.5 %collective-permute-start.10 = (f32[5,32,128]{2,1,0:T(8,128)S(1)}, f32[5,32,128]{2,1,0:T(8,128)S(1)}, u32[]{:S(2)}, u32[]{:S(2)}) collective-permute-start(f32[5,32,128]{2,1,0:T(8,128)S(1)} %bitcast.207), channel_id=1, source_target_pairs={{0,128},{64,192},{128,0},{192,64},{1,129},{65,193},{129,1},{193,65... | collective-permute-start | bytes 245768 | tf_op jit(solution)/shard_map/ppermute | solution.py:198
  88.3 4.6 %collective-permute-done.10 = f32[5,32,128]{2,1,0:T(8,128)S(1)} collective-permute-done((f32[5,32,128]{2,1,0:T(8,128)S(1)}, f32[5,32,128]{2,1,0:T(8,128)S(1)}, u32[]{:S(2)}, u32[]{:S(2)}) %collective-permute-start.10) | collective-permute-done | bytes 81952 | tf_op jit(solution)/shard_map/ppermute | solution.py:198
  93.8 1.3 %multiply_multiply_fusion = f32[16,32,512]{2,1,0:T(8,128)} fusion(f32[16,32,512]{2,1,0:T(8,128)S(1)} %multiply_reduce_fusion, f32[16,32,512]{2,1,0:T(8,128)S(1)} %copy-done, f32[16]{0:T(128)S(1)} %multiply_multiply_fusion.1, f32[16]{0:T(128)S(1)} %copy-done.11), kind=kLoop, calls=%fused_computation.11 | loop fusion | flops 1048576 | bytes 3145856 | tf_op jit(solution)/shard_map/mul | solution.py:207
  (101 shorter events, 9.2 us)
Async XLA Ops:
  0.0 6.7 %copy-start.6 = (f32[4,64,128]{2,1,0:T(8,128)S(1)}, f32[4,64,128]{2,1,0:T(8,128)}, u32[]{:S(2)}) copy-start(f32[4,64,128]{2,1,0:T(8,128)} %param.18) | copy-start | bytes 393220
  0.0 6.7 %copy-start.10 = (s32[4,64]{1,0:T(4,128)S(1)}, s32[4,64]{1,0:T(4,128)}, u32[]{:S(2)}) copy-start(s32[4,64]{1,0:T(4,128)} %param.19) | copy-start | bytes 3076
  0.0 6.9 %copy-start.2 = (f32[2,4,64,128]{3,2,1,0:T(8,128)S(1)}, f32[2,4,64,128]{3,2,1,0:T(8,128)}, u32[]{:S(2)}) copy-start(f32[2,4,64,128]{3,2,1,0:T(8,128)} %param.17) | copy-start | bytes 786436
  0.0 7.1 %copy-start.4 = (s32[4,64,128]{2,1,0:T(8,128)S(1)}, s32[4,64,128]{2,1,0:T(8,128)}, u32[]{:S(2)}) copy-start(s32[4,64,128]{2,1,0:T(8,128)} %param.15) | copy-start | bytes 393220
  0.0 7.1 %copy-start.5 = (s32[4,64,128]{2,1,0:T(8,128)S(1)}, s32[4,64,128]{2,1,0:T(8,128)}, u32[]{:S(2)}) copy-start(s32[4,64,128]{2,1,0:T(8,128)} %param.16) | copy-start | bytes 393220
  2.3 26.8 %copy-start.7 = (bf16[2,33,33]{2,0,1:T(2,128)(2,1)S(1)}, bf16[2,33,33]{2,0,1:T(2,128)(2,1)}, u32[]{:S(2)}) copy-start(bf16[2,33,33]{2,0,1:T(2,128)(2,1)} %param.13) | copy-start | bytes 13072
  4.0 18.2 %collective-permute-start = (f32[5,32,160]{2,1,0:T(8,128)S(1)}, f32[5,32,160]{2,1,0:T(8,128)S(1)}, u32[]{:S(2)}, u32[]{:S(2)}) collective-permute-start(f32[5,32,160]{2,1,0:T(8,128)S(1)} %get-tuple-element.5), channel_id=1, source_target_pairs={{0,64},{64,128},{128,192},{192,0},{1,65},{65,129},{129,193},{193,1... | collective-permute-start | bytes 307208 | tf_op jit(solution)/shard_map/ppermute | solution.py:178
  4.1 18.2 %collective-permute-start.1 = (f32[5,32,160]{2,1,0:T(8,128)S(1)}, f32[5,32,160]{2,1,0:T(8,128)S(1)}, u32[]{:S(2)}, u32[]{:S(2)}) collective-permute-start(f32[5,32,160]{2,1,0:T(8,128)S(1)} %get-tuple-element.7), channel_id=1, source_target_pairs={{0,128},{64,192},{128,0},{192,64},{1,129},{65,193},{129,1},{193,65... | collective-permute-start | bytes 307208 | tf_op jit(solution)/shard_map/ppermute | solution.py:178
  5.4 16.9 %collective-permute-start.2 = (f32[5,32,160]{2,1,0:T(8,128)S(1)}, f32[5,32,160]{2,1,0:T(8,128)S(1)}, u32[]{:S(2)}, u32[]{:S(2)}) collective-permute-start(f32[5,32,160]{2,1,0:T(8,128)S(1)} %get-tuple-element.6), channel_id=1, source_target_pairs={{0,192},{64,0},{128,64},{192,128},{1,193},{65,1},{129,65},{193,129... | collective-permute-start | bytes 307208 | tf_op jit(solution)/shard_map/ppermute | solution.py:178
  8.4 24.0 %copy-start.9 = (s32[32,128]{1,0:T(8,128)S(1)}, s32[32,128]{1,0:T(8,128)}, u32[]{:S(2)}) copy-start(s32[32,128]{1,0:T(8,128)} %param.14) | copy-start | bytes 49156
  8.4 36.8 %all-to-all-start = ((f32[4,256,128]{2,0,1:T(4,128)}), f32[4,256,128]{2,0,1:T(4,128)S(1)}, u32[]{:S(2)}, u32[]{:S(2)}) async-start(f32[4,256,128]{2,0,1:T(4,128)} %pad_maximum_fusion.1), calls=%async_computation | async-start | bytes 1048576 | tf_op jit(solution)/shard_map/all_to_all | solution.py:158
  22.4 10.6 %collective-permute-start.3 = (bf16[5,16,160]{2,1,0:T(8,128)(2,1)S(1)}, bf16[5,16,160]{2,1,0:T(8,128)(2,1)S(1)}, u32[]{:S(2)}, u32[]{:S(2)}) collective-permute-start(bf16[5,16,160]{2,1,0:T(8,128)(2,1)S(1)} %get-tuple-element.18), channel_id=1, source_target_pairs={{0,1},{1,2},{2,3},{3,4},{4,5},{5,6},{6,7},{7,8},{8,9},{9,10},{10,1... | collective-permute-start | bytes 76808 | tf_op jit(solution)/shard_map/ppermute | solution.py:22
  27.0 11.6 %collective-permute-start.4 = (bf16[5,16,160]{2,1,0:T(8,128)(2,1)S(1)}, bf16[5,16,160]{2,1,0:T(8,128)(2,1)S(1)}, u32[]{:S(2)}, u32[]{:S(2)}) collective-permute-start(bf16[5,16,160]{2,1,0:T(8,128)(2,1)S(1)} %get-tuple-element.19), channel_id=1, source_target_pairs={{1,0},{2,1},{3,2},{4,3},{5,4},{6,5},{7,6},{8,7},{9,8},{10,9},{11,1... | collective-permute-start | bytes 76808 | tf_op jit(solution)/shard_map/ppermute | solution.py:25
  46.0 12.7 %copy-start.3 = (f32[2,5,32,128]{3,2,1,0:T(8,128)S(1)}, f32[2,5,32,128]{3,2,1,0:T(8,128)}, u32[]{:S(2)}) copy-start(f32[2,5,32,128]{3,2,1,0:T(8,128)} %shard_map.100) | copy-start | bytes 491524
  58.8 2.7 %collective-permute-start.5 = (bf16[2,5,32,16]{3,2,1,0:T(8,128)(2,1)S(1)}, bf16[2,5,32,16]{3,2,1,0:T(8,128)(2,1)S(1)}, u32[]{:S(2)}, u32[]{:S(2)}) collective-permute-start(bf16[2,5,32,16]{3,2,1,0:T(8,128)(2,1)S(1)} %get-tuple-element.16), channel_id=1, source_target_pairs={{0,64},{64,128},{128,192},{1,65},{65,129},{129,193},{2,66},{66,130... | collective-permute-start | bytes 30728 | tf_op jit(solution)/shard_map/ppermute | solution.py:22
  60.1 5.5 %collective-permute-start.6 = (bf16[2,5,32,16]{3,2,1,0:T(8,128)(2,1)S(1)}, bf16[2,5,32,16]{3,2,1,0:T(8,128)(2,1)S(1)}, u32[]{:S(2)}, u32[]{:S(2)}) collective-permute-start(bf16[2,5,32,16]{3,2,1,0:T(8,128)(2,1)S(1)} %get-tuple-element.17), channel_id=1, source_target_pairs={{64,0},{128,64},{192,128},{65,1},{129,65},{193,129},{66,2},{130,66... | collective-permute-start | bytes 30728 | tf_op jit(solution)/shard_map/ppermute | solution.py:25
  65.7 6.9 %collective-permute-start.7 = (bf16[2,5,16,160]{3,2,1,0:T(8,128)(2,1)S(1)}, bf16[2,5,16,160]{3,2,1,0:T(8,128)(2,1)S(1)}, u32[]{:S(2)}, u32[]{:S(2)}) collective-permute-start(bf16[2,5,16,160]{3,2,1,0:T(8,128)(2,1)S(1)} %get-tuple-element.15), channel_id=1, source_target_pairs={{0,1},{1,2},{2,3},{3,4},{4,5},{5,6},{6,7},{7,8},{8,9},{9,10},{10,1... | collective-permute-start | bytes 153608 | tf_op jit(solution)/shard_map/ppermute | solution.py:22
  68.7 12.1 %collective-permute-start.8 = (bf16[2,5,16,160]{3,2,1,0:T(8,128)(2,1)S(1)}, bf16[2,5,16,160]{3,2,1,0:T(8,128)(2,1)S(1)}, u32[]{:S(2)}, u32[]{:S(2)}) collective-permute-start(bf16[2,5,16,160]{3,2,1,0:T(8,128)(2,1)S(1)} %get-tuple-element.14), channel_id=1, source_target_pairs={{1,0},{2,1},{3,2},{4,3},{5,4},{6,5},{7,6},{8,7},{9,8},{10,9},{11,1... | collective-permute-start | bytes 153608 | tf_op jit(solution)/shard_map/ppermute | solution.py:25
  82.4 2.0 %copy-start.8 = (f32[5,16]{1,0:T(8,128)S(1)}, f32[5,16]{1,0:T(8,128)}, u32[]{:S(2)}) copy-start(f32[5,16]{1,0:T(8,128)} %param.12) | copy-start | bytes 964
  82.7 11.1 %copy-start = (f32[16,32,512]{2,1,0:T(8,128)S(1)}, f32[16,32,512]{2,1,0:T(8,128)}, u32[]{:S(2)}) copy-start(f32[16,32,512]{2,1,0:T(8,128)} %param.10) | copy-start | bytes 3145732
  82.7 11.1 %copy-start.11 = (f32[16]{0:T(128)S(1)}, f32[16]{0:T(128)}, u32[]{:S(2)}) copy-start(f32[16]{0:T(128)} %param.11) | copy-start | bytes 196
  84.3 3.9 %collective-permute-start.9 = (f32[5,32,128]{2,1,0:T(8,128)S(1)}, f32[5,32,128]{2,1,0:T(8,128)S(1)}, u32[]{:S(2)}, u32[]{:S(2)}) collective-permute-start(f32[5,32,128]{2,1,0:T(8,128)S(1)} %bitcast.206), channel_id=1, source_target_pairs={{0,192},{64,0},{128,64},{192,128},{1,193},{65,1},{129,65},{193,129... | collective-permute-start | bytes 245768 | tf_op jit(solution)/shard_map/ppermute | solution.py:198
  84.5 8.4 %collective-permute-start.10 = (f32[5,32,128]{2,1,0:T(8,128)S(1)}, f32[5,32,128]{2,1,0:T(8,128)S(1)}, u32[]{:S(2)}, u32[]{:S(2)}) collective-permute-start(f32[5,32,128]{2,1,0:T(8,128)S(1)} %bitcast.207), channel_id=1, source_target_pairs={{0,128},{64,192},{128,0},{192,64},{1,129},{65,193},{129,1},{193,65... | collective-permute-start | bytes 245768 | tf_op jit(solution)/shard_map/ppermute | solution.py:198
  88.1 4.8 %collective-permute-start.11 = (f32[5,32,128]{2,1,0:T(8,128)S(1)}, f32[5,32,128]{2,1,0:T(8,128)S(1)}, u32[]{:S(2)}, u32[]{:S(2)}) collective-permute-start(f32[5,32,128]{2,1,0:T(8,128)S(1)} %bitcast.208), channel_id=1, source_target_pairs={{0,64},{64,128},{128,192},{192,0},{1,65},{65,129},{129,193},{193,1... | collective-permute-start | bytes 245768 | tf_op jit(solution)/shard_map/ppermute | solution.py:198
  (1 other events, 0.8 us)

commit v13 on v12

--- a/solution.py
+++ b/solution.py
@@ -192,17 +192,7 @@
         back_bands,
         preferred_element_type=jnp.float32,
     )
-    received = [bin_grad]
-    for shift in range(1, shell_count):
-        received.append(
-            lax.ppermute(
-                bin_grad, "shell", [(i, (i + shift) % shell_count) for i in range(shell_count)]
-            )
-        )
-    by_offset = jnp.stack([received[(-j) % shell_count] for j in range(shell_count)])
-    twice = jnp.concatenate([by_offset, by_offset], axis=0)
-    blocks = lax.dynamic_slice_in_dim(twice, (shell_count - me) % shell_count, shell_count, 0)
-    full_grad = jnp.transpose(blocks, (1, 2, 0, 3)).reshape(NBIN, height, width)
+    full_grad = lax.all_gather(bin_grad, "shell", axis=2, tiled=True)
     mixed = jnp.sum(lens_weight.T[:, :, None, None] * full_grad[None], axis=1)
     return sigma * growth * mixed
 

time: 95.6 us -> 97.6 us (1.021)
  blocking collectives: 0 us -> 8.13 us
  waiting for transfers between devices: 23.1 us -> 18.7 us
  starting transfers between devices: 35.5 us -> 31.7 us
    all_gather x0 -> x1, blocking collectives: none -> 8.13 us  [per_device(): full_grad = lax.all_gather(bin_grad, 'shell', axis=2, tiled=True)]
    ppermute x3 -> x0, waiting for transfers between devices: 4.64 us -> none  [per_device(): lax.ppermute(bin_grad, 'shell', [(i, (i + shift) % shell_count) for i in...]
    ppermute x3 -> x0, starting transfers between devices: 3.81 us -> none  [per_device(): lax.ppermute(bin_grad, 'shell', [(i, (i + shift) % shell_count) for i in...]
    unnamed x61 -> x55, local copies, waits for them, and re-layouts: 2.18 us -> 2.13 us
  transfers between devices with their start and end apart: 13 -> 10, of which waited for: 5 -> 4; matrix products, arithmetic and copies ran while one was open for 7% -> 7% of each run, Pallas kernels for 6% -> 6%
where the time goes in v13:
time: 97.6 us; the launch traced here: 96.3 us
  starting transfers between devices  31.7 us (32%)
  waiting for transfers between devices  18.7 us (19%)
  Pallas kernels  16.3 us (17%)
  other arithmetic  9.14 us (9%)
  blocking collectives  8.13 us (8%)
  local copies, waits for them, and re-layouts  8.08 us (8%)
  matrix products  3.59 us (4%)
    ppermute x3, waiting for transfers between devices, extended(): lax.ppermute(lax.slice_in_dim(block, 0, width, axis=dim), axis, backward)  18.1 us
    all_to_all x1, starting transfers between devices, per_device(): lax.all_to_all(packet.reshape(4, devices, -1), ('shell', 'tile'), split_a...  13.9 us
    pallas_call x1, Pallas kernels, deposit_sums(): pl.pallas_call(functools.partial(scatter_kernel, rows, columns), out_shap...  10.4 us
    ppermute x3, starting transfers between devices, extended(): lax.ppermute(lax.slice_in_dim(block, block.shape[dim] - width, None, axis...  8.86 us
    all_gather x1, blocking collectives, per_device(): full_grad = lax.all_gather(bin_grad, 'shell', axis=2, tiled=True)  8.13 us
    ppermute x3, starting transfers between devices, extended(): lax.ppermute(lax.slice_in_dim(block, 0, width, axis=dim), axis, backward)  6.28 us
    pallas_call x1, Pallas kernels, correlate_forward(): pl.pallas_call(correlate_kernel, out_shape=jax.ShapeDtypeStruct((kinds, b...  5.88 us
    ppermute x3, starting transfers between devices, per_device(): lax.ppermute(outgoing, 'shell', [(i, (i + shift) % shell_count) for i in...  2.73 us
  transfers between devices with their start and end apart: 10, of which 4 were waited for; matrix products, arithmetic and copies ran while one was open for 7% of the time, Pallas kernels for 6%

profile of v13, /device:TPU:124, one launch (start us, length us, event | category | flops | bytes accessed | tf_op | source)
XLA Modules:
  0.0 96.3 jit_solution(4546065988315962593)
XLA Ops:
  0.8 1.5 %fusion.13 = f32[16,32,512]{2,1,0:T(8,128)S(1)} fusion(f32[16,32,512]{2,1,0:T(8,128)} %param.10, f32[16]{0:T(128)S(1)} %multiply_multiply_fusion.1, f32[16]{0:T(128)} %param.11), kind=kLoop, calls=%fused_computation.14 | loop fusion | flops 786432 | bytes 2097280 | tf_op jit(solution)/shard_map/sub | solution.py:169
  2.3 1.3 %multiply_reduce_fusion.1 = f32[5,32,512]{2,1,0:T(8,128)S(1)} fusion(f32[16,32,512]{2,1,0:T(8,128)S(1)} %fusion.13, f32[5,16]{1,0:T(8,128)} %param.12), kind=kLoop, calls=%fused_computation.2 | loop fusion | flops 2539520 | bytes 1376576 | tf_op jit(solution)/shard_map/reduce_sum | solution.py:169
  4.1 1.3 %collective-permute-start.1 = (f32[5,32,160]{2,1,0:T(8,128)S(1)}, f32[5,32,160]{2,1,0:T(8,128)S(1)}, u32[]{:S(2)}, u32[]{:S(2)}) collective-permute-start(f32[5,32,160]{2,1,0:T(8,128)S(1)} %get-tuple-element.7), channel_id=1, source_target_pairs={{0,128},{64,192},{128,0},{192,64},{1,129},{65,193},{129,1},{193,65... | collective-permute-start | bytes 307208 | tf_op jit(solution)/shard_map/ppermute | solution.py:178
  5.4 1.4 %collective-permute-start.2 = (f32[5,32,160]{2,1,0:T(8,128)S(1)}, f32[5,32,160]{2,1,0:T(8,128)S(1)}, u32[]{:S(2)}, u32[]{:S(2)}) collective-permute-start(f32[5,32,160]{2,1,0:T(8,128)S(1)} %get-tuple-element.6), channel_id=1, source_target_pairs={{0,192},{64,0},{128,64},{192,128},{1,193},{65,1},{129,65},{193,129... | collective-permute-start | bytes 307208 | tf_op jit(solution)/shard_map/ppermute | solution.py:178
  7.2 1.1 %pad_maximum_fusion.1 = f32[4,256,128]{2,0,1:T(4,128)} fusion(f32[2,256,128]{2,0,1:T(2,128)S(1)} %bitcast.185, f32[1,256,128]{2,0,1:T(1,128)S(1)} %bitcast.184, f32[1,256,128]{2,0,1:T(1,128)S(1)} %bitcast.187), kind=kLoop, calls=%fused_computation.16 | loop fusion | flops 262144 | bytes 1048576 | tf_op jit(solution)/shard_map/concatenate | solution.py:154
  8.4 13.9 %all-to-all-start = ((f32[4,256,128]{2,0,1:T(4,128)}), f32[4,256,128]{2,0,1:T(4,128)S(1)}, u32[]{:S(2)}, u32[]{:S(2)}) async-start(f32[4,256,128]{2,0,1:T(4,128)} %pad_maximum_fusion.1), calls=%async_computation | async-start | bytes 1048576 | tf_op jit(solution)/shard_map/all_to_all | solution.py:158
  22.4 4.6 %collective-permute-start.3 = (bf16[5,16,160]{2,1,0:T(8,128)(2,1)S(1)}, bf16[5,16,160]{2,1,0:T(8,128)(2,1)S(1)}, u32[]{:S(2)}, u32[]{:S(2)}) collective-permute-start(bf16[5,16,160]{2,1,0:T(8,128)(2,1)S(1)} %get-tuple-element.18), channel_id=1, source_target_pairs={{0,1},{1,2},{2,3},{3,4},{4,5},{5,6},{6,7},{7,8},{8,9},{9,10},{10,1... | collective-permute-start | bytes 76808 | tf_op jit(solution)/shard_map/ppermute | solution.py:22
  27.0 2.1 %collective-permute-start.4 = (bf16[5,16,160]{2,1,0:T(8,128)(2,1)S(1)}, bf16[5,16,160]{2,1,0:T(8,128)(2,1)S(1)}, u32[]{:S(2)}, u32[]{:S(2)}) collective-permute-start(bf16[5,16,160]{2,1,0:T(8,128)(2,1)S(1)} %get-tuple-element.19), channel_id=1, source_target_pairs={{1,0},{2,1},{3,2},{4,3},{5,4},{6,5},{7,6},{8,7},{9,8},{10,9},{11,1... | collective-permute-start | bytes 76808 | tf_op jit(solution)/shard_map/ppermute | solution.py:25
  29.1 1.0 %fusion.3 = bf16[160,128,2,33]{1,3,2,0:T(8,128)(2,1)S(1)} fusion(bf16[2,33,33]{2,0,1:T(2,128)(2,1)S(1)} %copy-done.7), kind=kOutput, calls=%fused_computation.7 | convolution fusion | flops 90562560 | bytes 2707716 | tf_op jit(solution)/shard_map/kdv,vjc->kdjc/dot_general | solution.py:37
  30.1 2.2 %copy.51 = bf16[160,128,2,33]{1,0,3,2:T(8,128)(2,1)} copy(bf16[160,128,2,33]{1,3,2,0:T(8,128)(2,1)S(1)} %fusion.3) | data formatting | bytes 5406720 | tf_op jit(solution)/shard_map/kdv,vjc->kdjc/dot_general | solution.py:37
  32.9 5.7 %collective-permute-done.4 = bf16[5,16,160]{2,1,0:T(8,128)(2,1)S(1)} collective-permute-done((bf16[5,16,160]{2,1,0:T(8,128)(2,1)S(1)}, bf16[5,16,160]{2,1,0:T(8,128)(2,1)S(1)}, u32[]{:S(2)}, u32[]{:S(2)}) %collective-permute-start.4) | collective-permute-done | bytes 25632 | tf_op jit(solution)/shard_map/ppermute | solution.py:25
  39.3 5.9 %shard_map.100 = f32[2,5,32,128]{3,2,1,0:T(8,128)} custom-call(bf16[5,64,160]{2,1,0:T(8,128)(2,1)} %pad_maximum_fusion.3.x_ref, bf16[2,33,160,128]{3,2,1,0:T(8,128)(2,1)} %bitcast.183), custom_call_target="tpu_custom_call" | custom-call | flops 865075200 | bytes 2969600 | tf_op jit(solution)/shard_map/pallas_call | solution.py:118
  46.0 10.4 %shard_map.101 = f32[3,256,80]{2,1,0:T(8,128)} custom-call(f32[4,32768]{1,0:T(4,128)} %bitcast.186), custom_call_target="tpu_custom_call" | custom-call | flops 8053063680 | bytes 770048 | tf_op jit(solution)/shard_map/pallas_call | solution.py:89
  58.8 1.3 %collective-permute-start.5 = (bf16[2,5,32,16]{3,2,1,0:T(8,128)(2,1)S(1)}, bf16[2,5,32,16]{3,2,1,0:T(8,128)(2,1)S(1)}, u32[]{:S(2)}, u32[]{:S(2)}) collective-permute-start(bf16[2,5,32,16]{3,2,1,0:T(8,128)(2,1)S(1)} %get-tuple-element.16), channel_id=1, source_target_pairs={{0,64},{64,128},{128,192},{1,65},{65,129},{129,193},{2,66},{66,130... | collective-permute-start | bytes 30728 | tf_op jit(solution)/shard_map/ppermute | solution.py:22
  60.1 1.3 %collective-permute-start.6 = (bf16[2,5,32,16]{3,2,1,0:T(8,128)(2,1)S(1)}, bf16[2,5,32,16]{3,2,1,0:T(8,128)(2,1)S(1)}, u32[]{:S(2)}, u32[]{:S(2)}) collective-permute-start(bf16[2,5,32,16]{3,2,1,0:T(8,128)(2,1)S(1)} %get-tuple-element.17), channel_id=1, source_target_pairs={{64,0},{128,64},{192,128},{65,1},{129,65},{193,129},{66,2},{130,66... | collective-permute-start | bytes 30728 | tf_op jit(solution)/shard_map/ppermute | solution.py:25
  61.6 4.0 %collective-permute-done.6 = bf16[2,5,32,16]{3,2,1,0:T(8,128)(2,1)S(1)} collective-permute-done((bf16[2,5,32,16]{3,2,1,0:T(8,128)(2,1)S(1)}, bf16[2,5,32,16]{3,2,1,0:T(8,128)(2,1)S(1)}, u32[]{:S(2)}, u32[]{:S(2)}) %collective-permute-start.6) | collective-permute-done | bytes 10272 | tf_op jit(solution)/shard_map/ppermute | solution.py:25
  66.4 3.0 %collective-permute-start.7 = (bf16[2,5,16,160]{3,2,1,0:T(8,128)(2,1)}, bf16[2,5,16,160]{3,2,1,0:T(8,128)(2,1)}, u32[]{:S(2)}, u32[]{:S(2)}) collective-permute-start(bf16[2,5,16,160]{3,2,1,0:T(8,128)(2,1)} %get-tuple-element.15), channel_id=1, source_target_pairs={{0,1},{1,2},{2,3},{3,4},{4,5},{5,6},{6,7},{7,8},{8,9},{9,10},{10,1... | collective-permute-start | bytes 153608 | tf_op jit(solution)/shard_map/ppermute | solution.py:22
  69.4 2.9 %collective-permute-start.8 = (bf16[2,5,16,160]{3,2,1,0:T(8,128)(2,1)}, bf16[2,5,16,160]{3,2,1,0:T(8,128)(2,1)}, u32[]{:S(2)}, u32[]{:S(2)}) collective-permute-start(bf16[2,5,16,160]{3,2,1,0:T(8,128)(2,1)} %get-tuple-element.14), channel_id=1, source_target_pairs={{1,0},{2,1},{3,2},{4,3},{5,4},{6,5},{7,6},{8,7},{9,8},{10,9},{11,1... | collective-permute-start | bytes 153608 | tf_op jit(solution)/shard_map/ppermute | solution.py:25
  72.3 1.0 %convert_bitcast_fusion = bf16[2,33,160,128,1]{3,1,0,2,4:T(8,128)(2,1)S(1)} fusion(bf16[2,33,33]{2,0,1:T(2,128)(2,1)S(1)} %rev.4), kind=kOutput, calls=%fused_computation.3 | convolution fusion | flops 91914240 | bytes 2707716 | tf_op jit(solution)/shard_map/kdv,vjc->kdjc/dot_general | solution.py:37
  73.4 8.4 %collective-permute-done.8 = bf16[2,5,16,160]{3,2,1,0:T(8,128)(2,1)} collective-permute-done((bf16[2,5,16,160]{3,2,1,0:T(8,128)(2,1)}, bf16[2,5,16,160]{3,2,1,0:T(8,128)(2,1)}, u32[]{:S(2)}, u32[]{:S(2)}) %collective-permute-start.8) | collective-permute-done | bytes 51232 | tf_op jit(solution)/shard_map/ppermute | solution.py:25
  81.7 1.1 %pad_maximum_fusion.2 = (bf16[2,5,48,160]{3,2,1,0:T(8,128)(2,1)S(1)}, bf16[2,5,48,160]{3,2,1,0:T(8,128)(2,1)S(1)}) fusion(bf16[2,5,16,160]{3,2,1,0:T(8,128)(2,1)} %collective-permute-done.8, bf16[2,5,32,16]{3,2,1,0:T(8,128)(2,1)S(1)} %collective-permute-done.6, bf16[2,5,32,128]{3,2,1,0:T(8,128)(2,1)S(1)} %multiply_convert_fusion, ...), kind=kLoop, calls=%fused_computation.20 | loop fusion | flops 1228800 | bytes 512000 | tf_op jit(solution)/shard_map/concatenate | solution.py:26
  84.6 1.6 %fusion.10 = f32[5,32,128]{2,1,0:T(8,128)S(1)} fusion(bf16[2,5,33,32,160]{4,3,1,0,2:T(8,128)(2,1)S(1)} %fusion.16, bf16[2,33,160,128,1]{3,1,0,2,4:T(8,128)(2,1)S(1)} %convert_bitcast_fusion), kind=kOutput, calls=%fused_computation.11 | convolution fusion | flops 432537600 | bytes 6164480 | tf_op jit(solution)/shard_map/kbdrj,kdjc->brc/dot_general | solution.py:189
  86.2 8.1 %all_gather.3 = f32[5,32,512]{2,1,0:T(8,128)S(1)} all-gather(f32[5,32,128]{2,1,0:T(8,128)S(1)} %fusion.10), channel_id=1, replica_groups=mesh['shell'=4,'tile'=64] {'shell'}, dimensions={2}, use_global_device_ids=true | all-gather | bytes 409600 | tf_op jit(solution)/shard_map/all_gather | solution.py:195
  95.1 1.3 %multiply_multiply_fusion = f32[16,32,512]{2,1,0:T(8,128)} fusion(f32[16,32,512]{2,1,0:T(8,128)S(1)} %multiply_reduce_fusion, f32[16,32,512]{2,1,0:T(8,128)S(1)} %copy-done, f32[16]{0:T(128)S(1)} %multiply_multiply_fusion.1, f32[16]{0:T(128)S(1)} %copy-done.11), kind=kLoop, calls=%fused_computation.12 | loop fusion | flops 1048576 | bytes 3145856 | tf_op jit(solution)/shard_map/mul | solution.py:197
  (88 shorter events, 9.3 us)
Async XLA Ops:
  0.0 6.7 %copy-start.6 = (f32[4,64,128]{2,1,0:T(8,128)S(1)}, f32[4,64,128]{2,1,0:T(8,128)}, u32[]{:S(2)}) copy-start(f32[4,64,128]{2,1,0:T(8,128)} %param.18) | copy-start | bytes 393220
  0.0 6.7 %copy-start.10 = (s32[4,64]{1,0:T(4,128)S(1)}, s32[4,64]{1,0:T(4,128)}, u32[]{:S(2)}) copy-start(s32[4,64]{1,0:T(4,128)} %param.19) | copy-start | bytes 3076
  0.0 6.9 %copy-start.2 = (f32[2,4,64,128]{3,2,1,0:T(8,128)S(1)}, f32[2,4,64,128]{3,2,1,0:T(8,128)}, u32[]{:S(2)}) copy-start(f32[2,4,64,128]{3,2,1,0:T(8,128)} %param.17) | copy-start | bytes 786436
  0.0 7.1 %copy-start.4 = (s32[4,64,128]{2,1,0:T(8,128)S(1)}, s32[4,64,128]{2,1,0:T(8,128)}, u32[]{:S(2)}) copy-start(s32[4,64,128]{2,1,0:T(8,128)} %param.15) | copy-start | bytes 393220
  0.0 7.1 %copy-start.5 = (s32[4,64,128]{2,1,0:T(8,128)S(1)}, s32[4,64,128]{2,1,0:T(8,128)}, u32[]{:S(2)}) copy-start(s32[4,64,128]{2,1,0:T(8,128)} %param.16) | copy-start | bytes 393220
  2.3 26.8 %copy-start.7 = (bf16[2,33,33]{2,0,1:T(2,128)(2,1)S(1)}, bf16[2,33,33]{2,0,1:T(2,128)(2,1)}, u32[]{:S(2)}) copy-start(bf16[2,33,33]{2,0,1:T(2,128)(2,1)} %param.13) | copy-start | bytes 13072
  4.0 18.2 %collective-permute-start = (f32[5,32,160]{2,1,0:T(8,128)S(1)}, f32[5,32,160]{2,1,0:T(8,128)S(1)}, u32[]{:S(2)}, u32[]{:S(2)}) collective-permute-start(f32[5,32,160]{2,1,0:T(8,128)S(1)} %get-tuple-element.5), channel_id=1, source_target_pairs={{0,64},{64,128},{128,192},{192,0},{1,65},{65,129},{129,193},{193,1... | collective-permute-start | bytes 307208 | tf_op jit(solution)/shard_map/ppermute | solution.py:178
  4.1 18.2 %collective-permute-start.1 = (f32[5,32,160]{2,1,0:T(8,128)S(1)}, f32[5,32,160]{2,1,0:T(8,128)S(1)}, u32[]{:S(2)}, u32[]{:S(2)}) collective-permute-start(f32[5,32,160]{2,1,0:T(8,128)S(1)} %get-tuple-element.7), channel_id=1, source_target_pairs={{0,128},{64,192},{128,0},{192,64},{1,129},{65,193},{129,1},{193,65... | collective-permute-start | bytes 307208 | tf_op jit(solution)/shard_map/ppermute | solution.py:178
  5.4 16.9 %collective-permute-start.2 = (f32[5,32,160]{2,1,0:T(8,128)S(1)}, f32[5,32,160]{2,1,0:T(8,128)S(1)}, u32[]{:S(2)}, u32[]{:S(2)}) collective-permute-start(f32[5,32,160]{2,1,0:T(8,128)S(1)} %get-tuple-element.6), channel_id=1, source_target_pairs={{0,192},{64,0},{128,64},{192,128},{1,193},{65,1},{129,65},{193,129... | collective-permute-start | bytes 307208 | tf_op jit(solution)/shard_map/ppermute | solution.py:178
  8.4 24.0 %copy-start.9 = (s32[32,128]{1,0:T(8,128)S(1)}, s32[32,128]{1,0:T(8,128)}, u32[]{:S(2)}) copy-start(s32[32,128]{1,0:T(8,128)} %param.14) | copy-start | bytes 49156
  8.4 36.8 %all-to-all-start = ((f32[4,256,128]{2,0,1:T(4,128)}), f32[4,256,128]{2,0,1:T(4,128)S(1)}, u32[]{:S(2)}, u32[]{:S(2)}) async-start(f32[4,256,128]{2,0,1:T(4,128)} %pad_maximum_fusion.1), calls=%async_computation | async-start | bytes 1048576 | tf_op jit(solution)/shard_map/all_to_all | solution.py:158
  22.4 10.6 %collective-permute-start.3 = (bf16[5,16,160]{2,1,0:T(8,128)(2,1)S(1)}, bf16[5,16,160]{2,1,0:T(8,128)(2,1)S(1)}, u32[]{:S(2)}, u32[]{:S(2)}) collective-permute-start(bf16[5,16,160]{2,1,0:T(8,128)(2,1)S(1)} %get-tuple-element.18), channel_id=1, source_target_pairs={{0,1},{1,2},{2,3},{3,4},{4,5},{5,6},{6,7},{7,8},{8,9},{9,10},{10,1... | collective-permute-start | bytes 76808 | tf_op jit(solution)/shard_map/ppermute | solution.py:22
  27.0 11.6 %collective-permute-start.4 = (bf16[5,16,160]{2,1,0:T(8,128)(2,1)S(1)}, bf16[5,16,160]{2,1,0:T(8,128)(2,1)S(1)}, u32[]{:S(2)}, u32[]{:S(2)}) collective-permute-start(bf16[5,16,160]{2,1,0:T(8,128)(2,1)S(1)} %get-tuple-element.19), channel_id=1, source_target_pairs={{1,0},{2,1},{3,2},{4,3},{5,4},{6,5},{7,6},{8,7},{9,8},{10,9},{11,1... | collective-permute-start | bytes 76808 | tf_op jit(solution)/shard_map/ppermute | solution.py:25
  45.2 0.8 copy-start.1
  46.0 12.7 %copy-start.3 = (f32[2,5,32,128]{3,2,1,0:T(8,128)S(1)}, f32[2,5,32,128]{3,2,1,0:T(8,128)}, u32[]{:S(2)}) copy-start(f32[2,5,32,128]{3,2,1,0:T(8,128)} %shard_map.100) | copy-start | bytes 491524
  56.4 16.9 %copy-start.8 = (f32[5,16]{1,0:T(8,128)S(1)}, f32[5,16]{1,0:T(8,128)}, u32[]{:S(2)}) copy-start(f32[5,16]{1,0:T(8,128)} %param.12) | copy-start | bytes 964
  58.8 2.7 %collective-permute-start.5 = (bf16[2,5,32,16]{3,2,1,0:T(8,128)(2,1)S(1)}, bf16[2,5,32,16]{3,2,1,0:T(8,128)(2,1)S(1)}, u32[]{:S(2)}, u32[]{:S(2)}) collective-permute-start(bf16[2,5,32,16]{3,2,1,0:T(8,128)(2,1)S(1)} %get-tuple-element.16), channel_id=1, source_target_pairs={{0,64},{64,128},{128,192},{1,65},{65,129},{129,193},{2,66},{66,130... | collective-permute-start | bytes 30728 | tf_op jit(solution)/shard_map/ppermute | solution.py:22
  60.1 5.5 %collective-permute-start.6 = (bf16[2,5,32,16]{3,2,1,0:T(8,128)(2,1)S(1)}, bf16[2,5,32,16]{3,2,1,0:T(8,128)(2,1)S(1)}, u32[]{:S(2)}, u32[]{:S(2)}) collective-permute-start(bf16[2,5,32,16]{3,2,1,0:T(8,128)(2,1)S(1)} %get-tuple-element.17), channel_id=1, source_target_pairs={{64,0},{128,64},{192,128},{65,1},{129,65},{193,129},{66,2},{130,66... | collective-permute-start | bytes 30728 | tf_op jit(solution)/shard_map/ppermute | solution.py:25
  66.4 7.0 %collective-permute-start.7 = (bf16[2,5,16,160]{3,2,1,0:T(8,128)(2,1)}, bf16[2,5,16,160]{3,2,1,0:T(8,128)(2,1)}, u32[]{:S(2)}, u32[]{:S(2)}) collective-permute-start(bf16[2,5,16,160]{3,2,1,0:T(8,128)(2,1)} %get-tuple-element.15), channel_id=1, source_target_pairs={{0,1},{1,2},{2,3},{3,4},{4,5},{5,6},{6,7},{7,8},{8,9},{9,10},{10,1... | collective-permute-start | bytes 153608 | tf_op jit(solution)/shard_map/ppermute | solution.py:22
  69.4 12.4 %collective-permute-start.8 = (bf16[2,5,16,160]{3,2,1,0:T(8,128)(2,1)}, bf16[2,5,16,160]{3,2,1,0:T(8,128)(2,1)}, u32[]{:S(2)}, u32[]{:S(2)}) collective-permute-start(bf16[2,5,16,160]{3,2,1,0:T(8,128)(2,1)} %get-tuple-element.14), channel_id=1, source_target_pairs={{1,0},{2,1},{3,2},{4,3},{5,4},{6,5},{7,6},{8,7},{9,8},{10,9},{11,1... | collective-permute-start | bytes 153608 | tf_op jit(solution)/shard_map/ppermute | solution.py:25
  84.6 10.5 %copy-start = (f32[16,32,512]{2,1,0:T(8,128)S(1)}, f32[16,32,512]{2,1,0:T(8,128)}, u32[]{:S(2)}) copy-start(f32[16,32,512]{2,1,0:T(8,128)} %param.10) | copy-start | bytes 3145732
  84.6 10.5 %copy-start.11 = (f32[16]{0:T(128)S(1)}, f32[16]{0:T(128)}, u32[]{:S(2)}) copy-start(f32[16]{0:T(128)} %param.11) | copy-start | bytes 196
